TPU v7x, 256 devices: a whole 4x4x8 slice. The times are simulated.
256 devices in a mesh: rep: 2 (over y_hi), fsdp: 64 (over x, z, y_lo), tp: 2 (over core).
Axes of the slice: x: 4, y: 4 (y_hi: 2, y_lo: 2; y = y_hi * 2 + y_lo), z: 8, core: 2. Of those that a mesh axis runs over, the one named last changes fastest.
Arguments:
- attn_global: float32 [24, 1024, 1024], P('rep', 'fsdp', 'tp'), may hold values from -6 to 6
- attn_momentum: float32 [24, 1024, 1024], P('rep', 'fsdp', 'tp'), may hold values from -6 to 6
- attn_inner: bfloat16 [2, 24, 1024, 1024], P('rep', None, 'fsdp', 'tp'), may hold values from -6 to 6
- norm_global: float32 [4, 1024], P('rep', 'tp'), may hold values from 0.5 to 1.5
- norm_momentum: float32 [4, 1024], P('rep', 'tp'), may hold values from -4 to 4
- norm_inner: bfloat16 [2, 4, 1024], P('rep', None, 'tp'), may hold values from 0.5 to 1.5
- emb_global: float32 [64, 2, 251, 1024], P('fsdp', 'rep', None, 'tp'), may hold values from -6 to 6
- emb_momentum: float32 [64, 2, 251, 1024], P('fsdp', 'rep', None, 'tp'), may hold values from -6 to 6
- emb_inner: bfloat16 [2, 32128, 1024], P('rep', 'fsdp', 'tp'), may hold values from -6 to 6
- basis: float32 [1024, 64], replicated, may hold values from -0.1875 to 0.1875
- touched: int32 [2, 8192], replicated, may hold values from 0 to 32127
Outputs:
- new_attn_global: float32 [24, 1024, 1024], P('rep', 'fsdp', 'tp')
- new_attn_momentum: float32 [24, 1024, 1024], P('rep', 'fsdp', 'tp')
- attn_weights: float32 [24, 1024, 1024], P(None, 'fsdp', 'tp')
- new_norm_global: float32 [4, 1024], P('rep', 'tp')
- new_norm_momentum: float32 [4, 1024], P('rep', 'tp')
- norm_weights: float32 [4, 1024], P(None, 'tp')
- new_emb_global: float32 [64, 2, 251, 1024], P('fsdp', 'rep', None, 'tp')
- new_emb_momentum: float32 [64, 2, 251, 1024], P('fsdp', 'rep', None, 'tp')
- emb_weights: float32 [32128, 1024], P('fsdp', 'tp')
All inputs are finite; a program needn't handle non-finite values.
Results may differ from a plain program's by a relative error of at most 0.0003.
Values sent between devices are 32-bit elements; how exact they have to be, the bound alone decides.
No kernel may reach another device: no remote copies, remote signals or barrier semaphores. Data moves between devices by JAX's collectives and lax.ppermute only.
A program may use at most 64 MiB of HBM per device.

v0:
```python
import jax
import jax.numpy as jnp
from jax import lax
from jax.sharding import PartitionSpec as P


OUTER_RATE = 0.7
MOMENTUM = 0.9
GROUPS = 2

KEEP = 1.0 - OUTER_RATE * (1.0 + MOMENTUM)
DECAY = OUTER_RATE * MOMENTUM * MOMENTUM
SHARE = OUTER_RATE * (1.0 + MOMENTUM) / GROUPS
STEP = OUTER_RATE * (1.0 + MOMENTUM)

SWAP = [(0, 1), (1, 0)]


def swap(x, axis):
    return lax.ppermute(x, axis, perm=SWAP)


def place_pair(first_is_own, own, other):
    first = jnp.where(first_is_own, own, other)
    second = jnp.where(first_is_own, other, own)
    return jnp.concatenate([first, second], axis=0)


def outer_sends(global_part, momentum_part, inner_all, rep_index):
    owned = global_part.shape[0]
    own_inner = lax.dynamic_slice_in_dim(inner_all, rep_index * owned, owned, 0).astype(jnp.float32)
    given_inner = lax.dynamic_slice_in_dim(
        inner_all, (1 - rep_index) * owned, owned, 0
    ).astype(jnp.float32)
    partial = KEEP * global_part - DECAY * momentum_part + SHARE * own_inner
    return own_inner, given_inner, partial


def outer_finish(global_part, momentum_part, own_inner, given_inner, partial, got_inner, got_partial, first_is_own):
    new_global = partial + SHARE * got_inner
    grad = global_part - (own_inner + got_inner) / GROUPS
    new_momentum = MOMENTUM * momentum_part + grad
    weights = place_pair(first_is_own, partial, got_partial) + SHARE * place_pair(
        first_is_own, got_inner, given_inner
    )
    return new_global, new_momentum, weights


def step_body(
    attn_global,
    attn_momentum,
    attn_inner,
    norm_global,
    norm_momentum,
    norm_inner,
    emb_global,
    emb_momentum,
    emb_inner,
    basis,
    touched,
):
    rep_index = lax.axis_index("rep")
    first_is_own = rep_index == 0
    width = attn_global.shape[-1]
    attn_parts = outer_sends(attn_global, attn_momentum, attn_inner[0], rep_index)
    norm_parts = outer_sends(norm_global, norm_momentum, norm_inner[0], rep_index)
    attn_rows = attn_parts[1].size // width
    norm_rows = norm_parts[1].size // width
    sent = jnp.concatenate(
        [attn_parts[1].reshape(-1, width), attn_parts[2].reshape(-1, width), norm_parts[1], norm_parts[2]],
        axis=0,
    )
    sent = lax.optimization_barrier(sent)
    got = swap(sent, "rep")
    got_attn_inner = got[:attn_rows].reshape(attn_global.shape)
    got_attn_partial = got[attn_rows : 2 * attn_rows].reshape(attn_global.shape)
    got_norm_inner = got[2 * attn_rows : 2 * attn_rows + norm_rows]
    got_norm_partial = got[2 * attn_rows + norm_rows :]
    new_attn_global, new_attn_momentum, attn_weights = outer_finish(
        attn_global, attn_momentum, *attn_parts, got_attn_inner, got_attn_partial, first_is_own
    )
    new_norm_global, new_norm_momentum, norm_weights = outer_finish(
        norm_global, norm_momentum, *norm_parts, got_norm_inner, got_norm_partial, first_is_own
    )

    block_rows = emb_inner.shape[1]
    half_rows = emb_global.shape[2]
    half_width = emb_global.shape[3]
    row_start = lax.axis_index("fsdp") * block_rows
    half_start = rep_index * half_rows
    positions = row_start + jnp.arange(block_rows, dtype=jnp.int32)
    matches = touched[:, :, None] == positions[None, None, :]
    touched_masks = jnp.any(matches, axis=1).astype(jnp.float32)
    counts = jnp.sum(touched_masks, axis=0)
    own_mask = lax.dynamic_index_in_dim(touched_masks, rep_index, 0, keepdims=False)
    half_counts = lax.dynamic_slice_in_dim(counts, half_start, half_rows, 0)
    basis_half = lax.dynamic_slice_in_dim(basis, lax.axis_index("tp") * half_width, half_width, 0)
    own_rows = emb_global[0, 0]
    own_momentum = emb_momentum[0, 0]
    global_coeff = jnp.dot(
        own_rows, basis_half, precision=lax.Precision.HIGHEST, preferred_element_type=jnp.float32
    )
    inner_coeff = jnp.dot(
        emb_inner[0].astype(jnp.float32),
        basis_half,
        precision=lax.Precision.HIGHEST,
        preferred_element_type=jnp.float32,
    )
    placed_global = place_pair(
        first_is_own, half_counts[:, None] * global_coeff, jnp.zeros_like(global_coeff)
    )
    coeff_term = placed_global - own_mask[:, None] * inner_coeff
    coeff_chip = coeff_term + swap(coeff_term, "tp")
    kept_rows = own_rows - DECAY * own_momentum
    kept_rows, coeff_chip = lax.optimization_barrier((kept_rows, coeff_chip))
    coeff_sum = coeff_chip + swap(coeff_chip, "rep")
    got_rows = swap(kept_rows, "rep")
    emb_grad = (
        jnp.dot(
            coeff_sum,
            basis_half.T,
            precision=lax.Precision.HIGHEST,
            preferred_element_type=jnp.float32,
        )
        / GROUPS
    )
    emb_grad = lax.optimization_barrier(emb_grad)
    own_grad = lax.dynamic_slice_in_dim(emb_grad, half_start, half_rows, 0).reshape(emb_global.shape)
    new_emb_global = (emb_global - DECAY * emb_momentum) - STEP * own_grad
    new_emb_momentum = MOMENTUM * emb_momentum + own_grad
    new_emb_global, new_emb_momentum = lax.optimization_barrier((new_emb_global, new_emb_momentum))
    emb_weights = place_pair(first_is_own, kept_rows, got_rows) - STEP * emb_grad
    return (
        new_attn_global,
        new_attn_momentum,
        attn_weights,
        new_norm_global,
        new_norm_momentum,
        norm_weights,
        new_emb_global,
        new_emb_momentum,
        emb_weights,
    )


def solution(mesh):
    placed = (
        P("rep", "fsdp", "tp"),
        P("rep", "fsdp", "tp"),
        P("rep", None, "fsdp", "tp"),
        P("rep", "tp"),
        P("rep", "tp"),
        P("rep", None, "tp"),
        P("fsdp", "rep", None, "tp"),
        P("fsdp", "rep", None, "tp"),
        P("rep", "fsdp", "tp"),
        P(),
        P(),
    )
    return jax.shard_map(
        step_body,
        mesh=mesh,
        in_specs=placed,
        out_specs=(
            P("rep", "fsdp", "tp"),
            P("rep", "fsdp", "tp"),
            P(None, "fsdp", "tp"),
            P("rep", "tp"),
            P("rep", "tp"),
            P(None, "tp"),
            P("fsdp", "rep", None, "tp"),
            P("fsdp", "rep", None, "tp"),
            P("fsdp", "tp"),
        ),
        check_vma=False,
    )
```

profile of v0, /device:TPU:1, one launch (start us, length us, event | category | flops | bytes accessed | tf_op | source)
XLA Modules:
  0.0 54.9 jit_solution(3661587159032352281)
XLA Ops:
  0.7 5.2 %compare_reduce_fusion = pred[2,502]{1,0:T(4,128)(4,1)S(1)} fusion(s32[2,8192]{1,0:T(2,128)} %param.21, s32[502]{0:T(512)S(1)} %iota_add_fusion), kind=kLoop, calls=%fused_computation | loop fusion | flops 16448532 | bytes 68548 | tf_op jit(solution)/shard_map/reduce_or | solution.py:93
  6.0 0.1 dynamic_slice.29
  6.1 1.7 %select_bitcast_fusion.1 = (f32[251,64]{0,1:T(8,128)S(1)}, f32[251,64]{0,1:T(8,128)S(1)}) fusion(pred[]{:T(512)S(6)} %eq.16, f32[1,1,251,512]{3,1,2,0:T(1,128)} %param.17, f32[1024,64]{0,1:T(8,128)} %param.20, s32[]{:T(128)S(6)} %select_n.109, f32[251]{0:T(256)S(1)} %dynamic_slice.29), kind=kOutput, calls=%fused_computation.36 | convolution fusion | flops 98745408 | bytes 774641 | tf_op jit(solution)/shard_map/dot_general | solution.py:100
  7.9 1.6 %fusion.1 = f32[502,64]{0,1:T(8,128)S(1)} fusion(bf16[1,502,512]{2,1,0:T(8,128)(2,1)S(1)} %copy-done, f32[251,64]{0,1:T(8,128)S(1)} %get-tuple-element.59, f32[251,64]{0,1:T(8,128)S(1)} %get-tuple-element.58, f32[1024,64]{0,1:T(8,128)} %param.20, s32[]{:T(128)S(6)} %select_n.109, f32[502]{0:T(512)S(1)} %bitcast.46), kind=kOutput, calls=%fused_computation.4 | convolution fusion | flops 197490816 | bytes 904156 | tf_op jit(solution)/shard_map/dot_general | solution.py:103
  9.4 3.3 %collective-permute-start.1 = (f32[502,64]{0,1:T(8,128)S(1)}, f32[502,64]{0,1:T(8,128)S(1)}, u32[]{:S(2)}, u32[]{:S(2)}) collective-permute-start(f32[502,64]{0,1:T(8,128)S(1)} %fusion.1), channel_id=1, source_target_pairs={{0,1},{1,0},{2,3},{3,2},{4,5},{5,4},{6,7},{7,6},{8,9},{9,8},{10,11... | collective-permute-start | bytes 385544 | tf_op jit(solution)/shard_map/ppermute | solution.py:20
  12.7 0.1 bitcast_subtract_fusion
  12.9 1.1 %fusion.5 = f32[12,16,512]{2,1,0:T(8,128)S(1)} fusion(f32[12,16,512]{2,1,0:T(8,128)S(1)} %copy-done.4, f32[12,16,512]{2,1,0:T(8,128)} %param.11, bf16[1,24,16,512]{3,2,1,0:T(8,128)(2,1)S(1)} %copy-done.3, s32[]{:T(128)S(6)} %select_n.93), kind=kLoop, calls=%fused_computation.19 | loop fusion | flops 589824 | bytes 1376260 | tf_op jit(solution)/shard_map/add | solution.py:35
  14.2 1.3 %collective-permute-start.2 = (f32[502,64]{0,1:T(8,128)S(1)}, f32[502,64]{0,1:T(8,128)S(1)}, u32[]{:S(2)}, u32[]{:S(2)}) collective-permute-start(f32[502,64]{0,1:T(8,128)S(1)} %add.91), channel_id=1, source_target_pairs={{0,128},{128,0},{1,129},{129,1},{2,130},{130,2},{3,131},{131,3},{4... | collective-permute-start | bytes 385544 | tf_op jit(solution)/shard_map/ppermute | solution.py:20
  15.5 0.1 pad_maximum_fusion
  15.5 1.9 %collective-permute-start = (f32[388,512]{1,0:T(8,128)S(1)}, f32[388,512]{1,0:T(8,128)S(1)}, u32[]{:S(2)}, u32[]{:S(2)}) collective-permute-start(f32[388,512]{1,0:T(8,128)S(1)} %pad_maximum_fusion), channel_id=1, source_target_pairs={{0,128},{128,0},{1,129},{129,1},{2,130},{130,2},{3,131},{131,3},{4... | collective-permute-start | bytes 2383880 | tf_op jit(solution)/shard_map/ppermute | solution.py:20
  17.4 1.2 %collective-permute-start.3 = (f32[251,512]{1,0:T(8,128)S(1)}, f32[251,512]{1,0:T(8,128)S(1)}, u32[]{:S(2)}, u32[]{:S(2)}) collective-permute-start(f32[251,512]{1,0:T(8,128)S(1)} %bitcast_subtract_fusion), channel_id=1, source_target_pairs={{0,128},{128,0},{1,129},{129,1},{2,130},{130,2},{3,131},{131,3},{4... | collective-permute-start | bytes 1542152 | tf_op jit(solution)/shard_map/ppermute | solution.py:20
  18.6 2.2 %collective-permute-done.2 = f32[502,64]{0,1:T(8,128)S(1)} collective-permute-done((f32[502,64]{0,1:T(8,128)S(1)}, f32[502,64]{0,1:T(8,128)S(1)}, u32[]{:S(2)}, u32[]{:S(2)}) %collective-permute-start.2) | collective-permute-done | bytes 128544 | tf_op jit(solution)/shard_map/ppermute | solution.py:20
  20.8 1.0 %convolution_multiply_fusion = f32[502,512]{1,0:T(8,128)S(1)} fusion(f32[502,64]{0,1:T(8,128)S(1)} %add.91, f32[502,64]{0,1:T(8,128)S(1)} %collective-permute-done.2, f32[1024,64]{0,1:T(8,128)S(1)} %copy-done.6, s32[]{:T(128)S(6)} %select_n.109), kind=kOutput, calls=%fused_computation.1 | convolution fusion | flops 197683584 | bytes 1421316 | tf_op jit(solution)/shard_map/dot_general | solution.py:119
  21.8 0.2 bitcast_subtract_fusion.1
  22.0 1.5 %reshape_add_fusion = f32[1,1,251,512]{3,1,2,0:T(1,128)} fusion(f32[251,512]{1,0:T(8,128)S(1)} %get-tuple-element.36, f32[1,1,251,512]{3,1,2,0:T(1,128)S(1)} %copy-done.2), kind=kLoop, calls=%fused_computation.15 | loop fusion | flops 257024 | bytes 1542144 | tf_op jit(solution)/shard_map/add | solution.py:130
  23.5 1.3 %copy.25 = f32[1,1,251,512]{3,1,2,0:T(1,128)} copy(f32[1,1,251,512]{3,2,1,0:T(8,128)S(1)} %get-tuple-element.32) | data formatting | bytes 1028096
  24.8 24.4 %collective-permute-done.3 = f32[251,512]{1,0:T(8,128)S(1)} collective-permute-done((f32[251,512]{1,0:T(8,128)S(1)}, f32[251,512]{1,0:T(8,128)S(1)}, u32[]{:S(2)}, u32[]{:S(2)}) %collective-permute-start.3) | collective-permute-done | bytes 514080 | tf_op jit(solution)/shard_map/ppermute | solution.py:20
  49.2 0.1 broadcast_select_fusion.1
  49.3 1.2 %maximum_subtract_fusion = f32[502,512]{1,0:T(8,128)} fusion(f32[251,512]{1,0:T(8,128)S(1)} %get-tuple-element.38, f32[251,512]{1,0:T(8,128)S(1)} %get-tuple-element.37, f32[502,512]{1,0:T(8,128)S(1)} %convolution_multiply_fusion), kind=kLoop, calls=%fused_computation.6 | loop fusion | flops 771072 | bytes 3084288 | tf_op jit(solution)/shard_map/sub | solution.py:132
  50.6 0.9 %copy-done.5 = f32[12,16,512]{2,1,0:T(8,128)S(1)} copy-done((f32[12,16,512]{2,1,0:T(8,128)S(1)}, f32[12,16,512]{2,1,0:T(8,128)}, u32[]{:S(2)}) %copy-start.5) | copy-done | bytes 393240
  51.5 1.2 %bitcast_select_fusion.1 = (f32[12,16,512]{2,1,0:T(8,128)S(1)}, f32[12,16,512]{2,1,0:T(8,128)S(1)}, f32[12,16,512]{2,1,0:T(8,128)}, f32[12,16,512]{2,1,0:T(8,128...) fusion(f32[12,16,512]{2,1,0:T(8,128)S(1)} %bitcast.45, pred[]{:T(512)S(6)} %eq.16, ...), kind=kLoop, calls=%fused_computation.24 | loop fusion | flops 1277952 | bytes 4718601 | tf_op jit(solution)/shard_map/jit(_where)/select_n | solution.py:24
  52.7 0.6 %broadcast_select_fusion.5 = (f32[2,512]{1,0:T(2,128)S(1)}, f32[2,512]{1,0:T(2,128)}, f32[2,512]{1,0:T(2,128)S(1)}, f32[2,512]{1,0:T(2,128)}, f32[2,512]{1,0:T(2,128)S(1)}, /*index=5*/f32[2,512]{1,0:T(2,128)S(1)}) fusion(pred[]{:T(512)S(6)} %eq.16, f32[388,512]{1,0:T(8,128)S(1)} %collective-permute-done, bf16[1,4,512]{2,1,0:T(4,128)(2,1)S(1)} %copy-done.9, ...), kind=kLoop, calls=%fused_computation.47 | loop fusion | flops 13312 | bytes 49161 | tf_op jit(solution)/shard_map/jit(_where)/select_n | solution.py:24
  53.3 0.6 %maximum_add_fusion.1 = f32[4,512]{1,0:T(4,128)} fusion(f32[2,512]{1,0:T(2,128)S(1)} %get-tuple-element.46, f32[2,512]{1,0:T(2,128)S(1)} %get-tuple-element.47, f32[2,512]{1,0:T(2,128)S(1)} %get-tuple-element.41, f32[2,512]{1,0:T(2,128)S(1)} %get-tuple-element.39), kind=kLoop, calls=%fused_computation.37 | loop fusion | flops 8192 | bytes 24576 | tf_op jit(solution)/shard_map/add | solution.py:43
  53.9 1.0 %maximum_add_fusion = f32[24,16,512]{2,1,0:T(8,128)} fusion(f32[12,16,512]{2,1,0:T(8,128)S(1)} %get-tuple-element.56, f32[12,16,512]{2,1,0:T(8,128)S(1)} %get-tuple-element.57, f32[12,16,512]{2,1,0:T(8,128)S(1)} %get-tuple-element.51, f32[12,16,512]{2,1,0:T(8,128)S(1)} %get-tuple-element.50), kind=kLoop, calls=%fused_computation.8 | loop fusion | flops 786432 | bytes 2359296 | tf_op jit(solution)/shard_map/add | solution.py:43
  (30 shorter events, 0.2 us)
Async XLA Ops:
  0.6 7.1 %copy-start = (bf16[1,502,512]{2,1,0:T(8,128)(2,1)S(1)}, bf16[1,502,512]{2,1,0:T(8,128)(2,1)}, u32[]{:S(2)}) copy-start(bf16[1,502,512]{2,1,0:T(8,128)(2,1)} %param.19) | copy-start | bytes 1542148
  0.7 12.1 %copy-start.1 = (f32[1,1,251,512]{3,1,2,0:T(1,128)S(1)}, f32[1,1,251,512]{3,1,2,0:T(1,128)}, u32[]{:S(2)}) copy-start(f32[1,1,251,512]{3,1,2,0:T(1,128)} %param.17) | copy-start | bytes 1542148
  0.7 12.1 %copy-start.2 = (f32[1,1,251,512]{3,1,2,0:T(1,128)S(1)}, f32[1,1,251,512]{3,1,2,0:T(1,128)}, u32[]{:S(2)}) copy-start(f32[1,1,251,512]{3,1,2,0:T(1,128)} %param.18) | copy-start | bytes 1542148
  7.8 5.0 %copy-start.7 = (f32[2,512]{1,0:T(2,128)S(1)}, f32[2,512]{1,0:T(2,128)}, u32[]{:S(2)}) copy-start(f32[2,512]{1,0:T(2,128)} %param.15) | copy-start | bytes 12292
  7.8 5.0 %copy-start.8 = (f32[2,512]{1,0:T(2,128)S(1)}, f32[2,512]{1,0:T(2,128)}, u32[]{:S(2)}) copy-start(f32[2,512]{1,0:T(2,128)} %param.14) | copy-start | bytes 12292
  7.8 5.0 %copy-start.9 = (bf16[1,4,512]{2,1,0:T(4,128)(2,1)S(1)}, bf16[1,4,512]{2,1,0:T(4,128)(2,1)}, u32[]{:S(2)}) copy-start(bf16[1,4,512]{2,1,0:T(4,128)(2,1)} %param.16) | copy-start | bytes 12292
  7.8 5.1 %copy-start.3 = (bf16[1,24,16,512]{3,2,1,0:T(8,128)(2,1)S(1)}, bf16[1,24,16,512]{3,2,1,0:T(8,128)(2,1)}, u32[]{:S(2)}) copy-start(bf16[1,24,16,512]{3,2,1,0:T(8,128)(2,1)} %param.13) | copy-start | bytes 1179652
  7.8 5.1 %copy-start.4 = (f32[12,16,512]{2,1,0:T(8,128)S(1)}, f32[12,16,512]{2,1,0:T(8,128)}, u32[]{:S(2)}) copy-start(f32[12,16,512]{2,1,0:T(8,128)} %param.12) | copy-start | bytes 1179652
  9.4 4.7 %collective-permute-start.1 = (f32[502,64]{0,1:T(8,128)S(1)}, f32[502,64]{0,1:T(8,128)S(1)}, u32[]{:S(2)}, u32[]{:S(2)}) collective-permute-start(f32[502,64]{0,1:T(8,128)S(1)} %fusion.1), channel_id=1, source_target_pairs={{0,1},{1,0},{2,3},{3,2},{4,5},{5,4},{6,7},{7,6},{8,9},{9,8},{10,11... | collective-permute-start | bytes 385544 | tf_op jit(solution)/shard_map/ppermute | solution.py:20
  14.1 6.7 %copy-start.6 = (f32[1024,64]{0,1:T(8,128)S(1)}, f32[1024,64]{0,1:T(8,128)}, u32[]{:S(2)}) copy-start(f32[1024,64]{0,1:T(8,128)} %param.20) | copy-start | bytes 786436
  14.2 6.6 %collective-permute-start.2 = (f32[502,64]{0,1:T(8,128)S(1)}, f32[502,64]{0,1:T(8,128)S(1)}, u32[]{:S(2)}, u32[]{:S(2)}) collective-permute-start(f32[502,64]{0,1:T(8,128)S(1)} %add.91), channel_id=1, source_target_pairs={{0,128},{128,0},{1,129},{129,1},{2,130},{130,2},{3,131},{131,3},{4... | collective-permute-start | bytes 385544 | tf_op jit(solution)/shard_map/ppermute | solution.py:20
  15.5 35.0 %collective-permute-start = (f32[388,512]{1,0:T(8,128)S(1)}, f32[388,512]{1,0:T(8,128)S(1)}, u32[]{:S(2)}, u32[]{:S(2)}) collective-permute-start(f32[388,512]{1,0:T(8,128)S(1)} %pad_maximum_fusion), channel_id=1, source_target_pairs={{0,128},{128,0},{1,129},{129,1},{2,130},{130,2},{3,131},{131,3},{4... | collective-permute-start | bytes 2383880 | tf_op jit(solution)/shard_map/ppermute | solution.py:20
  17.4 31.8 %collective-permute-start.3 = (f32[251,512]{1,0:T(8,128)S(1)}, f32[251,512]{1,0:T(8,128)S(1)}, u32[]{:S(2)}, u32[]{:S(2)}) collective-permute-start(f32[251,512]{1,0:T(8,128)S(1)} %bitcast_subtract_fusion), channel_id=1, source_target_pairs={{0,128},{128,0},{1,129},{129,1},{2,130},{130,2},{3,131},{131,3},{4... | collective-permute-start | bytes 1542152 | tf_op jit(solution)/shard_map/ppermute | solution.py:20
  50.5 1.0 %copy-start.5 = (f32[12,16,512]{2,1,0:T(8,128)S(1)}, f32[12,16,512]{2,1,0:T(8,128)}, u32[]{:S(2)}) copy-start(f32[12,16,512]{2,1,0:T(8,128)} %param.11) | copy-start | bytes 1179652
where the time goes:
time: 55.2 us; the launch traced here: 54.9 us
  waiting for transfers between devices  26.6 us (48%)
  other arithmetic  13.1 us (24%)
  starting transfers between devices  7.64 us (14%)
  matrix products  4.32 us (8%)
  local copies, waits for them, and re-layouts  2.45 us (4%)
  between operations  0.88 us (2%)
    ppermute x4, waiting for transfers between devices, swap(): return lax.ppermute(x, axis, perm=SWAP)  26.6 us
    ppermute x4, starting transfers between devices, swap(): return lax.ppermute(x, axis, perm=SWAP)  7.64 us
    reduce_or x1, other arithmetic, step_body(): touched_masks = jnp.any(matches, axis=1).astype(jnp.float32)  5.23 us
    unnamed x21, local copies, waits for them, and re-layouts  2.31 us
    select_n x3, other arithmetic, place_pair(): first = jnp.where(first_is_own, own, other)  1.87 us
    dot_general x1, matrix products, step_body(): jnp.dot(own_rows, basis_half, precision=lax.Precision.HIGHEST, preferred_...  1.72 us
    add x2, other arithmetic, outer_finish(): place_pair(first_is_own, partial, got_partial)  1.65 us
    dot_general x1, matrix products, step_body(): jnp.dot(emb_inner[0].astype(jnp.float32), basis_half, precision=lax.Preci...  1.58 us
  transfers between devices with their start and end apart: 4, of which 2 were waited for; matrix products, arithmetic and copies ran while one was open for 12% of the time, Pallas kernels for 0%

commit v1 on v0

--- a/solution.py
+++ b/solution.py
@@ -26,14 +26,19 @@
     return jnp.concatenate([first, second], axis=0)
 
 
-def outer_sends(global_part, momentum_part, inner_all, rep_index):
+def outer_sends(global_part, inner_all, rep_index):
     owned = global_part.shape[0]
-    own_inner = lax.dynamic_slice_in_dim(inner_all, rep_index * owned, owned, 0).astype(jnp.float32)
     given_inner = lax.dynamic_slice_in_dim(
         inner_all, (1 - rep_index) * owned, owned, 0
     ).astype(jnp.float32)
+    return lax.optimization_barrier(given_inner)
+
+
+def outer_partial(global_part, momentum_part, inner_all, rep_index):
+    owned = global_part.shape[0]
+    own_inner = lax.dynamic_slice_in_dim(inner_all, rep_index * owned, owned, 0).astype(jnp.float32)
     partial = KEEP * global_part - DECAY * momentum_part + SHARE * own_inner
-    return own_inner, given_inner, partial
+    return lax.optimization_barrier((own_inner, partial))
 
 
 def outer_finish(global_part, momentum_part, own_inner, given_inner, partial, got_inner, got_partial, first_is_own):
@@ -62,20 +67,23 @@
     rep_index = lax.axis_index("rep")
     first_is_own = rep_index == 0
     width = attn_global.shape[-1]
-    attn_parts = outer_sends(attn_global, attn_momentum, attn_inner[0], rep_index)
-    norm_parts = outer_sends(norm_global, norm_momentum, norm_inner[0], rep_index)
-    attn_rows = attn_parts[1].size // width
-    norm_rows = norm_parts[1].size // width
+    given_attn = outer_sends(attn_global, attn_inner[0], rep_index)
+    got_attn_inner = swap(given_attn, "rep")
+    given_norm = outer_sends(norm_global, norm_inner[0], rep_index)
+    attn_parts = (given_attn,) + outer_partial(attn_global, attn_momentum, attn_inner[0], rep_index)
+    norm_parts = (given_norm,) + outer_partial(norm_global, norm_momentum, norm_inner[0], rep_index)
+    attn_parts = (attn_parts[1], attn_parts[0], attn_parts[2])
+    norm_parts = (norm_parts[1], norm_parts[0], norm_parts[2])
+    norm_rows = given_norm.shape[0]
     sent = jnp.concatenate(
-        [attn_parts[1].reshape(-1, width), attn_parts[2].reshape(-1, width), norm_parts[1], norm_parts[2]],
-        axis=0,
+        [attn_parts[2].reshape(-1, width), given_norm, norm_parts[2]], axis=0
     )
     sent = lax.optimization_barrier(sent)
     got = swap(sent, "rep")
-    got_attn_inner = got[:attn_rows].reshape(attn_global.shape)
-    got_attn_partial = got[attn_rows : 2 * attn_rows].reshape(attn_global.shape)
-    got_norm_inner = got[2 * attn_rows : 2 * attn_rows + norm_rows]
-    got_norm_partial = got[2 * attn_rows + norm_rows :]
+    attn_rows = attn_parts[2].size // width
+    got_attn_partial = got[:attn_rows].reshape(attn_global.shape)
+    got_norm_inner = got[attn_rows : attn_rows + norm_rows]
+    got_norm_partial = got[attn_rows + norm_rows :]
     new_attn_global, new_attn_momentum, attn_weights = outer_finish(
         attn_global, attn_momentum, *attn_parts, got_attn_inner, got_attn_partial, first_is_own
     )
@@ -113,7 +121,11 @@
     coeff_chip = coeff_term + swap(coeff_term, "tp")
     kept_rows = own_rows - DECAY * own_momentum
     kept_rows, coeff_chip = lax.optimization_barrier((kept_rows, coeff_chip))
-    coeff_sum = coeff_chip + swap(coeff_chip, "rep")
+    tp_index = lax.axis_index("tp")
+    chip_rows = coeff_chip.shape[0] // 2
+    coeff_mine = lax.dynamic_slice_in_dim(coeff_chip, tp_index * chip_rows, chip_rows, 0)
+    coeff_half = coeff_mine + swap(coeff_mine, "rep")
+    coeff_sum = place_pair(tp_index == 0, coeff_half, swap(coeff_half, "tp"))
     got_rows = swap(kept_rows, "rep")
     emb_grad = (
         jnp.dot(

time: 55.2 us -> 56 us (1.014)
  waiting for transfers between devices: 26.6 us -> 17.8 us
  other arithmetic: 13.1 us -> 19.1 us
  starting transfers between devices: 7.64 us -> 10.1 us
  matrix products: 4.32 us -> 5.11 us
    ppermute x4 -> x6, waiting for transfers between devices: 26.6 us -> 17.8 us  [swap(): return lax.ppermute(x, axis, perm=SWAP)]
    select_n x3 -> x4, other arithmetic: 1.87 us -> 4.67 us  [place_pair(): first = jnp.where(first_is_own, own, other)]
    ppermute x4 -> x6, starting transfers between devices: 7.64 us -> 10.1 us  [swap(): return lax.ppermute(x, axis, perm=SWAP)]
    add x1, other arithmetic: 0.02 us -> 1.02 us  [step_body(): coeff_chip = coeff_term + swap(coeff_term, 'tp')]
    slice x1, local copies, waits for them, and re-layouts: 0.05 us -> 1.02 us  [step_body(): got_attn_partial = got[:attn_rows].reshape(attn_global.shape)]
    unnamed x21 -> x23, local copies, waits for them, and re-layouts: 2.31 us -> 1.38 us
    convert_element_type x2, other arithmetic: 0.05 us -> 0.98 us  [outer_sends(): given_inner = lax.dynamic_slice_in_dim(inner_all, (1 - rep_index) * owned...]
    concatenate x1, other arithmetic: 0.06 us -> 0.78 us  [step_body(): jnp.concatenate([attn_parts[2].reshape(-1, width), given_norm, norm_parts...]
  transfers between devices with their start and end apart: 4 -> 6, of which waited for: 2 -> 3; matrix products, arithmetic and copies ran while one was open for 12% -> 29% of each run, Pallas kernels for 0% -> 0%
where the time goes in v1:
time: 56 us; the launch traced here: 55.6 us
  other arithmetic  19.1 us (34%)
  waiting for transfers between devices  17.8 us (32%)
  starting transfers between devices  10.1 us (18%)
  matrix products  5.11 us (9%)
  local copies, waits for them, and re-layouts  2.58 us (5%)
  between operations  0.89 us (2%)
    ppermute x6, waiting for transfers between devices, swap(): return lax.ppermute(x, axis, perm=SWAP)  17.8 us
    ppermute x6, starting transfers between devices, swap(): return lax.ppermute(x, axis, perm=SWAP)  10.1 us
    reduce_or x1, other arithmetic, step_body(): touched_masks = jnp.any(matches, axis=1).astype(jnp.float32)  5.2 us
    select_n x4, other arithmetic, place_pair(): first = jnp.where(first_is_own, own, other)  4.67 us
    dot_general x1, matrix products, step_body(): jnp.dot(emb_inner[0].astype(jnp.float32), basis_half, precision=lax.Preci...  2.25 us
    dot_general x1, matrix products, step_body(): jnp.dot(own_rows, basis_half, precision=lax.Precision.HIGHEST, preferred_...  1.72 us
    add x2, other arithmetic, outer_finish(): place_pair(first_is_own, partial, got_partial)  1.65 us
    add x1, other arithmetic, step_body(): new_emb_momentum = MOMENTUM * emb_momentum + own_grad  1.49 us
  transfers between devices with their start and end apart: 6, of which 3 were waited for; matrix products, arithmetic and copies ran while one was open for 29% of the time, Pallas kernels for 0%

profile of v1, /device:TPU:1, one launch (start us, length us, event | category | flops | bytes accessed | tf_op | source)
XLA Modules:
  0.0 55.6 jit_solution(4070938508829442146)
XLA Ops:
  0.7 5.2 %compare_reduce_fusion = pred[2,502]{1,0:T(4,128)(4,1)S(1)} fusion(s32[2,8192]{1,0:T(2,128)} %param.21, s32[502]{0:T(512)S(1)} %iota_add_fusion), kind=kLoop, calls=%fused_computation | loop fusion | flops 16448532 | bytes 68548 | tf_op jit(solution)/shard_map/reduce_or | solution.py:101
  6.0 1.7 %select_bitcast_fusion.1 = (f32[251,64]{0,1:T(8,128)S(1)}, f32[251,64]{0,1:T(8,128)S(1)}) fusion(pred[]{:T(512)S(6)} %eq.19, f32[1,1,251,512]{3,1,2,0:T(1,128)} %param.17, f32[1024,64]{0,1:T(8,128)} %param.20, s32[]{:T(128)S(6)} %select_n.123, f32[251]{0:T(256)S(1)} %dynamic_slice.32), kind=kOutput, calls=%fused_computation.35 | convolution fusion | flops 98745408 | bytes 774641 | tf_op jit(solution)/shard_map/dot_general | solution.py:108
  7.8 2.2 %fusion.1 = f32[502,64]{0,1:T(8,128)} fusion(bf16[1,502,512]{2,1,0:T(8,128)(2,1)S(1)} %copy-done, f32[251,64]{0,1:T(8,128)S(1)} %get-tuple-element.69, f32[251,64]{0,1:T(8,128)S(1)} %get-tuple-element.68, f32[1024,64]{0,1:T(8,128)} %param.20, s32[]{:T(128)S(6)} %select_n.123, f32[502]{0:T(512)S(1)} %bitcast.42), kind=kOutput, calls=%fused_computation.4 | convolution fusion | flops 197490816 | bytes 904156 | tf_op jit(solution)/shard_map/dot_general | solution.py:111
  10.0 3.2 %collective-permute-start.2 = (f32[502,64]{0,1:T(8,128)}, f32[502,64]{0,1:T(8,128)}, u32[]{:S(2)}, u32[]{:S(2)}) collective-permute-start(f32[502,64]{0,1:T(8,128)} %fusion.1), channel_id=1, source_target_pairs={{0,1},{1,0},{2,3},{3,2},{4,5},{5,4},{6,7},{7,6},{8,9},{9,8},{10,11... | collective-permute-start | bytes 385544 | tf_op jit(solution)/shard_map/ppermute | solution.py:20
  13.2 1.0 %bitcast_convert_fusion = (f32[12,16,512]{2,1,0:T(8,128)}, f32[12,16,512]{2,1,0:T(8,128)}) fusion(bf16[1,24,16,512]{3,2,1,0:T(8,128)(2,1)S(1)} %copy-done.6, s32[]{:T(128)S(6)} %select_n.107, s32[]{:T(128)S(6)} %select_n.106), kind=kLoop, calls=%fused_computation.22 | loop fusion | flops 196608 | bytes 1179656 | tf_op jit(solution)/shard_map/convert_element_type | solution.py:33
  14.2 1.2 %collective-permute-start = (f32[12,16,512]{2,1,0:T(8,128)}, f32[12,16,512]{2,1,0:T(8,128)}, u32[]{:S(2)}, u32[]{:S(2)}) collective-permute-start(f32[12,16,512]{2,1,0:T(8,128)} %get-tuple-element.64), channel_id=1, source_target_pairs={{0,128},{128,0},{1,129},{129,1},{2,130},{130,2},{3,131},{131,3},{4... | collective-permute-start | bytes 1179656 | tf_op jit(solution)/shard_map/ppermute | solution.py:20
  15.6 1.0 %multiply_add_fusion.1 = f32[12,16,512]{2,1,0:T(8,128)S(1)} fusion(f32[12,16,512]{2,1,0:T(8,128)S(1)} %copy-done.4, f32[12,16,512]{2,1,0:T(8,128)S(1)} %copy-done.3, bf16[1,24,16,512]{3,2,1,0:T(8,128)(2,1)} %param.13, s32[]{:T(128)S(6)} %select_n.106), kind=kLoop, calls=%fused_computation.19 | loop fusion | flops 589824 | bytes 1376260 | tf_op jit(solution)/shard_map/add | solution.py:40
  16.7 1.0 %add.94 = f32[502,64]{0,1:T(8,128)S(1)} add(f32[502,64]{0,1:T(8,128)} %fusion.1, f32[502,64]{0,1:T(8,128)} %collective-permute-done.2) | non-fusion elementwise | flops 32128 | bytes 385536 | tf_op jit(solution)/shard_map/add | solution.py:121
  17.8 1.9 %collective-permute-start.3 = (f32[251,64]{0,1:T(8,128)S(1)}, f32[251,64]{0,1:T(8,128)S(1)}, u32[]{:S(2)}, u32[]{:S(2)}) collective-permute-start(f32[251,64]{0,1:T(8,128)S(1)} %constant_dynamic-slice_fusion.1), channel_id=1, source_target_pairs={{0,128},{128,0},{1,129},{129,1},{2,130},{130,2},{3,131},{131,3},{4... | collective-permute-start | bytes 192776 | tf_op jit(solution)/shard_map/ppermute | solution.py:20
  19.7 8.3 %collective-permute-done.3 = f32[251,64]{0,1:T(8,128)S(1)} collective-permute-done((f32[251,64]{0,1:T(8,128)S(1)}, f32[251,64]{0,1:T(8,128)S(1)}, u32[]{:S(2)}, u32[]{:S(2)}) %collective-permute-start.3) | collective-permute-done | bytes 64288 | tf_op jit(solution)/shard_map/ppermute | solution.py:20
  28.7 0.9 %collective-permute-start.4 = (f32[251,64]{0,1:T(8,128)}, f32[251,64]{0,1:T(8,128)}, u32[]{:S(2)}, u32[]{:S(2)}) collective-permute-start(f32[251,64]{0,1:T(8,128)} %fusion.19), channel_id=1, source_target_pairs={{0,1},{1,0},{2,3},{3,2},{4,5},{5,4},{6,7},{7,6},{8,9},{9,8},{10,11... | collective-permute-start | bytes 192776 | tf_op jit(solution)/shard_map/ppermute | solution.py:20
  30.4 1.2 %collective-permute-start.1 = (f32[196,512]{1,0:T(8,128)}, f32[196,512]{1,0:T(8,128)}, u32[]{:S(2)}, u32[]{:S(2)}) collective-permute-start(f32[196,512]{1,0:T(8,128)} %pad_maximum_fusion), channel_id=1, source_target_pairs={{0,128},{128,0},{1,129},{129,1},{2,130},{130,2},{3,131},{131,3},{4... | collective-permute-start | bytes 1204232 | tf_op jit(solution)/shard_map/ppermute | solution.py:20
  31.6 1.8 %collective-permute-start.5 = (f32[251,512]{1,0:T(8,128)S(1)}, f32[251,512]{1,0:T(8,128)S(1)}, u32[]{:S(2)}, u32[]{:S(2)}) collective-permute-start(f32[251,512]{1,0:T(8,128)S(1)} %bitcast_subtract_fusion), channel_id=1, source_target_pairs={{0,128},{128,0},{1,129},{129,1},{2,130},{130,2},{3,131},{131,3},{4... | collective-permute-start | bytes 1542152 | tf_op jit(solution)/shard_map/ppermute | solution.py:20
  33.3 0.9 %broadcast_select_fusion.7 = (f32[251,64]{0,1:T(8,128)S(1)}, f32[251,64]{0,1:T(8,128)S(1)}) fusion(f32[251,64]{0,1:T(8,128)} %fusion.19, f32[251,64]{0,1:T(8,128)} %collective-permute-done.4, pred[]{:T(512)S(6)} %eq.20), kind=kLoop, calls=%fused_computation.37 | loop fusion | flops 32128 | bytes 257025 | tf_op jit(solution)/shard_map/jit(_where)/select_n | solution.py:24
  34.2 1.1 %convolution_multiply_fusion = f32[502,512]{1,0:T(8,128)S(1)} fusion(f32[251,64]{0,1:T(8,128)S(1)} %get-tuple-element.67, f32[251,64]{0,1:T(8,128)S(1)} %get-tuple-element.66, f32[1024,64]{0,1:T(8,128)S(1)} %copy-done.7, s32[]{:T(128)S(6)} %select_n.123), kind=kOutput, calls=%fused_computation.1 | convolution fusion | flops 197683584 | bytes 1290244 | tf_op jit(solution)/shard_map/dot_general | solution.py:131
  35.6 1.5 %reshape_add_fusion = f32[1,1,251,512]{3,1,2,0:T(1,128)} fusion(f32[251,512]{1,0:T(8,128)S(1)} %get-tuple-element.44, f32[1,1,251,512]{3,1,2,0:T(1,128)S(1)} %copy-done.2), kind=kLoop, calls=%fused_computation.14 | loop fusion | flops 257024 | bytes 1542144 | tf_op jit(solution)/shard_map/add | solution.py:142
  37.1 1.3 %copy.25 = f32[1,1,251,512]{3,1,2,0:T(1,128)} copy(f32[1,1,251,512]{3,2,1,0:T(8,128)S(1)} %get-tuple-element.40) | data formatting | bytes 1028096
  38.4 4.8 %collective-permute-done.1 = f32[196,512]{1,0:T(8,128)} collective-permute-done((f32[196,512]{1,0:T(8,128)}, f32[196,512]{1,0:T(8,128)}, u32[]{:S(2)}, u32[]{:S(2)}) %collective-permute-start.1) | collective-permute-done | bytes 401440 | tf_op jit(solution)/shard_map/ppermute | solution.py:20
  43.2 1.4 %broadcast_select_fusion.9 = (f32[2,512]{1,0:T(2,128)S(1)}, f32[2,512]{1,0:T(2,128)S(1)}, f32[2,512]{1,0:T(2,128)}, f32[2,512]{1,0:T(2,128)}, f32[2,512]{1,0:T(2,128)S(1)}, /*index=5*/f32[2,512]{1,0:T(2,128)S(1)}) fusion(f32[2,512]{1,0:T(2,128)S(1)} %get-tuple-element.70, pred[]{:T(512)S(6)} %eq.19, f32[196,512]{1,0:T(8,128)} %collective-permute-done.1, ...), kind=kLoop, calls=%fused_computation.44 | loop fusion | flops 11264 | bytes 53249 | tf_op jit(solution)/shard_map/jit(_where)/select_n | solution.py:24
  45.2 1.0 %slice.12 = f32[192,512]{1,0:T(8,128)S(1)} slice(f32[196,512]{1,0:T(8,128)} %collective-permute-done.1), slice={[0:192], [0:512]} | slice | bytes 786432 | tf_op jit(solution)/shard_map/slice | solution.py:84
  46.2 2.3 %broadcast_select_fusion.3 = (f32[12,16,512]{2,1,0:T(8,128)S(1)}, f32[12,16,512]{2,1,0:T(8,128)S(1)}, f32[12,16,512]{2,1,0:T(8,128)}, f32[12,16,512]{2,1,0:T(8,1...) fusion(f32[12,16,512]{2,1,0:T(8,128)} %collective-permute-done, f32[12,16,512]{2,1,0:T(8,128)} %get-tuple-element.64, ...), kind=kLoop, calls=%fused_computation.25 | loop fusion | flops 1081344 | bytes 5111809 | tf_op jit(solution)/shard_map/jit(_where)/select_n | solution.py:24
  48.6 1.0 %maximum_add_fusion = f32[24,16,512]{2,1,0:T(8,128)} fusion(f32[12,16,512]{2,1,0:T(8,128)S(1)} %get-tuple-element.62, f32[12,16,512]{2,1,0:T(8,128)S(1)} %get-tuple-element.63, f32[12,16,512]{2,1,0:T(8,128)S(1)} %get-tuple-element.48, f32[12,16,512]{2,1,0:T(8,128)S(1)} %get-tuple-element.47), kind=kLoop, calls=%fused_computation.7 | loop fusion | flops 786432 | bytes 2359296 | tf_op jit(solution)/shard_map/add | solution.py:48
  49.6 4.7 %collective-permute-done.5 = f32[251,512]{1,0:T(8,128)S(1)} collective-permute-done((f32[251,512]{1,0:T(8,128)S(1)}, f32[251,512]{1,0:T(8,128)S(1)}, u32[]{:S(2)}, u32[]{:S(2)}) %collective-permute-start.5) | collective-permute-done | bytes 514080 | tf_op jit(solution)/shard_map/ppermute | solution.py:20
  54.4 1.2 %maximum_subtract_fusion = f32[502,512]{1,0:T(8,128)} fusion(f32[251,512]{1,0:T(8,128)S(1)} %get-tuple-element.46, f32[251,512]{1,0:T(8,128)S(1)} %get-tuple-element.45, f32[502,512]{1,0:T(8,128)S(1)} %convolution_multiply_fusion), kind=kLoop, calls=%fused_computation.6 | loop fusion | flops 771072 | bytes 3084288 | tf_op jit(solution)/shard_map/sub | solution.py:144
  (39 shorter events, 2.8 us)
Async XLA Ops:
  0.6 7.1 %copy-start = (bf16[1,502,512]{2,1,0:T(8,128)(2,1)S(1)}, bf16[1,502,512]{2,1,0:T(8,128)(2,1)}, u32[]{:S(2)}) copy-start(bf16[1,502,512]{2,1,0:T(8,128)(2,1)} %param.19) | copy-start | bytes 1542148
  0.7 12.6 %copy-start.6 = (bf16[1,24,16,512]{3,2,1,0:T(8,128)(2,1)S(1)}, bf16[1,24,16,512]{3,2,1,0:T(8,128)(2,1)}, u32[]{:S(2)}) copy-start(bf16[1,24,16,512]{3,2,1,0:T(8,128)(2,1)} %param.13) | copy-start | bytes 1179652
  7.8 7.7 %copy-start.1 = (f32[1,1,251,512]{3,1,2,0:T(1,128)S(1)}, f32[1,1,251,512]{3,1,2,0:T(1,128)}, u32[]{:S(2)}) copy-start(f32[1,1,251,512]{3,1,2,0:T(1,128)} %param.17) | copy-start | bytes 1542148
  7.8 7.6 %copy-start.2 = (f32[1,1,251,512]{3,1,2,0:T(1,128)S(1)}, f32[1,1,251,512]{3,1,2,0:T(1,128)}, u32[]{:S(2)}) copy-start(f32[1,1,251,512]{3,1,2,0:T(1,128)} %param.18) | copy-start | bytes 1542148
  10.0 6.7 %collective-permute-start.2 = (f32[502,64]{0,1:T(8,128)}, f32[502,64]{0,1:T(8,128)}, u32[]{:S(2)}, u32[]{:S(2)}) collective-permute-start(f32[502,64]{0,1:T(8,128)} %fusion.1), channel_id=1, source_target_pairs={{0,1},{1,0},{2,3},{3,2},{4,5},{5,4},{6,7},{7,6},{8,9},{9,8},{10,11... | collective-permute-start | bytes 385544 | tf_op jit(solution)/shard_map/ppermute | solution.py:20
  14.2 1.4 %copy-start.3 = (f32[12,16,512]{2,1,0:T(8,128)S(1)}, f32[12,16,512]{2,1,0:T(8,128)}, u32[]{:S(2)}) copy-start(f32[12,16,512]{2,1,0:T(8,128)} %param.11) | copy-start | bytes 1179652
  14.2 1.4 %copy-start.4 = (f32[12,16,512]{2,1,0:T(8,128)S(1)}, f32[12,16,512]{2,1,0:T(8,128)}, u32[]{:S(2)}) copy-start(f32[12,16,512]{2,1,0:T(8,128)} %param.12) | copy-start | bytes 1179652
  14.2 32.0 %collective-permute-start = (f32[12,16,512]{2,1,0:T(8,128)}, f32[12,16,512]{2,1,0:T(8,128)}, u32[]{:S(2)}, u32[]{:S(2)}) collective-permute-start(f32[12,16,512]{2,1,0:T(8,128)} %get-tuple-element.64), channel_id=1, source_target_pairs={{0,128},{128,0},{1,129},{129,1},{2,130},{130,2},{3,131},{131,3},{4... | collective-permute-start | bytes 1179656 | tf_op jit(solution)/shard_map/ppermute | solution.py:20
  15.5 1.1 %copy-start.8 = (f32[2,512]{1,0:T(2,128)S(1)}, f32[2,512]{1,0:T(2,128)}, u32[]{:S(2)}) copy-start(f32[2,512]{1,0:T(2,128)} %param.15) | copy-start | bytes 12292
  15.5 1.1 %copy-start.9 = (f32[2,512]{1,0:T(2,128)S(1)}, f32[2,512]{1,0:T(2,128)}, u32[]{:S(2)}) copy-start(f32[2,512]{1,0:T(2,128)} %param.14) | copy-start | bytes 12292
  15.6 1.1 %copy-start.10 = (bf16[1,4,512]{2,1,0:T(4,128)(2,1)S(1)}, bf16[1,4,512]{2,1,0:T(4,128)(2,1)}, u32[]{:S(2)}) copy-start(bf16[1,4,512]{2,1,0:T(4,128)(2,1)} %param.16) | copy-start | bytes 12292
  16.7 17.5 %copy-start.7 = (f32[1024,64]{0,1:T(8,128)S(1)}, f32[1024,64]{0,1:T(8,128)}, u32[]{:S(2)}) copy-start(f32[1024,64]{0,1:T(8,128)} %param.20) | copy-start | bytes 786436
  17.8 10.2 %collective-permute-start.3 = (f32[251,64]{0,1:T(8,128)S(1)}, f32[251,64]{0,1:T(8,128)S(1)}, u32[]{:S(2)}, u32[]{:S(2)}) collective-permute-start(f32[251,64]{0,1:T(8,128)S(1)} %constant_dynamic-slice_fusion.1), channel_id=1, source_target_pairs={{0,128},{128,0},{1,129},{129,1},{2,130},{130,2},{3,131},{131,3},{4... | collective-permute-start | bytes 192776 | tf_op jit(solution)/shard_map/ppermute | solution.py:20
  28.7 4.6 %collective-permute-start.4 = (f32[251,64]{0,1:T(8,128)}, f32[251,64]{0,1:T(8,128)}, u32[]{:S(2)}, u32[]{:S(2)}) collective-permute-start(f32[251,64]{0,1:T(8,128)} %fusion.19), channel_id=1, source_target_pairs={{0,1},{1,0},{2,3},{3,2},{4,5},{5,4},{6,7},{7,6},{8,9},{9,8},{10,11... | collective-permute-start | bytes 192776 | tf_op jit(solution)/shard_map/ppermute | solution.py:20
  30.4 12.8 %collective-permute-start.1 = (f32[196,512]{1,0:T(8,128)}, f32[196,512]{1,0:T(8,128)}, u32[]{:S(2)}, u32[]{:S(2)}) collective-permute-start(f32[196,512]{1,0:T(8,128)} %pad_maximum_fusion), channel_id=1, source_target_pairs={{0,128},{128,0},{1,129},{129,1},{2,130},{130,2},{3,131},{131,3},{4... | collective-permute-start | bytes 1204232 | tf_op jit(solution)/shard_map/ppermute | solution.py:20
  31.6 22.8 %collective-permute-start.5 = (f32[251,512]{1,0:T(8,128)S(1)}, f32[251,512]{1,0:T(8,128)S(1)}, u32[]{:S(2)}, u32[]{:S(2)}) collective-permute-start(f32[251,512]{1,0:T(8,128)S(1)} %bitcast_subtract_fusion), channel_id=1, source_target_pairs={{0,128},{128,0},{1,129},{129,1},{2,130},{130,2},{3,131},{131,3},{4... | collective-permute-start | bytes 1542152 | tf_op jit(solution)/shard_map/ppermute | solution.py:20
  37.1 9.2 %copy-start.5 = (f32[12,16,512]{2,1,0:T(8,128)S(1)}, f32[12,16,512]{2,1,0:T(8,128)}, u32[]{:S(2)}) copy-start(f32[12,16,512]{2,1,0:T(8,128)} %get-tuple-element.18) | copy-start | bytes 1179652

commit v2 on v1

--- a/solution.py
+++ b/solution.py
@@ -14,6 +14,7 @@
 STEP = OUTER_RATE * (1.0 + MOMENTUM)
 
 SWAP = [(0, 1), (1, 0)]
+LOW = 32
 
 
 def swap(x, axis):
@@ -74,21 +75,11 @@
     norm_parts = (given_norm,) + outer_partial(norm_global, norm_momentum, norm_inner[0], rep_index)
     attn_parts = (attn_parts[1], attn_parts[0], attn_parts[2])
     norm_parts = (norm_parts[1], norm_parts[0], norm_parts[2])
-    norm_rows = given_norm.shape[0]
-    sent = jnp.concatenate(
-        [attn_parts[2].reshape(-1, width), given_norm, norm_parts[2]], axis=0
-    )
-    sent = lax.optimization_barrier(sent)
-    got = swap(sent, "rep")
-    attn_rows = attn_parts[2].size // width
-    got_attn_partial = got[:attn_rows].reshape(attn_global.shape)
-    got_norm_inner = got[attn_rows : attn_rows + norm_rows]
-    got_norm_partial = got[attn_rows + norm_rows :]
+    sent = lax.optimization_barrier(attn_parts[2])
+    norm_sent = jnp.concatenate([given_norm, norm_parts[2]], axis=0)
+    got_attn_partial = swap(sent, "rep")
     new_attn_global, new_attn_momentum, attn_weights = outer_finish(
         attn_global, attn_momentum, *attn_parts, got_attn_inner, got_attn_partial, first_is_own
-    )
-    new_norm_global, new_norm_momentum, norm_weights = outer_finish(
-        norm_global, norm_momentum, *norm_parts, got_norm_inner, got_norm_partial, first_is_own
     )
 
     block_rows = emb_inner.shape[1]
@@ -96,9 +87,20 @@
     half_width = emb_global.shape[3]
     row_start = lax.axis_index("fsdp") * block_rows
     half_start = rep_index * half_rows
-    positions = row_start + jnp.arange(block_rows, dtype=jnp.int32)
-    matches = touched[:, :, None] == positions[None, None, :]
-    touched_masks = jnp.any(matches, axis=1).astype(jnp.float32)
+    offsets = touched - row_start
+    inside = (offsets >= 0) & (offsets < block_rows)
+    high_count = -(-block_rows // LOW)
+    high_hot = (
+        (offsets[:, None, :] // LOW) == jnp.arange(high_count, dtype=jnp.int32)[None, :, None]
+    ) & inside[:, None, :]
+    low_hot = (offsets[:, None, :] % LOW) == jnp.arange(LOW, dtype=jnp.int32)[None, :, None]
+    hits = jnp.einsum(
+        "gik,gjk->gij",
+        high_hot.astype(jnp.bfloat16),
+        low_hot.astype(jnp.bfloat16),
+        preferred_element_type=jnp.float32,
+    )
+    touched_masks = (hits > 0).astype(jnp.float32).reshape(hits.shape[0], -1)[:, :block_rows]
     counts = jnp.sum(touched_masks, axis=0)
     own_mask = lax.dynamic_index_in_dim(touched_masks, rep_index, 0, keepdims=False)
     half_counts = lax.dynamic_slice_in_dim(counts, half_start, half_rows, 0)
@@ -124,7 +126,15 @@
     tp_index = lax.axis_index("tp")
     chip_rows = coeff_chip.shape[0] // 2
     coeff_mine = lax.dynamic_slice_in_dim(coeff_chip, tp_index * chip_rows, chip_rows, 0)
-    coeff_half = coeff_mine + swap(coeff_mine, "rep")
+    coeff_width = coeff_mine.shape[1]
+    coeff_sent = jnp.concatenate([coeff_mine, norm_sent.reshape(-1, coeff_width)], axis=0)
+    coeff_got = swap(coeff_sent, "rep")
+    coeff_half = coeff_mine + coeff_got[:chip_rows]
+    norm_rows = given_norm.shape[0]
+    norm_got = coeff_got[chip_rows:].reshape(-1, width)
+    new_norm_global, new_norm_momentum, norm_weights = outer_finish(
+        norm_global, norm_momentum, *norm_parts, norm_got[:norm_rows], norm_got[norm_rows:], first_is_own
+    )
     coeff_sum = place_pair(tp_index == 0, coeff_half, swap(coeff_half, "tp"))
     got_rows = swap(kept_rows, "rep")
     emb_grad = (
@@ -140,8 +150,12 @@
     own_grad = lax.dynamic_slice_in_dim(emb_grad, half_start, half_rows, 0).reshape(emb_global.shape)
     new_emb_global = (emb_global - DECAY * emb_momentum) - STEP * own_grad
     new_emb_momentum = MOMENTUM * emb_momentum + own_grad
-    new_emb_global, new_emb_momentum = lax.optimization_barrier((new_emb_global, new_emb_momentum))
-    emb_weights = place_pair(first_is_own, kept_rows, got_rows) - STEP * emb_grad
+    own_flat = kept_rows - STEP * lax.dynamic_slice_in_dim(emb_grad, half_start, half_rows, 0)
+    other_grad = lax.dynamic_slice_in_dim(emb_grad, (1 - rep_index) * half_rows, half_rows, 0)
+    new_emb_global, new_emb_momentum, own_flat, other_grad = lax.optimization_barrier(
+        (new_emb_global, new_emb_momentum, own_flat, other_grad)
+    )
+    emb_weights = place_pair(first_is_own, own_flat, got_rows - STEP * other_grad)
     return (
         new_attn_global,
         new_attn_momentum,

time: 56 us -> 44.9 us (0.80)
  waiting for transfers between devices: 17.8 us -> 2.8 us
  local copies, waits for them, and re-layouts: 2.58 us -> 9.6 us
  other arithmetic: 19.1 us -> 17.1 us
  matrix products: 5.11 us -> 3.63 us
    ppermute x6, waiting for transfers between devices: 17.8 us -> 2.8 us  [swap(): return lax.ppermute(x, axis, perm=SWAP)]
    reduce_or x1 -> x0, other arithmetic: 5.2 us -> none  [step_body(): touched_masks = jnp.any(matches, axis=1).astype(jnp.float32)]
    slice x1 -> x5, local copies, waits for them, and re-layouts: 1.02 us -> 5.84 us  [the longest x3 3.05 us: step_body(): norm_got[norm_rows:]]
    reshape x0 -> x3, local copies, waits for them, and re-layouts: none -> 1.57 us  [the longest x2 1.48 us: step_body(): norm_sent.reshape(-1, coeff_width)]
    convert_element_type x2, other arithmetic: 0.98 us -> 2.54 us  [outer_sends(): given_inner = lax.dynamic_slice_in_dim(inner_all, (1 - rep_index) * owned...]
    dot_general x1, matrix products: 1.72 us -> 0.61 us  [step_body(): jnp.dot(own_rows, basis_half, precision=lax.Precision.HIGHEST, preferred_...]
    concatenate x1 -> x3, other arithmetic: 0.78 us -> 1.8 us  [the longest x1 1.06 us: place_pair(): return jnp.concatenate([first, second], axis=0)]
    dot_general x1, matrix products: 2.25 us -> 1.26 us  [step_body(): jnp.dot(emb_inner[0].astype(jnp.float32), basis_half, precision=lax.Preci...]
  transfers between devices with their start and end apart: 6 -> 6, of which waited for: 3 -> 1; matrix products, arithmetic and copies ran while one was open for 29% -> 58% of each run, Pallas kernels for 0% -> 0%
where the time goes in v2:
time: 44.9 us; the launch traced here: 44.3 us
  other arithmetic  17.1 us (38%)
  starting transfers between devices  10.4 us (23%)
  local copies, waits for them, and re-layouts  9.6 us (21%)
  matrix products  3.63 us (8%)
  waiting for transfers between devices  2.8 us (6%)
  between operations  0.85 us (2%)
    ppermute x6, starting transfers between devices, swap(): return lax.ppermute(x, axis, perm=SWAP)  10.4 us
    select_n x4, other arithmetic, place_pair(): first = jnp.where(first_is_own, own, other)  4.97 us
    slice x3, local copies, waits for them, and re-layouts, step_body(): norm_got[norm_rows:]  3.05 us
    ppermute x6, waiting for transfers between devices, swap(): return lax.ppermute(x, axis, perm=SWAP)  2.8 us
    slice x2, local copies, waits for them, and re-layouts, step_body(): norm_got[:norm_rows]  2.79 us
    convert_element_type x2, other arithmetic, outer_sends(): given_inner = lax.dynamic_slice_in_dim(inner_all, (1 - rep_index) * owned...  2.54 us
    unnamed x25, local copies, waits for them, and re-layouts  2.02 us
    add x2, other arithmetic, outer_partial(): partial = KEEP * global_part - DECAY * momentum_part + SHARE * own_inner  1.81 us
  transfers between devices with their start and end apart: 6, of which 1 were waited for; matrix products, arithmetic and copies ran while one was open for 58% of the time, Pallas kernels for 0%

profile of v2, /device:TPU:1, one launch (start us, length us, event | category | flops | bytes accessed | tf_op | source)
XLA Modules:
  0.0 44.3 jit_solution(1090858553528585196)
XLA Ops:
  0.7 1.9 %bitcast_convert_fusion = (f32[12,16,512]{2,1,0:T(8,128)S(1)}, f32[12,16,512]{2,1,0:T(8,128)}) fusion(bf16[1,24,16,512]{3,2,1,0:T(8,128)(2,1)} %param.13, s32[]{:T(128)S(6)} %select_n.125, s32[]{:T(128)S(6)} %select_n.124), kind=kLoop, calls=%fused_computation.30 | loop fusion | flops 196608 | bytes 1179656 | tf_op jit(solution)/shard_map/convert_element_type | solution.py:34
  2.6 3.7 %collective-permute-start = (f32[12,16,512]{2,1,0:T(8,128)S(1)}, f32[12,16,512]{2,1,0:T(8,128)}, u32[]{:S(2)}, u32[]{:S(2)}) collective-permute-start(f32[12,16,512]{2,1,0:T(8,128)S(1)} %get-tuple-element.60), channel_id=1, source_target_pairs={{0,128},{128,0},{1,129},{129,1},{2,130},{130,2},{3,131},{131,3},{4... | collective-permute-start | bytes 1179656 | tf_op jit(solution)/shard_map/ppermute | solution.py:21
  8.2 1.3 %fusion.2 = f32[502,64]{0,1:T(8,128)} fusion(bf16[1,502,512]{2,1,0:T(8,128)(2,1)S(1)} %copy-done, f32[251,64]{0,1:T(8,128)S(1)} %get-tuple-element.67, f32[251,64]{0,1:T(8,128)S(1)} %get-tuple-element.66, f32[1024,64]{0,1:T(8,128)S(1)} %copy-done.6, s32[]{:T(128)S(6)} %select_n.136, f32[502]{0:T(512)S(1)} %bitcast.42), kind=kOutput, calls=%fused_computation.5 | convolution fusion | flops 197490816 | bytes 908804 | tf_op jit(solution)/shard_map/dot_general | solution.py:113
  9.4 1.0 %collective-permute-start.2 = (f32[502,64]{0,1:T(8,128)}, f32[502,64]{0,1:T(8,128)}, u32[]{:S(2)}, u32[]{:S(2)}) collective-permute-start(f32[502,64]{0,1:T(8,128)} %fusion.2), channel_id=1, source_target_pairs={{0,1},{1,0},{2,3},{3,2},{4,5},{5,4},{6,7},{7,6},{8,9},{9,8},{10,11... | collective-permute-start | bytes 385544 | tf_op jit(solution)/shard_map/ppermute | solution.py:21
  11.9 0.8 %copy.24 = f32[32,64]{0,1:T(8,128)S(1)} copy(f32[32,64]{1,0:T(8,128)} %reshape.77) | data formatting | bytes 16384 | tf_op jit(solution)/shard_map/reshape | solution.py:130
  12.7 1.0 %add.91 = f32[502,64]{0,1:T(8,128)S(1)} add(f32[502,64]{0,1:T(8,128)} %fusion.2, f32[502,64]{0,1:T(8,128)} %collective-permute-done.2) | non-fusion elementwise | flops 32128 | bytes 385536 | tf_op jit(solution)/shard_map/add | solution.py:123
  15.1 1.8 %collective-permute-start.3 = (f32[283,64]{0,1:T(8,128)}, f32[283,64]{0,1:T(8,128)}, u32[]{:S(2)}, u32[]{:S(2)}) collective-permute-start(f32[283,64]{0,1:T(8,128)} %pad_maximum_fusion.1), channel_id=1, source_target_pairs={{0,128},{128,0},{1,129},{129,1},{2,130},{130,2},{3,131},{131,3},{4... | collective-permute-start | bytes 217352 | tf_op jit(solution)/shard_map/ppermute | solution.py:21
  16.9 1.8 %multiply_add_fusion.1 = f32[12,16,512]{2,1,0:T(8,128)} fusion(f32[12,16,512]{2,1,0:T(8,128)S(1)} %copy-done.4, f32[12,16,512]{2,1,0:T(8,128)S(1)} %copy-done.3, bf16[1,24,16,512]{3,2,1,0:T(8,128)(2,1)} %param.13, s32[]{:T(128)S(6)} %select_n.124), kind=kLoop, calls=%fused_computation.27 | loop fusion | flops 589824 | bytes 1376260 | tf_op jit(solution)/shard_map/add | solution.py:41
  18.7 1.2 %collective-permute-start.1 = (f32[12,16,512]{2,1,0:T(8,128)}, f32[12,16,512]{2,1,0:T(8,128)}, u32[]{:S(2)}, u32[]{:S(2)}) collective-permute-start(f32[12,16,512]{2,1,0:T(8,128)} %multiply_add_fusion.1), channel_id=1, source_target_pairs={{0,128},{128,0},{1,129},{129,1},{2,130},{130,2},{3,131},{131,3},{4... | collective-permute-start | bytes 1179656 | tf_op jit(solution)/shard_map/ppermute | solution.py:21
  19.9 1.8 %collective-permute-start.5 = (f32[251,512]{1,0:T(8,128)S(1)}, f32[251,512]{1,0:T(8,128)}, u32[]{:S(2)}, u32[]{:S(2)}) collective-permute-start(f32[251,512]{1,0:T(8,128)S(1)} %bitcast_subtract_fusion), channel_id=1, source_target_pairs={{0,128},{128,0},{1,129},{129,1},{2,130},{130,2},{3,131},{131,3},{4... | collective-permute-start | bytes 1542152 | tf_op jit(solution)/shard_map/ppermute | solution.py:21
  21.7 1.6 %fusion.27 = (f32[16,64]{0,1:T(8,128)S(1)}, f32[16,64]{0,1:T(8,128)}) fusion(f32[283,64]{0,1:T(8,128)} %collective-permute-done.3), kind=kLoop, calls=%fused_computation.82 | loop fusion | bytes 16384 | tf_op jit(solution)/shard_map/slice | solution.py:136
  23.3 1.4 %copy.25 = f32[16,64]{1,0:T(8,128)} copy(f32[16,64]{0,1:T(8,128)} %get-tuple-element.65) | data formatting | bytes 8192 | tf_op jit(solution)/shard_map/slice | solution.py:136
  24.7 1.4 %slice.27 = f32[2,512]{1,0:T(2,128)} reshape(f32[16,64]{1,0:T(8,128)} %copy.25) | data formatting | bytes 8192 | tf_op jit(solution)/shard_map/slice | solution.py:136
  27.5 1.0 %slice_add_fusion = f32[251,64]{0,1:T(8,128)S(1)} fusion(f32[283,64]{0,1:T(8,128)} %collective-permute-done.3, f32[502,64]{0,1:T(8,128)} %copy-done.7, s32[]{:T(128)S(6)} %select_n.142), kind=kLoop, calls=%fused_computation.49 | loop fusion | flops 16064 | bytes 192772 | tf_op jit(solution)/shard_map/add | solution.py:132
  28.5 0.9 %collective-permute-start.4 = (f32[251,64]{0,1:T(8,128)S(1)}, f32[251,64]{0,1:T(8,128)S(1)}, u32[]{:S(2)}, u32[]{:S(2)}) collective-permute-start(f32[251,64]{0,1:T(8,128)S(1)} %slice_add_fusion), channel_id=1, source_target_pairs={{0,1},{1,0},{2,3},{3,2},{4,5},{5,4},{6,7},{7,6},{8,9},{9,8},{10,11... | collective-permute-start | bytes 192776 | tf_op jit(solution)/shard_map/ppermute | solution.py:21
  29.5 1.3 %broadcast_select_fusion.9 = (f32[2,512]{1,0:T(2,128)S(1)}, f32[2,512]{1,0:T(2,128)S(1)}, f32[2,512]{1,0:T(2,128)}, f32[2,512]{1,0:T(2,128)}, f32[2,512]{1,0:T(2,128)S(1)}, /*index=5*/f32[2,512]{1,0:T(2,128)S(1)}) fusion(f32[2,512]{1,0:T(2,128)} %slice.27, f32[2,512]{1,0:T(2,128)S(1)} %get-tuple-element.78, pred[]{:T(512)S(6)} %eq.34, f32[2,512]{1,0:T(2,128)} %param.14, ...), kind=kLoop, calls=%fused_computation.64 | loop fusion | flops 11264 | bytes 53249 | tf_op jit(solution)/shard_map/jit(_where)/select_n | solution.py:25
  31.4 1.1 %convolution_multiply_fusion = f32[502,512]{1,0:T(8,128)S(1)} fusion(f32[251,64]{0,1:T(8,128)S(1)} %get-tuple-element.63, f32[251,64]{0,1:T(8,128)S(1)} %get-tuple-element.62, f32[1024,64]{0,1:T(8,128)S(1)} %copy-done.6, s32[]{:T(128)S(6)} %select_n.136), kind=kOutput, calls=%fused_computation.2 | convolution fusion | flops 197683584 | bytes 1290244 | tf_op jit(solution)/shard_map/dot_general | solution.py:141
  33.0 1.5 %reshape_add_fusion = f32[1,1,251,512]{3,1,2,0:T(1,128)} fusion(f32[251,512]{1,0:T(8,128)S(1)} %get-tuple-element.48, f32[1,1,251,512]{3,1,2,0:T(1,128)S(1)} %copy-done.2), kind=kLoop, calls=%fused_computation.22 | loop fusion | flops 257024 | bytes 1542144 | tf_op jit(solution)/shard_map/add | solution.py:152
  34.5 1.3 %copy.28 = f32[1,1,251,512]{3,1,2,0:T(1,128)} copy(f32[1,1,251,512]{3,2,1,0:T(8,128)S(1)} %bitcast_subtract_fusion.1) | data formatting | bytes 1028096
  35.8 2.5 %broadcast_select_fusion.3 = (f32[12,16,512]{2,1,0:T(8,128)S(1)}, f32[12,16,512]{2,1,0:T(8,128)S(1)}, f32[12,16,512]{2,1,0:T(8,128)}, f32[12,16,512]{2,1,0:T(8,1...) fusion(f32[12,16,512]{2,1,0:T(8,128)} %collective-permute-done, f32[12,16,512]{2,1,0:T(8,128)S(1)} %get-tuple-element.60, ...), kind=kLoop, calls=%fused_computation.33 | loop fusion | flops 1081344 | bytes 5111809 | tf_op jit(solution)/shard_map/jit(_where)/select_n | solution.py:25
  38.3 1.0 %maximum_add_fusion = f32[24,16,512]{2,1,0:T(8,128)} fusion(f32[12,16,512]{2,1,0:T(8,128)S(1)} %get-tuple-element.58, f32[12,16,512]{2,1,0:T(8,128)S(1)} %get-tuple-element.59, f32[12,16,512]{2,1,0:T(8,128)S(1)} %get-tuple-element.53, f32[12,16,512]{2,1,0:T(8,128)S(1)} %get-tuple-element.52), kind=kLoop, calls=%fused_computation.12 | loop fusion | flops 786432 | bytes 2359296 | tf_op jit(solution)/shard_map/add | solution.py:49
  39.3 2.8 %collective-permute-done.5 = f32[251,512]{1,0:T(8,128)} collective-permute-done((f32[251,512]{1,0:T(8,128)S(1)}, f32[251,512]{1,0:T(8,128)}, u32[]{:S(2)}, u32[]{:S(2)}) %collective-permute-start.5) | collective-permute-done | bytes 514080 | tf_op jit(solution)/shard_map/ppermute | solution.py:21
  42.1 1.2 %broadcast_select_fusion.1 = (f32[251,512]{1,0:T(8,128)S(1)}, f32[251,512]{1,0:T(8,128)S(1)}) fusion(f32[251,512]{1,0:T(8,128)S(1)} %get-tuple-element.27, pred[]{:T(512)S(6)} %eq.34, f32[251,512]{1,0:T(8,128)} %collective-permute-done.5, f32[251,512]{1,0:T(8,128)S(1)} %get-tuple-element.28), kind=kLoop, calls=%fused_computation.29 | loop fusion | flops 514048 | bytes 2570241 | tf_op jit(solution)/shard_map/jit(_where)/select_n | solution.py:25
  43.3 1.1 %pad_maximum_fusion = f32[502,512]{1,0:T(8,128)} fusion(f32[251,512]{1,0:T(8,128)S(1)} %get-tuple-element.50, f32[251,512]{1,0:T(8,128)S(1)} %get-tuple-element.49), kind=kLoop, calls=%fused_computation.11 | loop fusion | flops 257024 | bytes 2056192 | tf_op jit(solution)/shard_map/concatenate | solution.py:27
  (51 shorter events, 7.2 us)
Async XLA Ops:
  0.6 7.5 %copy-start = (bf16[1,502,512]{2,1,0:T(8,128)(2,1)S(1)}, bf16[1,502,512]{2,1,0:T(8,128)(2,1)}, u32[]{:S(2)}) copy-start(bf16[1,502,512]{2,1,0:T(8,128)(2,1)} %param.19) | copy-start | bytes 1542148
  0.7 5.7 %copy-start.8 = (s32[2,8192]{1,0:T(2,128)S(1)}, s32[2,8192]{1,0:T(2,128)}, u32[]{:S(2)}) copy-start(s32[2,8192]{1,0:T(2,128)} %param.21) | copy-start | bytes 196612
  2.6 4.9 %copy-start.1 = (f32[1,1,251,512]{3,1,2,0:T(1,128)S(1)}, f32[1,1,251,512]{3,1,2,0:T(1,128)}, u32[]{:S(2)}) copy-start(f32[1,1,251,512]{3,1,2,0:T(1,128)} %param.17) | copy-start | bytes 1542148
  2.6 4.9 %copy-start.6 = (f32[1024,64]{0,1:T(8,128)S(1)}, f32[1024,64]{0,1:T(8,128)}, u32[]{:S(2)}) copy-start(f32[1024,64]{0,1:T(8,128)} %param.20) | copy-start | bytes 786436
  2.6 33.2 %collective-permute-start = (f32[12,16,512]{2,1,0:T(8,128)S(1)}, f32[12,16,512]{2,1,0:T(8,128)}, u32[]{:S(2)}, u32[]{:S(2)}) collective-permute-start(f32[12,16,512]{2,1,0:T(8,128)S(1)} %get-tuple-element.60), channel_id=1, source_target_pairs={{0,128},{128,0},{1,129},{129,1},{2,130},{130,2},{3,131},{131,3},{4... | collective-permute-start | bytes 1179656 | tf_op jit(solution)/shard_map/ppermute | solution.py:21
  7.3 3.1 %copy-start.2 = (f32[1,1,251,512]{3,1,2,0:T(1,128)S(1)}, f32[1,1,251,512]{3,1,2,0:T(1,128)}, u32[]{:S(2)}) copy-start(f32[1,1,251,512]{3,1,2,0:T(1,128)} %param.18) | copy-start | bytes 1542148
  8.1 2.4 %copy-start.9 = (f32[2,512]{1,0:T(2,128)S(1)}, f32[2,512]{1,0:T(2,128)}, u32[]{:S(2)}) copy-start(f32[2,512]{1,0:T(2,128)} %param.15) | copy-start | bytes 12292
  8.1 2.4 %copy-start.10 = (f32[2,512]{1,0:T(2,128)S(1)}, f32[2,512]{1,0:T(2,128)}, u32[]{:S(2)}) copy-start(f32[2,512]{1,0:T(2,128)} %param.14) | copy-start | bytes 12292
  8.2 2.4 %copy-start.11 = (bf16[1,4,512]{2,1,0:T(4,128)(2,1)S(1)}, bf16[1,4,512]{2,1,0:T(4,128)(2,1)}, u32[]{:S(2)}) copy-start(bf16[1,4,512]{2,1,0:T(4,128)(2,1)} %param.16) | copy-start | bytes 12292
  9.4 3.2 %collective-permute-start.2 = (f32[502,64]{0,1:T(8,128)}, f32[502,64]{0,1:T(8,128)}, u32[]{:S(2)}, u32[]{:S(2)}) collective-permute-start(f32[502,64]{0,1:T(8,128)} %fusion.2), channel_id=1, source_target_pairs={{0,1},{1,0},{2,3},{3,2},{4,5},{5,4},{6,7},{7,6},{8,9},{9,8},{10,11... | collective-permute-start | bytes 385544 | tf_op jit(solution)/shard_map/ppermute | solution.py:21
  10.4 6.5 %copy-start.3 = (f32[12,16,512]{2,1,0:T(8,128)S(1)}, f32[12,16,512]{2,1,0:T(8,128)}, u32[]{:S(2)}) copy-start(f32[12,16,512]{2,1,0:T(8,128)} %param.11) | copy-start | bytes 1179652
  10.4 6.5 %copy-start.4 = (f32[12,16,512]{2,1,0:T(8,128)S(1)}, f32[12,16,512]{2,1,0:T(8,128)}, u32[]{:S(2)}) copy-start(f32[12,16,512]{2,1,0:T(8,128)} %param.12) | copy-start | bytes 1179652
  13.7 0.7 %copy-start.7 = (f32[502,64]{0,1:T(8,128)}, f32[502,64]{0,1:T(8,128)S(1)}, u32[]{:S(2)}) copy-start(f32[502,64]{0,1:T(8,128)S(1)} %add.91) | copy-start | bytes 385540
  15.1 6.5 %collective-permute-start.3 = (f32[283,64]{0,1:T(8,128)}, f32[283,64]{0,1:T(8,128)}, u32[]{:S(2)}, u32[]{:S(2)}) collective-permute-start(f32[283,64]{0,1:T(8,128)} %pad_maximum_fusion.1), channel_id=1, source_target_pairs={{0,128},{128,0},{1,129},{129,1},{2,130},{130,2},{3,131},{131,3},{4... | collective-permute-start | bytes 217352 | tf_op jit(solution)/shard_map/ppermute | solution.py:21
  18.7 17.1 %collective-permute-start.1 = (f32[12,16,512]{2,1,0:T(8,128)}, f32[12,16,512]{2,1,0:T(8,128)}, u32[]{:S(2)}, u32[]{:S(2)}) collective-permute-start(f32[12,16,512]{2,1,0:T(8,128)} %multiply_add_fusion.1), channel_id=1, source_target_pairs={{0,128},{128,0},{1,129},{129,1},{2,130},{130,2},{3,131},{131,3},{4... | collective-permute-start | bytes 1179656 | tf_op jit(solution)/shard_map/ppermute | solution.py:21
  19.9 22.2 %collective-permute-start.5 = (f32[251,512]{1,0:T(8,128)S(1)}, f32[251,512]{1,0:T(8,128)}, u32[]{:S(2)}, u32[]{:S(2)}) collective-permute-start(f32[251,512]{1,0:T(8,128)S(1)} %bitcast_subtract_fusion), channel_id=1, source_target_pairs={{0,128},{128,0},{1,129},{129,1},{2,130},{130,2},{3,131},{131,3},{4... | collective-permute-start | bytes 1542152 | tf_op jit(solution)/shard_map/ppermute | solution.py:21
  28.5 2.9 %collective-permute-start.4 = (f32[251,64]{0,1:T(8,128)S(1)}, f32[251,64]{0,1:T(8,128)S(1)}, u32[]{:S(2)}, u32[]{:S(2)}) collective-permute-start(f32[251,64]{0,1:T(8,128)S(1)} %slice_add_fusion), channel_id=1, source_target_pairs={{0,1},{1,0},{2,3},{3,2},{4,5},{5,4},{6,7},{7,6},{8,9},{9,8},{10,11... | collective-permute-start | bytes 192776 | tf_op jit(solution)/shard_map/ppermute | solution.py:21
  33.0 2.8 %copy-start.5 = (f32[12,16,512]{2,1,0:T(8,128)S(1)}, f32[12,16,512]{2,1,0:T(8,128)}, u32[]{:S(2)}) copy-start(f32[12,16,512]{2,1,0:T(8,128)} %get-tuple-element.20) | copy-start | bytes 1179652

commit v3 on v2

--- a/solution.py
+++ b/solution.py
@@ -42,14 +42,22 @@
     return lax.optimization_barrier((own_inner, partial))
 
 
-def outer_finish(global_part, momentum_part, own_inner, given_inner, partial, got_inner, got_partial, first_is_own):
+def outer_own(global_part, momentum_part, own_inner, partial, got_inner):
     new_global = partial + SHARE * got_inner
     grad = global_part - (own_inner + got_inner) / GROUPS
     new_momentum = MOMENTUM * momentum_part + grad
-    weights = place_pair(first_is_own, partial, got_partial) + SHARE * place_pair(
-        first_is_own, got_inner, given_inner
-    )
-    return new_global, new_momentum, weights
+    return new_global, new_momentum
+
+
+def place_own(own, rep_index):
+    rows = own.shape[0]
+    empty = jnp.zeros((2 * rows,) + own.shape[1:], own.dtype)
+    return lax.dynamic_update_slice_in_dim(empty, own, rep_index * rows, 0)
+
+
+def place_other(placed, other, rep_index):
+    rows = other.shape[0]
+    return lax.dynamic_update_slice_in_dim(placed, other, (1 - rep_index) * rows, 0)
 
 
 def step_body(
@@ -71,16 +79,23 @@
     given_attn = outer_sends(attn_global, attn_inner[0], rep_index)
     got_attn_inner = swap(given_attn, "rep")
     given_norm = outer_sends(norm_global, norm_inner[0], rep_index)
-    attn_parts = (given_attn,) + outer_partial(attn_global, attn_momentum, attn_inner[0], rep_index)
+    attn_parts = (given_attn,) + outer_partial(
+        attn_global, attn_momentum, lax.optimization_barrier(attn_inner[0]), rep_index
+    )
     norm_parts = (given_norm,) + outer_partial(norm_global, norm_momentum, norm_inner[0], rep_index)
     attn_parts = (attn_parts[1], attn_parts[0], attn_parts[2])
     norm_parts = (norm_parts[1], norm_parts[0], norm_parts[2])
     sent = lax.optimization_barrier(attn_parts[2])
     norm_sent = jnp.concatenate([given_norm, norm_parts[2]], axis=0)
     got_attn_partial = swap(sent, "rep")
-    new_attn_global, new_attn_momentum, attn_weights = outer_finish(
-        attn_global, attn_momentum, *attn_parts, got_attn_inner, got_attn_partial, first_is_own
-    )
+    new_attn_global, new_attn_momentum = outer_own(
+        attn_global, attn_momentum, attn_parts[0], attn_parts[2], got_attn_inner
+    )
+    attn_placed = place_own(new_attn_global, rep_index)
+    new_attn_global, new_attn_momentum, attn_placed = lax.optimization_barrier(
+        (new_attn_global, new_attn_momentum, attn_placed)
+    )
+    attn_weights = place_other(attn_placed, got_attn_partial + SHARE * given_attn, rep_index)
 
     block_rows = emb_inner.shape[1]
     half_rows = emb_global.shape[2]
@@ -132,8 +147,11 @@
     coeff_half = coeff_mine + coeff_got[:chip_rows]
     norm_rows = given_norm.shape[0]
     norm_got = coeff_got[chip_rows:].reshape(-1, width)
-    new_norm_global, new_norm_momentum, norm_weights = outer_finish(
-        norm_global, norm_momentum, *norm_parts, norm_got[:norm_rows], norm_got[norm_rows:], first_is_own
+    new_norm_global, new_norm_momentum = outer_own(
+        norm_global, norm_momentum, norm_parts[0], norm_parts[2], norm_got[:norm_rows]
+    )
+    norm_weights = place_other(
+        place_own(new_norm_global, rep_index), norm_got[norm_rows:] + SHARE * given_norm, rep_index
     )
     coeff_sum = place_pair(tp_index == 0, coeff_half, swap(coeff_half, "tp"))
     got_rows = swap(kept_rows, "rep")
@@ -152,10 +170,11 @@
     new_emb_momentum = MOMENTUM * emb_momentum + own_grad
     own_flat = kept_rows - STEP * lax.dynamic_slice_in_dim(emb_grad, half_start, half_rows, 0)
     other_grad = lax.dynamic_slice_in_dim(emb_grad, (1 - rep_index) * half_rows, half_rows, 0)
-    new_emb_global, new_emb_momentum, own_flat, other_grad = lax.optimization_barrier(
-        (new_emb_global, new_emb_momentum, own_flat, other_grad)
-    )
-    emb_weights = place_pair(first_is_own, own_flat, got_rows - STEP * other_grad)
+    emb_placed = place_own(own_flat, rep_index)
+    new_emb_global, new_emb_momentum, emb_placed, other_grad = lax.optimization_barrier(
+        (new_emb_global, new_emb_momentum, emb_placed, other_grad)
+    )
+    emb_weights = place_other(emb_placed, got_rows - STEP * other_grad, rep_index)
     return (
         new_attn_global,
         new_attn_momentum,

time: 44.9 us -> 46.4 us (1.033)
  waiting for transfers between devices: 2.8 us -> 6.63 us
  other arithmetic: 17.1 us -> 14.4 us
    select_n x4 -> x1, other arithmetic: 4.97 us -> 0.01 us  [place_pair(): first = jnp.where(first_is_own, own, other)]
    dynamic_update_slice x0 -> x2, local copies, waits for them, and re-layouts: none -> 4.84 us  [the longest x1 2.97 us: place_own(): return lax.dynamic_update_slice_in_dim(empty, own, rep_index * rows, 0)]
    dynamic_update_slice x0 -> x4, other arithmetic: none -> 3.9 us  [the longest x2 2.83 us: place_own(): return lax.dynamic_update_slice_in_dim(empty, own, rep_index * rows, 0)]
    ppermute x6, waiting for transfers between devices: 2.8 us -> 6.63 us  [swap(): return lax.ppermute(x, axis, perm=SWAP)]
    slice x3, local copies, waits for them, and re-layouts: 3.05 us -> 0.23 us  [step_body(): norm_got[norm_rows:] + SHARE * given_norm]
    slice x2, local copies, waits for them, and re-layouts: 2.79 us -> 0.14 us  [step_body(): norm_got[:norm_rows]]
    convert_element_type x2, other arithmetic: 2.54 us -> 0.65 us  [outer_sends(): given_inner = lax.dynamic_slice_in_dim(inner_all, (1 - rep_index) * owned...]
    add x2 -> x0, other arithmetic: 1.65 us -> none  [outer_finish(): place_pair(first_is_own, partial, got_partial)]
  transfers between devices with their start and end apart: 6 -> 6, of which waited for: 1 -> 2; matrix products, arithmetic and copies ran while one was open for 58% -> 43% of each run, Pallas kernels for 0% -> 0%
where the time goes in v3:
time: 46.4 us; the launch traced here: 45.9 us
  other arithmetic  14.4 us (31%)
  starting transfers between devices  10.7 us (23%)
  local copies, waits for them, and re-layouts  9.55 us (21%)
  waiting for transfers between devices  6.63 us (14%)
  matrix products  3.63 us (8%)
  between operations  0.95 us (2%)
    ppermute x6, starting transfers between devices, swap(): return lax.ppermute(x, axis, perm=SWAP)  10.7 us
    ppermute x6, waiting for transfers between devices, swap(): return lax.ppermute(x, axis, perm=SWAP)  6.63 us
    dynamic_update_slice x1, local copies, waits for them, and re-layouts, place_own(): return lax.dynamic_update_slice_in_dim(empty, own, rep_index * rows, 0)  2.97 us
    dynamic_update_slice x2, other arithmetic, place_own(): return lax.dynamic_update_slice_in_dim(empty, own, rep_index * rows, 0)  2.83 us
    dynamic_update_slice x1, local copies, waits for them, and re-layouts, place_other(): lax.dynamic_update_slice_in_dim(placed, other, (1 - rep_index) * rows, 0)  1.88 us
    add x2, other arithmetic, outer_partial(): partial = KEEP * global_part - DECAY * momentum_part + SHARE * own_inner  1.85 us
    add x1, other arithmetic, step_body(): new_emb_momentum = MOMENTUM * emb_momentum + own_grad  1.49 us
    reshape x2, local copies, waits for them, and re-layouts, step_body(): norm_sent.reshape(-1, coeff_width)  1.48 us
  transfers between devices with their start and end apart: 6, of which 2 were waited for; matrix products, arithmetic and copies ran while one was open for 43% of the time, Pallas kernels for 0%

profile of v3, /device:TPU:1, one launch (start us, length us, event | category | flops | bytes accessed | tf_op | source)
XLA Modules:
  0.0 45.9 jit_solution(771466951550603866)
XLA Ops:
  0.7 1.2 %and_select_fusion.1 = (s32[2,8192]{1,0:T(2,128)S(1)}, s32[2,8192]{1,0:T(2,128)S(1)}) fusion(s32[2,8192]{1,0:T(2,128)} %param.21, s32[]{:T(128)S(6)} %mul.159), kind=kLoop, calls=%fused_computation.33 | loop fusion | flops 327680 | bytes 196612 | tf_op jit(solution)/shard_map/jit(floor_divide)/jit(_where)/select_n | solution.py:109
  1.9 0.9 %compare_and_fusion = pred[2,8192]{1,0:T(4,128)(4,1)S(1)} fusion(s32[2,8192]{1,0:T(2,128)} %param.21, s32[]{:T(128)S(6)} %mul.159), kind=kLoop, calls=%fused_computation.32 | loop fusion | flops 65536 | bytes 81924 | tf_op jit(solution)/shard_map/and | solution.py:106
  4.3 1.3 %fusion.2 = f32[502,64]{0,1:T(8,128)} fusion(bf16[1,502,512]{2,1,0:T(8,128)(2,1)S(1)} %copy-done, f32[251,64]{0,1:T(8,128)S(1)} %get-tuple-element.66, f32[251,64]{0,1:T(8,128)S(1)} %get-tuple-element.65, f32[1024,64]{0,1:T(8,128)S(1)} %copy-done.12, s32[]{:T(128)S(6)} %select_n.85, f32[502]{0:T(512)S(1)} %bitcast.40), kind=kOutput, calls=%fused_computation.5 | convolution fusion | flops 197490816 | bytes 908804 | tf_op jit(solution)/shard_map/dot_general | solution.py:128
  5.5 3.2 %collective-permute-start.2 = (f32[502,64]{0,1:T(8,128)}, f32[502,64]{0,1:T(8,128)}, u32[]{:S(2)}, u32[]{:S(2)}) collective-permute-start(f32[502,64]{0,1:T(8,128)} %fusion.2), channel_id=1, source_target_pairs={{0,1},{1,0},{2,3},{3,2},{4,5},{5,4},{6,7},{7,6},{8,9},{9,8},{10,11... | collective-permute-start | bytes 385544 | tf_op jit(solution)/shard_map/ppermute | solution.py:21
  8.8 1.3 %collective-permute-start = (f32[12,16,512]{2,1,0:T(8,128)S(1)}, f32[12,16,512]{2,1,0:T(8,128)}, u32[]{:S(2)}, u32[]{:S(2)}) collective-permute-start(f32[12,16,512]{2,1,0:T(8,128)S(1)} %bitcast_convert_fusion), channel_id=1, source_target_pairs={{0,128},{128,0},{1,129},{129,1},{2,130},{130,2},{3,131},{131,3},{4... | collective-permute-start | bytes 1179656 | tf_op jit(solution)/shard_map/ppermute | solution.py:21
  11.6 0.8 %copy.24 = f32[32,64]{0,1:T(8,128)S(1)} copy(f32[32,64]{1,0:T(8,128)} %reshape.74) | data formatting | bytes 16384 | tf_op jit(solution)/shard_map/reshape | solution.py:145
  12.4 1.8 %multiply_add_fusion.1 = f32[12,16,512]{2,1,0:T(8,128)} fusion(f32[12,16,512]{2,1,0:T(8,128)S(1)} %copy-done.4, f32[12,16,512]{2,1,0:T(8,128)S(1)} %copy-done.6, bf16[24,16,512]{2,1,0:T(8,128)(2,1)} %bitcast.38, s32[]{:T(128)S(6)} %select_n.78), kind=kLoop, calls=%fused_computation.25 | loop fusion | flops 589824 | bytes 1376260 | tf_op jit(solution)/shard_map/add | solution.py:41
  14.2 1.0 %add.97 = f32[502,64]{0,1:T(8,128)S(1)} add(f32[502,64]{0,1:T(8,128)} %fusion.2, f32[502,64]{0,1:T(8,128)} %collective-permute-done.2) | non-fusion elementwise | flops 32128 | bytes 385536 | tf_op jit(solution)/shard_map/add | solution.py:138
  15.4 1.9 %collective-permute-start.3 = (f32[283,64]{0,1:T(8,128)S(1)}, f32[283,64]{0,1:T(8,128)S(1)}, u32[]{:S(2)}, u32[]{:S(2)}) collective-permute-start(f32[283,64]{0,1:T(8,128)S(1)} %pad_maximum_fusion), channel_id=1, source_target_pairs={{0,128},{128,0},{1,129},{129,1},{2,130},{130,2},{3,131},{131,3},{4... | collective-permute-start | bytes 217352 | tf_op jit(solution)/shard_map/ppermute | solution.py:21
  18.1 1.2 %collective-permute-start.1 = (f32[12,16,512]{2,1,0:T(8,128)}, f32[12,16,512]{2,1,0:T(8,128)}, u32[]{:S(2)}, u32[]{:S(2)}) collective-permute-start(f32[12,16,512]{2,1,0:T(8,128)} %multiply_add_fusion.1), channel_id=1, source_target_pairs={{0,128},{128,0},{1,129},{129,1},{2,130},{130,2},{3,131},{131,3},{4... | collective-permute-start | bytes 1179656 | tf_op jit(solution)/shard_map/ppermute | solution.py:21
  19.3 1.8 %collective-permute-start.5 = (f32[251,512]{1,0:T(8,128)S(1)}, f32[251,512]{1,0:T(8,128)}, u32[]{:S(2)}, u32[]{:S(2)}) collective-permute-start(f32[251,512]{1,0:T(8,128)S(1)} %bitcast_subtract_fusion), channel_id=1, source_target_pairs={{0,128},{128,0},{1,129},{129,1},{2,130},{130,2},{3,131},{131,3},{4... | collective-permute-start | bytes 1542152 | tf_op jit(solution)/shard_map/ppermute | solution.py:21
  21.1 2.1 %collective-permute-done.3 = f32[283,64]{0,1:T(8,128)S(1)} collective-permute-done((f32[283,64]{0,1:T(8,128)S(1)}, f32[283,64]{0,1:T(8,128)S(1)}, u32[]{:S(2)}, u32[]{:S(2)}) %collective-permute-start.3) | collective-permute-done | bytes 72480 | tf_op jit(solution)/shard_map/ppermute | solution.py:21
  23.3 1.4 %collective-permute-start.4 = (f32[251,64]{0,1:T(8,128)S(1)}, f32[251,64]{0,1:T(8,128)S(1)}, u32[]{:S(2)}, u32[]{:S(2)}) collective-permute-start(f32[251,64]{0,1:T(8,128)S(1)} %slice_add_fusion), channel_id=1, source_target_pairs={{0,1},{1,0},{2,3},{3,2},{4,5},{5,4},{6,7},{7,6},{8,9},{9,8},{10,11... | collective-permute-start | bytes 192776 | tf_op jit(solution)/shard_map/ppermute | solution.py:21
  25.8 1.1 %convolution_multiply_fusion = f32[502,512]{1,0:T(8,128)S(1)} fusion(f32[251,64]{0,1:T(8,128)S(1)} %get-tuple-element.62, f32[251,64]{0,1:T(8,128)S(1)} %get-tuple-element.61, f32[1024,64]{0,1:T(8,128)S(1)} %copy-done.12, s32[]{:T(128)S(6)} %select_n.85), kind=kOutput, calls=%fused_computation.2 | convolution fusion | flops 197683584 | bytes 1290244 | tf_op jit(solution)/shard_map/dot_general | solution.py:159
  27.2 1.0 %bitcast_subtract_fusion.1 = f32[1,1,251,512]{3,2,1,0:T(8,128)} fusion(f32[251,512]{1,0:T(8,128)S(1)} %get-tuple-element.54, f32[1,1,251,512]{3,1,2,0:T(1,128)S(1)} %copy-done.1, f32[1,1,251,512]{3,1,2,0:T(1,128)S(1)} %copy-done.2), kind=kLoop, calls=%fused_computation.13 | loop fusion | flops 514048 | bytes 2056192 | tf_op jit(solution)/shard_map/sub | solution.py:169
  28.1 1.5 %reshape_add_fusion = f32[1,1,251,512]{3,1,2,0:T(1,128)} fusion(f32[251,512]{1,0:T(8,128)S(1)} %get-tuple-element.54, f32[1,1,251,512]{3,1,2,0:T(1,128)S(1)} %copy-done.2), kind=kLoop, calls=%fused_computation.19 | loop fusion | flops 257024 | bytes 1542144 | tf_op jit(solution)/shard_map/add | solution.py:170
  29.6 1.1 %broadcast_in_dim.22 = f32[502,512]{1,0:T(8,128)} broadcast(f32[]{:T(128)} %constant.40.clone.1), dimensions={} | broadcast | bytes 1028100 | tf_op jit(solution)/shard_map/broadcast_in_dim | solution.py:54
  30.7 3.0 %dynamic_update_slice.22 = f32[502,512]{1,0:T(8,128)} dynamic-update-slice(f32[502,512]{1,0:T(8,128)} %broadcast_in_dim.22, f32[251,512]{1,0:T(8,128)S(1)} %get-tuple-element.53, s32[]{:T(128)S(6)} %select_n.84, s32[]{:T(128)} %constant.32.clone.1) | dynamic-update-slice | bytes 1028100 | tf_op jit(solution)/shard_map/dynamic_update_slice | solution.py:55
  33.7 1.3 %copy.28 = f32[1,1,251,512]{3,1,2,0:T(1,128)} copy(f32[1,1,251,512]{3,2,1,0:T(8,128)S(1)} %copy-done.3) | data formatting | bytes 1028096
  35.1 2.2 %constant_dynamic-update-slice_fusion.1 = (f32[24,16,512]{2,1,0:T(8,128)S(1)}, f32[12,16,512]{2,1,0:T(8,128)}, f32[12,16,512]{2,1,0:T(8,128)}) fusion(f32[24,16,512]{2,1,0:T(8,128)S(1)} %broadcast_in_dim.8, s32[]{:T(128)S(6)} %select_n.78, f32[12,16,512]{2,1,0:T(8,128)} %multiply_add_fusion.1, f32[12,16,512]{2,1,0:T(8,128)} %collective-permute-done, ...), kind=kLoop, calls=%fused_computation.64 | loop fusion | flops 688128 | bytes 3145732 | tf_op jit(solution)/shard_map/dynamic_update_slice | solution.py:55
  37.3 1.1 %add_dynamic-update-slice_fusion = f32[24,16,512]{2,1,0:T(8,128)S(1)} fusion(f32[24,16,512]{2,1,0:T(8,128)S(1)} %get-tuple-element.26, s32[]{:T(128)S(6)} %select_n.79, f32[12,16,512]{2,1,0:T(8,128)} %collective-permute-done.1, f32[12,16,512]{2,1,0:T(8,128)S(1)} %bitcast_convert_fusion), kind=kLoop, calls=%fused_computation.22 | loop fusion | flops 196608 | bytes 1179652 | tf_op jit(solution)/shard_map/dynamic_update_slice | solution.py:60
  38.4 4.5 %collective-permute-done.5 = f32[251,512]{1,0:T(8,128)} collective-permute-done((f32[251,512]{1,0:T(8,128)S(1)}, f32[251,512]{1,0:T(8,128)}, u32[]{:S(2)}, u32[]{:S(2)}) %collective-permute-start.5) | collective-permute-done | bytes 514080 | tf_op jit(solution)/shard_map/ppermute | solution.py:21
  42.9 1.1 %multiply_subtract_fusion = f32[251,512]{1,0:T(8,128)S(1)} fusion(f32[251,512]{1,0:T(8,128)} %collective-permute-done.5, f32[251,512]{1,0:T(8,128)S(1)} %get-tuple-element.34), kind=kLoop, calls=%fused_computation.15 | loop fusion | flops 257024 | bytes 1542144 | tf_op jit(solution)/shard_map/sub | solution.py:177
  44.1 1.9 %dynamic_update_slice.23 = f32[502,512]{1,0:T(8,128)} dynamic-update-slice(f32[502,512]{1,0:T(8,128)} %dynamic_update_slice.22, f32[251,512]{1,0:T(8,128)S(1)} %multiply_subtract_fusion, s32[]{:T(128)S(6)} %select_n.96, s32[]{:T(128)} %constant.32.clone.1) | dynamic-update-slice | bytes 1028100 | tf_op jit(solution)/shard_map/dynamic_update_slice | solution.py:60
  (72 shorter events, 5.4 us)
Async XLA Ops:
  0.6 3.6 %copy-start = (bf16[1,502,512]{2,1,0:T(8,128)(2,1)S(1)}, bf16[1,502,512]{2,1,0:T(8,128)(2,1)}, u32[]{:S(2)}) copy-start(bf16[1,502,512]{2,1,0:T(8,128)(2,1)} %param.19) | copy-start | bytes 1542148
  0.7 3.0 %copy-start.1 = (f32[1,1,251,512]{3,1,2,0:T(1,128)S(1)}, f32[1,1,251,512]{3,1,2,0:T(1,128)}, u32[]{:S(2)}) copy-start(f32[1,1,251,512]{3,1,2,0:T(1,128)} %param.17) | copy-start | bytes 1542148
  0.7 3.0 %copy-start.12 = (f32[1024,64]{0,1:T(8,128)S(1)}, f32[1024,64]{0,1:T(8,128)}, u32[]{:S(2)}) copy-start(f32[1024,64]{0,1:T(8,128)} %param.20) | copy-start | bytes 786436
  3.4 5.3 %copy-start.9 = (bf16[1,24,16,512]{3,2,1,0:T(8,128)(2,1)S(1)}, bf16[1,24,16,512]{3,2,1,0:T(8,128)(2,1)}, u32[]{:S(2)}) copy-start(bf16[1,24,16,512]{3,2,1,0:T(8,128)(2,1)} %param.13) | copy-start | bytes 1179652
  3.6 6.5 %copy-start.2 = (f32[1,1,251,512]{3,1,2,0:T(1,128)S(1)}, f32[1,1,251,512]{3,1,2,0:T(1,128)}, u32[]{:S(2)}) copy-start(f32[1,1,251,512]{3,1,2,0:T(1,128)} %param.18) | copy-start | bytes 1542148
  5.5 8.7 %collective-permute-start.2 = (f32[502,64]{0,1:T(8,128)}, f32[502,64]{0,1:T(8,128)}, u32[]{:S(2)}, u32[]{:S(2)}) collective-permute-start(f32[502,64]{0,1:T(8,128)} %fusion.2), channel_id=1, source_target_pairs={{0,1},{1,0},{2,3},{3,2},{4,5},{5,4},{6,7},{7,6},{8,9},{9,8},{10,11... | collective-permute-start | bytes 385544 | tf_op jit(solution)/shard_map/ppermute | solution.py:21
  8.7 1.5 %copy-start.18 = (bf16[1,4,512]{2,1,0:T(4,128)(2,1)S(1)}, bf16[1,4,512]{2,1,0:T(4,128)(2,1)}, u32[]{:S(2)}) copy-start(bf16[1,4,512]{2,1,0:T(4,128)(2,1)} %param.16) | copy-start | bytes 12292
  8.7 2.1 %copy-start.14 = (f32[2,512]{1,0:T(2,128)S(1)}, f32[2,512]{1,0:T(2,128)}, u32[]{:S(2)}) copy-start(f32[2,512]{1,0:T(2,128)} %param.15) | copy-start | bytes 12292
  8.7 2.1 %copy-start.16 = (f32[2,512]{1,0:T(2,128)S(1)}, f32[2,512]{1,0:T(2,128)}, u32[]{:S(2)}) copy-start(f32[2,512]{1,0:T(2,128)} %param.14) | copy-start | bytes 12292
  8.7 3.6 %copy-start.4 = (f32[12,16,512]{2,1,0:T(8,128)S(1)}, f32[12,16,512]{2,1,0:T(8,128)}, u32[]{:S(2)}) copy-start(f32[12,16,512]{2,1,0:T(8,128)} %param.12) | copy-start | bytes 1179652
  8.7 3.6 %copy-start.6 = (f32[12,16,512]{2,1,0:T(8,128)S(1)}, f32[12,16,512]{2,1,0:T(8,128)}, u32[]{:S(2)}) copy-start(f32[12,16,512]{2,1,0:T(8,128)} %param.11) | copy-start | bytes 1179652
  8.8 26.2 %collective-permute-start = (f32[12,16,512]{2,1,0:T(8,128)S(1)}, f32[12,16,512]{2,1,0:T(8,128)}, u32[]{:S(2)}, u32[]{:S(2)}) collective-permute-start(f32[12,16,512]{2,1,0:T(8,128)S(1)} %bitcast_convert_fusion), channel_id=1, source_target_pairs={{0,128},{128,0},{1,129},{129,1},{2,130},{130,2},{3,131},{131,3},{4... | collective-permute-start | bytes 1179656 | tf_op jit(solution)/shard_map/ppermute | solution.py:21
  12.4 4.9 %copy-start.10 = (bf16[1,24,16,512]{3,2,1,0:T(8,128)(2,1)S(1)}, bf16[1,24,16,512]{3,2,1,0:T(8,128)(2,1)}, u32[]{:S(2)}) copy-start(bf16[1,24,16,512]{3,2,1,0:T(8,128)(2,1)} %param.13) | copy-start | bytes 1179652
  14.2 10.8 %copy-start.13 = (f32[2,512]{1,0:T(2,128)S(1)}, f32[2,512]{1,0:T(2,128)}, u32[]{:S(2)}) copy-start(f32[2,512]{1,0:T(2,128)} %get-tuple-element.29) | copy-start | bytes 12292
  14.2 10.9 %copy-start.15 = (f32[2,512]{1,0:T(2,128)S(1)}, f32[2,512]{1,0:T(2,128)}, u32[]{:S(2)}) copy-start(f32[2,512]{1,0:T(2,128)} %param.15) | copy-start | bytes 12292
  14.2 10.9 %copy-start.17 = (f32[2,512]{1,0:T(2,128)S(1)}, f32[2,512]{1,0:T(2,128)}, u32[]{:S(2)}) copy-start(f32[2,512]{1,0:T(2,128)} %param.14) | copy-start | bytes 12292
  15.4 7.7 %collective-permute-start.3 = (f32[283,64]{0,1:T(8,128)S(1)}, f32[283,64]{0,1:T(8,128)S(1)}, u32[]{:S(2)}, u32[]{:S(2)}) collective-permute-start(f32[283,64]{0,1:T(8,128)S(1)} %pad_maximum_fusion), channel_id=1, source_target_pairs={{0,128},{128,0},{1,129},{129,1},{2,130},{130,2},{3,131},{131,3},{4... | collective-permute-start | bytes 217352 | tf_op jit(solution)/shard_map/ppermute | solution.py:21
  18.1 19.3 %collective-permute-start.1 = (f32[12,16,512]{2,1,0:T(8,128)}, f32[12,16,512]{2,1,0:T(8,128)}, u32[]{:S(2)}, u32[]{:S(2)}) collective-permute-start(f32[12,16,512]{2,1,0:T(8,128)} %multiply_add_fusion.1), channel_id=1, source_target_pairs={{0,128},{128,0},{1,129},{129,1},{2,130},{130,2},{3,131},{131,3},{4... | collective-permute-start | bytes 1179656 | tf_op jit(solution)/shard_map/ppermute | solution.py:21
  19.3 23.6 %collective-permute-start.5 = (f32[251,512]{1,0:T(8,128)S(1)}, f32[251,512]{1,0:T(8,128)}, u32[]{:S(2)}, u32[]{:S(2)}) collective-permute-start(f32[251,512]{1,0:T(8,128)S(1)} %bitcast_subtract_fusion), channel_id=1, source_target_pairs={{0,128},{128,0},{1,129},{129,1},{2,130},{130,2},{3,131},{131,3},{4... | collective-permute-start | bytes 1542152 | tf_op jit(solution)/shard_map/ppermute | solution.py:21
  23.3 2.5 %collective-permute-start.4 = (f32[251,64]{0,1:T(8,128)S(1)}, f32[251,64]{0,1:T(8,128)S(1)}, u32[]{:S(2)}, u32[]{:S(2)}) collective-permute-start(f32[251,64]{0,1:T(8,128)S(1)} %slice_add_fusion), channel_id=1, source_target_pairs={{0,1},{1,0},{2,3},{3,2},{4,5},{5,4},{6,7},{7,6},{8,9},{9,8},{10,11... | collective-permute-start | bytes 192776 | tf_op jit(solution)/shard_map/ppermute | solution.py:21
  29.6 4.1 %copy-start.3 = (f32[1,1,251,512]{3,2,1,0:T(8,128)S(1)}, f32[1,1,251,512]{3,2,1,0:T(8,128)}, u32[]{:S(2)}) copy-start(f32[1,1,251,512]{3,2,1,0:T(8,128)} %bitcast_subtract_fusion.1) | copy-start | bytes 1542148
  33.7 1.4 %copy-start.7 = (f32[12,16,512]{2,1,0:T(8,128)S(1)}, f32[12,16,512]{2,1,0:T(8,128)}, u32[]{:S(2)}) copy-start(f32[12,16,512]{2,1,0:T(8,128)} %param.11) | copy-start | bytes 1179652
  33.7 1.4 %copy-start.8 = (f32[12,16,512]{2,1,0:T(8,128)S(1)}, f32[12,16,512]{2,1,0:T(8,128)}, u32[]{:S(2)}) copy-start(f32[12,16,512]{2,1,0:T(8,128)} %dynamic-slice_convert_fusion) | copy-start | bytes 1179652
  38.4 4.5 %copy-start.11 = (f32[24,16,512]{2,1,0:T(8,128)}, f32[24,16,512]{2,1,0:T(8,128)S(1)}, u32[]{:S(2)}) copy-start(f32[24,16,512]{2,1,0:T(8,128)S(1)} %add_dynamic-update-slice_fusion) | copy-start | bytes 2359300
  (2 other events, 2.8 us)

commit v4 on v3

--- a/solution.py
+++ b/solution.py
@@ -170,11 +170,10 @@
     new_emb_momentum = MOMENTUM * emb_momentum + own_grad
     own_flat = kept_rows - STEP * lax.dynamic_slice_in_dim(emb_grad, half_start, half_rows, 0)
     other_grad = lax.dynamic_slice_in_dim(emb_grad, (1 - rep_index) * half_rows, half_rows, 0)
-    emb_placed = place_own(own_flat, rep_index)
-    new_emb_global, new_emb_momentum, emb_placed, other_grad = lax.optimization_barrier(
-        (new_emb_global, new_emb_momentum, emb_placed, other_grad)
-    )
-    emb_weights = place_other(emb_placed, got_rows - STEP * other_grad, rep_index)
+    new_emb_global, new_emb_momentum, own_flat, other_grad = lax.optimization_barrier(
+        (new_emb_global, new_emb_momentum, own_flat, other_grad)
+    )
+    emb_weights = place_pair(first_is_own, own_flat, got_rows - STEP * other_grad)
     return (
         new_attn_global,
         new_attn_momentum,

time: 46.4 us -> 44.6 us (0.961)
  other arithmetic: 14.4 us -> 18 us
  waiting for transfers between devices: 6.63 us -> 3.14 us
  local copies, waits for them, and re-layouts: 9.55 us -> 7.73 us
    dynamic_update_slice x2 -> x0, local copies, waits for them, and re-layouts: 4.84 us -> none  [the longest x1 2.97 us: place_own(): return lax.dynamic_update_slice_in_dim(empty, own, rep_index * rows, 0)]
    ppermute x6, waiting for transfers between devices: 6.63 us -> 3.14 us  [swap(): return lax.ppermute(x, axis, perm=SWAP)]
    slice x3, local copies, waits for them, and re-layouts: 0.23 us -> 3.05 us  [step_body(): norm_got[norm_rows:] + SHARE * given_norm]
    slice x2, local copies, waits for them, and re-layouts: 0.14 us -> 2.79 us  [step_body(): norm_got[:norm_rows]]
    reshape x2, local copies, waits for them, and re-layouts: 1.48 us -> 0.16 us  [step_body(): norm_sent.reshape(-1, coeff_width)]
    select_n x1 -> x2, other arithmetic: 0.01 us -> 1.17 us  [place_pair(): first = jnp.where(first_is_own, own, other)]
    sub x1 -> x0, other arithmetic: 1.13 us -> none  [step_body(): got_rows - STEP * other_grad]
    broadcast_in_dim x3 -> x2, local copies, waits for them, and re-layouts: 1.17 us -> 0.08 us  [place_own(): empty = jnp.zeros((2 * rows,) + own.shape[1:], own.dtype)]
  transfers between devices with their start and end apart: 6 -> 6, of which waited for: 2 -> 2; matrix products, arithmetic and copies ran while one was open for 43% -> 59% of each run, Pallas kernels for 0% -> 0%
where the time goes in v4:
time: 44.6 us; the launch traced here: 44 us
  other arithmetic  18 us (40%)
  starting transfers between devices  10.6 us (24%)
  local copies, waits for them, and re-layouts  7.73 us (17%)
  matrix products  3.63 us (8%)
  waiting for transfers between devices  3.14 us (7%)
  between operations  0.92 us (2%)
    ppermute x6, starting transfers between devices, swap(): return lax.ppermute(x, axis, perm=SWAP)  10.6 us
    dynamic_update_slice x2, other arithmetic, place_own(): return lax.dynamic_update_slice_in_dim(empty, own, rep_index * rows, 0)  3.58 us
    ppermute x6, waiting for transfers between devices, swap(): return lax.ppermute(x, axis, perm=SWAP)  3.14 us
    slice x3, local copies, waits for them, and re-layouts, step_body(): norm_got[norm_rows:] + SHARE * given_norm  3.05 us
    slice x2, local copies, waits for them, and re-layouts, step_body(): norm_got[:norm_rows]  2.79 us
    add x2, other arithmetic, outer_partial(): partial = KEEP * global_part - DECAY * momentum_part + SHARE * own_inner  1.86 us
    convert_element_type x2, other arithmetic, outer_sends(): given_inner = lax.dynamic_slice_in_dim(inner_all, (1 - rep_index) * owned...  1.66 us
    add x1, other arithmetic, step_body(): new_emb_momentum = MOMENTUM * emb_momentum + own_grad  1.49 us
  transfers between devices with their start and end apart: 6, of which 2 were waited for; matrix products, arithmetic and copies ran while one was open for 59% of the time, Pallas kernels for 0%

profile of v4, /device:TPU:1, one launch (start us, length us, event | category | flops | bytes accessed | tf_op | source)
XLA Modules:
  0.0 44.0 jit_solution(13104418845026216564)
XLA Ops:
  0.7 1.1 %bitcast_convert_fusion = f32[12,16,512]{2,1,0:T(8,128)S(1)} fusion(bf16[1,24,16,512]{3,2,1,0:T(8,128)(2,1)} %param.13, s32[]{:T(128)S(6)} %select_n.89), kind=kLoop, calls=%fused_computation.29 | loop fusion | flops 98304 | bytes 589828 | tf_op jit(solution)/shard_map/convert_element_type | solution.py:34
  1.8 3.8 %collective-permute-start = (f32[12,16,512]{2,1,0:T(8,128)S(1)}, f32[12,16,512]{2,1,0:T(8,128)}, u32[]{:S(2)}, u32[]{:S(2)}) collective-permute-start(f32[12,16,512]{2,1,0:T(8,128)S(1)} %bitcast_convert_fusion), channel_id=1, source_target_pairs={{0,128},{128,0},{1,129},{129,1},{2,130},{130,2},{3,131},{131,3},{4... | collective-permute-start | bytes 1179656 | tf_op jit(solution)/shard_map/ppermute | solution.py:21
  5.6 1.1 %and_select_fusion.1 = (s32[2,8192]{1,0:T(2,128)S(1)}, s32[2,8192]{1,0:T(2,128)S(1)}) fusion(s32[2,8192]{1,0:T(2,128)} %param.21, s32[]{:T(128)S(6)} %mul.157), kind=kLoop, calls=%fused_computation.36 | loop fusion | flops 327680 | bytes 196612 | tf_op jit(solution)/shard_map/jit(floor_divide)/jit(_where)/select_n | solution.py:109
  9.1 1.3 %fusion.2 = f32[502,64]{0,1:T(8,128)} fusion(bf16[1,502,512]{2,1,0:T(8,128)(2,1)S(1)} %copy-done, f32[251,64]{0,1:T(8,128)S(1)} %get-tuple-element.68, f32[251,64]{0,1:T(8,128)S(1)} %get-tuple-element.67, f32[1024,64]{0,1:T(8,128)S(1)} %copy-done.8, s32[]{:T(128)S(6)} %select_n.95, f32[502]{0:T(512)S(1)} %bitcast.40), kind=kOutput, calls=%fused_computation.5 | convolution fusion | flops 197490816 | bytes 908804 | tf_op jit(solution)/shard_map/dot_general | solution.py:128
  10.3 1.0 %collective-permute-start.2 = (f32[502,64]{0,1:T(8,128)}, f32[502,64]{0,1:T(8,128)}, u32[]{:S(2)}, u32[]{:S(2)}) collective-permute-start(f32[502,64]{0,1:T(8,128)} %fusion.2), channel_id=1, source_target_pairs={{0,1},{1,0},{2,3},{3,2},{4,5},{5,4},{6,7},{7,6},{8,9},{9,8},{10,11... | collective-permute-start | bytes 385544 | tf_op jit(solution)/shard_map/ppermute | solution.py:21
  12.2 1.9 %multiply_add_fusion.1 = f32[12,16,512]{2,1,0:T(8,128)} fusion(f32[12,16,512]{2,1,0:T(8,128)S(1)} %copy-done.3, f32[12,16,512]{2,1,0:T(8,128)S(1)} %copy-done.4, bf16[24,16,512]{2,1,0:T(8,128)(2,1)} %bitcast.38, s32[]{:T(128)S(6)} %select_n.88), kind=kLoop, calls=%fused_computation.26 | loop fusion | flops 589824 | bytes 1376260 | tf_op jit(solution)/shard_map/add | solution.py:41
  14.1 1.0 %add.95 = f32[502,64]{0,1:T(8,128)S(1)} add(f32[502,64]{0,1:T(8,128)} %fusion.2, f32[502,64]{0,1:T(8,128)} %collective-permute-done.2) | non-fusion elementwise | flops 32128 | bytes 385536 | tf_op jit(solution)/shard_map/add | solution.py:138
  15.9 1.8 %collective-permute-start.3 = (f32[283,64]{0,1:T(8,128)}, f32[283,64]{0,1:T(8,128)}, u32[]{:S(2)}, u32[]{:S(2)}) collective-permute-start(f32[283,64]{0,1:T(8,128)} %pad_maximum_fusion.1), channel_id=1, source_target_pairs={{0,128},{128,0},{1,129},{129,1},{2,130},{130,2},{3,131},{131,3},{4... | collective-permute-start | bytes 217352 | tf_op jit(solution)/shard_map/ppermute | solution.py:21
  18.5 1.2 %collective-permute-start.1 = (f32[12,16,512]{2,1,0:T(8,128)}, f32[12,16,512]{2,1,0:T(8,128)}, u32[]{:S(2)}, u32[]{:S(2)}) collective-permute-start(f32[12,16,512]{2,1,0:T(8,128)} %multiply_add_fusion.1), channel_id=1, source_target_pairs={{0,128},{128,0},{1,129},{129,1},{2,130},{130,2},{3,131},{131,3},{4... | collective-permute-start | bytes 1179656 | tf_op jit(solution)/shard_map/ppermute | solution.py:21
  19.7 1.8 %collective-permute-start.5 = (f32[251,512]{1,0:T(8,128)S(1)}, f32[251,512]{1,0:T(8,128)}, u32[]{:S(2)}, u32[]{:S(2)}) collective-permute-start(f32[251,512]{1,0:T(8,128)S(1)} %bitcast_subtract_fusion), channel_id=1, source_target_pairs={{0,128},{128,0},{1,129},{129,1},{2,130},{130,2},{3,131},{131,3},{4... | collective-permute-start | bytes 1542152 | tf_op jit(solution)/shard_map/ppermute | solution.py:21
  21.9 1.6 %fusion.27 = (f32[16,64]{0,1:T(8,128)S(1)}, f32[16,64]{0,1:T(8,128)}) fusion(f32[283,64]{0,1:T(8,128)} %collective-permute-done.3), kind=kLoop, calls=%fused_computation.74 | loop fusion | bytes 16384 | tf_op jit(solution)/shard_map/slice | solution.py:154
  23.5 1.4 %copy.25 = f32[16,64]{1,0:T(8,128)} copy(f32[16,64]{0,1:T(8,128)} %get-tuple-element.66) | data formatting | bytes 8192 | tf_op jit(solution)/shard_map/slice | solution.py:151
  25.0 1.4 %slice.27 = f32[2,512]{1,0:T(2,128)} reshape(f32[16,64]{1,0:T(8,128)} %copy.25) | data formatting | bytes 8192 | tf_op jit(solution)/shard_map/slice | solution.py:151
  27.8 1.0 %slice_add_fusion = f32[251,64]{0,1:T(8,128)S(1)} fusion(f32[283,64]{0,1:T(8,128)} %collective-permute-done.3, f32[502,64]{0,1:T(8,128)} %copy-done.9, s32[]{:T(128)S(6)} %select_n.101), kind=kLoop, calls=%fused_computation.44 | loop fusion | flops 16064 | bytes 192772 | tf_op jit(solution)/shard_map/add | solution.py:147
  28.8 1.1 %collective-permute-start.4 = (f32[251,64]{0,1:T(8,128)S(1)}, f32[251,64]{0,1:T(8,128)S(1)}, u32[]{:S(2)}, u32[]{:S(2)}) collective-permute-start(f32[251,64]{0,1:T(8,128)S(1)} %slice_add_fusion), channel_id=1, source_target_pairs={{0,1},{1,0},{2,3},{3,2},{4,5},{5,4},{6,7},{7,6},{8,9},{9,8},{10,11... | collective-permute-start | bytes 192776 | tf_op jit(solution)/shard_map/ppermute | solution.py:21
  29.9 1.3 %constant_dynamic-update-slice_fusion = (f32[4,512]{1,0:T(4,128)S(1)}, f32[2,512]{1,0:T(2,128)}, f32[2,512]{1,0:T(2,128)}) fusion(f32[4,512]{1,0:T(4,128)S(1)} %broadcast_in_dim.8, s32[]{:T(128)S(6)} %select_n.90, f32[2,512]{1,0:T(2,128)S(1)} %multiply_add_fusion.3, f32[2,512]{1,0:T(2,128)} %slice.27, f32[2,512]{1,0:T(2,128)} %param.14, ...), kind=kLoop, calls=%fused_computation.61 | loop fusion | flops 7168 | bytes 32772 | tf_op jit(solution)/shard_map/dynamic_update_slice | solution.py:55
  31.3 1.1 %convolution_multiply_fusion = f32[502,512]{1,0:T(8,128)S(1)} fusion(f32[251,64]{0,1:T(8,128)S(1)} %get-tuple-element.64, f32[251,64]{0,1:T(8,128)S(1)} %get-tuple-element.63, f32[1024,64]{0,1:T(8,128)S(1)} %copy-done.8, s32[]{:T(128)S(6)} %select_n.95), kind=kOutput, calls=%fused_computation.2 | convolution fusion | flops 197683584 | bytes 1290244 | tf_op jit(solution)/shard_map/dot_general | solution.py:159
  32.9 1.5 %reshape_add_fusion = f32[1,1,251,512]{3,1,2,0:T(1,128)} fusion(f32[251,512]{1,0:T(8,128)S(1)} %get-tuple-element.54, f32[1,1,251,512]{3,1,2,0:T(1,128)S(1)} %copy-done.2), kind=kLoop, calls=%fused_computation.20 | loop fusion | flops 257024 | bytes 1542144 | tf_op jit(solution)/shard_map/add | solution.py:170
  34.4 1.3 %copy.28 = f32[1,1,251,512]{3,1,2,0:T(1,128)} copy(f32[1,1,251,512]{3,2,1,0:T(8,128)S(1)} %bitcast_subtract_fusion.1) | data formatting | bytes 1028096
  35.8 2.2 %constant_dynamic-update-slice_fusion.1 = (f32[24,16,512]{2,1,0:T(8,128)S(1)}, f32[12,16,512]{2,1,0:T(8,128)}, f32[12,16,512]{2,1,0:T(8,128)}) fusion(f32[24,16,512]{2,1,0:T(8,128)S(1)} %broadcast_in_dim.6, s32[]{:T(128)S(6)} %select_n.88, f32[12,16,512]{2,1,0:T(8,128)} %multiply_add_fusion.1, f32[12,16,512]{2,1,0:T(8,128)} %collective-permute-done, ...), kind=kLoop, calls=%fused_computation.67 | loop fusion | flops 688128 | bytes 3145732 | tf_op jit(solution)/shard_map/dynamic_update_slice | solution.py:55
  38.0 1.1 %add_dynamic-update-slice_fusion = f32[24,16,512]{2,1,0:T(8,128)S(1)} fusion(f32[24,16,512]{2,1,0:T(8,128)S(1)} %get-tuple-element.26, s32[]{:T(128)S(6)} %select_n.89, f32[12,16,512]{2,1,0:T(8,128)} %collective-permute-done.1, f32[12,16,512]{2,1,0:T(8,128)S(1)} %bitcast_convert_fusion), kind=kLoop, calls=%fused_computation.23 | loop fusion | flops 196608 | bytes 1179652 | tf_op jit(solution)/shard_map/dynamic_update_slice | solution.py:60
  39.1 2.6 %collective-permute-done.5 = f32[251,512]{1,0:T(8,128)} collective-permute-done((f32[251,512]{1,0:T(8,128)S(1)}, f32[251,512]{1,0:T(8,128)}, u32[]{:S(2)}, u32[]{:S(2)}) %collective-permute-start.5) | collective-permute-done | bytes 514080 | tf_op jit(solution)/shard_map/ppermute | solution.py:21
  41.8 1.2 %broadcast_select_fusion.1 = (f32[251,512]{1,0:T(8,128)S(1)}, f32[251,512]{1,0:T(8,128)S(1)}) fusion(f32[251,512]{1,0:T(8,128)S(1)} %get-tuple-element.33, pred[]{:T(512)S(6)} %eq.34, f32[251,512]{1,0:T(8,128)} %collective-permute-done.5, f32[251,512]{1,0:T(8,128)S(1)} %get-tuple-element.34), kind=kLoop, calls=%fused_computation.28 | loop fusion | flops 514048 | bytes 2570241 | tf_op jit(solution)/shard_map/jit(_where)/select_n | solution.py:25
  42.9 1.1 %pad_maximum_fusion = f32[502,512]{1,0:T(8,128)} fusion(f32[251,512]{1,0:T(8,128)S(1)} %get-tuple-element.60, f32[251,512]{1,0:T(8,128)S(1)} %get-tuple-element.59), kind=kLoop, calls=%fused_computation.11 | loop fusion | flops 257024 | bytes 2056192 | tf_op jit(solution)/shard_map/concatenate | solution.py:27
  (58 shorter events, 7.4 us)
Async XLA Ops:
  0.6 8.4 %copy-start = (bf16[1,502,512]{2,1,0:T(8,128)(2,1)S(1)}, bf16[1,502,512]{2,1,0:T(8,128)(2,1)}, u32[]{:S(2)}) copy-start(bf16[1,502,512]{2,1,0:T(8,128)(2,1)} %param.19) | copy-start | bytes 1542148
  0.7 7.8 %copy-start.1 = (f32[1,1,251,512]{3,1,2,0:T(1,128)S(1)}, f32[1,1,251,512]{3,1,2,0:T(1,128)}, u32[]{:S(2)}) copy-start(f32[1,1,251,512]{3,1,2,0:T(1,128)} %param.17) | copy-start | bytes 1542148
  0.7 7.8 %copy-start.8 = (f32[1024,64]{0,1:T(8,128)S(1)}, f32[1024,64]{0,1:T(8,128)}, u32[]{:S(2)}) copy-start(f32[1024,64]{0,1:T(8,128)} %param.20) | copy-start | bytes 786436
  1.8 33.9 %collective-permute-start = (f32[12,16,512]{2,1,0:T(8,128)S(1)}, f32[12,16,512]{2,1,0:T(8,128)}, u32[]{:S(2)}, u32[]{:S(2)}) collective-permute-start(f32[12,16,512]{2,1,0:T(8,128)S(1)} %bitcast_convert_fusion), channel_id=1, source_target_pairs={{0,128},{128,0},{1,129},{129,1},{2,130},{130,2},{3,131},{131,3},{4... | collective-permute-start | bytes 1179656 | tf_op jit(solution)/shard_map/ppermute | solution.py:21
  8.2 3.1 %copy-start.12 = (bf16[1,4,512]{2,1,0:T(4,128)(2,1)S(1)}, bf16[1,4,512]{2,1,0:T(4,128)(2,1)}, u32[]{:S(2)}) copy-start(bf16[1,4,512]{2,1,0:T(4,128)(2,1)} %param.16) | copy-start | bytes 12292
  8.2 3.7 %copy-start.10 = (f32[2,512]{1,0:T(2,128)S(1)}, f32[2,512]{1,0:T(2,128)}, u32[]{:S(2)}) copy-start(f32[2,512]{1,0:T(2,128)} %param.15) | copy-start | bytes 12292
  8.2 3.7 %copy-start.11 = (f32[2,512]{1,0:T(2,128)S(1)}, f32[2,512]{1,0:T(2,128)}, u32[]{:S(2)}) copy-start(f32[2,512]{1,0:T(2,128)} %param.14) | copy-start | bytes 12292
  8.2 3.9 %copy-start.2 = (f32[1,1,251,512]{3,1,2,0:T(1,128)S(1)}, f32[1,1,251,512]{3,1,2,0:T(1,128)}, u32[]{:S(2)}) copy-start(f32[1,1,251,512]{3,1,2,0:T(1,128)} %param.18) | copy-start | bytes 1542148
  10.3 1.9 %copy-start.3 = (f32[12,16,512]{2,1,0:T(8,128)S(1)}, f32[12,16,512]{2,1,0:T(8,128)}, u32[]{:S(2)}) copy-start(f32[12,16,512]{2,1,0:T(8,128)} %param.12) | copy-start | bytes 1179652
  10.3 1.9 %copy-start.4 = (f32[12,16,512]{2,1,0:T(8,128)S(1)}, f32[12,16,512]{2,1,0:T(8,128)}, u32[]{:S(2)}) copy-start(f32[12,16,512]{2,1,0:T(8,128)} %param.11) | copy-start | bytes 1179652
  10.3 3.8 %collective-permute-start.2 = (f32[502,64]{0,1:T(8,128)}, f32[502,64]{0,1:T(8,128)}, u32[]{:S(2)}, u32[]{:S(2)}) collective-permute-start(f32[502,64]{0,1:T(8,128)} %fusion.2), channel_id=1, source_target_pairs={{0,1},{1,0},{2,3},{3,2},{4,5},{5,4},{6,7},{7,6},{8,9},{9,8},{10,11... | collective-permute-start | bytes 385544 | tf_op jit(solution)/shard_map/ppermute | solution.py:21
  12.2 5.5 %copy-start.6 = (bf16[1,24,16,512]{3,2,1,0:T(8,128)(2,1)S(1)}, bf16[1,24,16,512]{3,2,1,0:T(8,128)(2,1)}, u32[]{:S(2)}) copy-start(bf16[1,24,16,512]{3,2,1,0:T(8,128)(2,1)} %param.13) | copy-start | bytes 1179652
  15.1 3.4 %copy-start.9 = (f32[502,64]{0,1:T(8,128)}, f32[502,64]{0,1:T(8,128)S(1)}, u32[]{:S(2)}) copy-start(f32[502,64]{0,1:T(8,128)S(1)} %add.95) | copy-start | bytes 385540
  15.9 6.0 %collective-permute-start.3 = (f32[283,64]{0,1:T(8,128)}, f32[283,64]{0,1:T(8,128)}, u32[]{:S(2)}, u32[]{:S(2)}) collective-permute-start(f32[283,64]{0,1:T(8,128)} %pad_maximum_fusion.1), channel_id=1, source_target_pairs={{0,128},{128,0},{1,129},{129,1},{2,130},{130,2},{3,131},{131,3},{4... | collective-permute-start | bytes 217352 | tf_op jit(solution)/shard_map/ppermute | solution.py:21
  18.5 19.5 %collective-permute-start.1 = (f32[12,16,512]{2,1,0:T(8,128)}, f32[12,16,512]{2,1,0:T(8,128)}, u32[]{:S(2)}, u32[]{:S(2)}) collective-permute-start(f32[12,16,512]{2,1,0:T(8,128)} %multiply_add_fusion.1), channel_id=1, source_target_pairs={{0,128},{128,0},{1,129},{129,1},{2,130},{130,2},{3,131},{131,3},{4... | collective-permute-start | bytes 1179656 | tf_op jit(solution)/shard_map/ppermute | solution.py:21
  19.7 22.1 %collective-permute-start.5 = (f32[251,512]{1,0:T(8,128)S(1)}, f32[251,512]{1,0:T(8,128)}, u32[]{:S(2)}, u32[]{:S(2)}) collective-permute-start(f32[251,512]{1,0:T(8,128)S(1)} %bitcast_subtract_fusion), channel_id=1, source_target_pairs={{0,128},{128,0},{1,129},{129,1},{2,130},{130,2},{3,131},{131,3},{4... | collective-permute-start | bytes 1542152 | tf_op jit(solution)/shard_map/ppermute | solution.py:21
  28.8 2.5 %collective-permute-start.4 = (f32[251,64]{0,1:T(8,128)S(1)}, f32[251,64]{0,1:T(8,128)S(1)}, u32[]{:S(2)}, u32[]{:S(2)}) collective-permute-start(f32[251,64]{0,1:T(8,128)S(1)} %slice_add_fusion), channel_id=1, source_target_pairs={{0,1},{1,0},{2,3},{3,2},{4,5},{5,4},{6,7},{7,6},{8,9},{9,8},{10,11... | collective-permute-start | bytes 192776 | tf_op jit(solution)/shard_map/ppermute | solution.py:21
  31.3 1.4 %copy-start.13 = (f32[4,512]{1,0:T(4,128)}, f32[4,512]{1,0:T(4,128)S(1)}, u32[]{:S(2)}) copy-start(f32[4,512]{1,0:T(4,128)S(1)} %add_dynamic-update-slice_fusion.1) | copy-start | bytes 24580
  34.4 1.4 %copy-start.5 = (f32[12,16,512]{2,1,0:T(8,128)S(1)}, f32[12,16,512]{2,1,0:T(8,128)}, u32[]{:S(2)}) copy-start(f32[12,16,512]{2,1,0:T(8,128)} %dynamic-slice_convert_fusion) | copy-start | bytes 1179652
  39.1 3.8 %copy-start.7 = (f32[24,16,512]{2,1,0:T(8,128)}, f32[24,16,512]{2,1,0:T(8,128)S(1)}, u32[]{:S(2)}) copy-start(f32[24,16,512]{2,1,0:T(8,128)S(1)} %add_dynamic-update-slice_fusion) | copy-start | bytes 2359300

commit v5 on v4

--- a/solution.py
+++ b/solution.py
@@ -85,9 +85,11 @@
     norm_parts = (given_norm,) + outer_partial(norm_global, norm_momentum, norm_inner[0], rep_index)
     attn_parts = (attn_parts[1], attn_parts[0], attn_parts[2])
     norm_parts = (norm_parts[1], norm_parts[0], norm_parts[2])
-    sent = lax.optimization_barrier(attn_parts[2])
-    norm_sent = jnp.concatenate([given_norm, norm_parts[2]], axis=0)
-    got_attn_partial = swap(sent, "rep")
+    attn_rows = attn_parts[2].size // width
+    norm_rows = given_norm.shape[0]
+    sent = jnp.concatenate([attn_parts[2].reshape(-1, width), given_norm, norm_parts[2]], axis=0)
+    sent = lax.optimization_barrier(sent)
+    got_buffer = swap(sent, "rep")
     new_attn_global, new_attn_momentum = outer_own(
         attn_global, attn_momentum, attn_parts[0], attn_parts[2], got_attn_inner
     )
@@ -95,7 +97,15 @@
     new_attn_global, new_attn_momentum, attn_placed = lax.optimization_barrier(
         (new_attn_global, new_attn_momentum, attn_placed)
     )
-    attn_weights = place_other(attn_placed, got_attn_partial + SHARE * given_attn, rep_index)
+    attn_other = got_buffer[:attn_rows] + SHARE * given_attn.reshape(-1, width)
+    attn_weights = place_other(attn_placed, attn_other.reshape(attn_global.shape), rep_index)
+    norm_got = got_buffer[attn_rows:]
+    new_norm_global, new_norm_momentum = outer_own(
+        norm_global, norm_momentum, norm_parts[0], norm_parts[2], norm_got[:norm_rows]
+    )
+    norm_weights = place_other(
+        place_own(new_norm_global, rep_index), norm_got[norm_rows:] + SHARE * given_norm, rep_index
+    )
 
     block_rows = emb_inner.shape[1]
     half_rows = emb_global.shape[2]
@@ -135,24 +145,14 @@
         first_is_own, half_counts[:, None] * global_coeff, jnp.zeros_like(global_coeff)
     )
     coeff_term = placed_global - own_mask[:, None] * inner_coeff
-    coeff_chip = coeff_term + swap(coeff_term, "tp")
+    tp_index = lax.axis_index("tp")
+    chip_rows = coeff_term.shape[0] // 2
+    coeff_given = lax.dynamic_slice_in_dim(coeff_term, (1 - tp_index) * chip_rows, chip_rows, 0)
+    coeff_kept = lax.dynamic_slice_in_dim(coeff_term, tp_index * chip_rows, chip_rows, 0)
+    coeff_mine = coeff_kept + swap(coeff_given, "tp")
     kept_rows = own_rows - DECAY * own_momentum
-    kept_rows, coeff_chip = lax.optimization_barrier((kept_rows, coeff_chip))
-    tp_index = lax.axis_index("tp")
-    chip_rows = coeff_chip.shape[0] // 2
-    coeff_mine = lax.dynamic_slice_in_dim(coeff_chip, tp_index * chip_rows, chip_rows, 0)
-    coeff_width = coeff_mine.shape[1]
-    coeff_sent = jnp.concatenate([coeff_mine, norm_sent.reshape(-1, coeff_width)], axis=0)
-    coeff_got = swap(coeff_sent, "rep")
-    coeff_half = coeff_mine + coeff_got[:chip_rows]
-    norm_rows = given_norm.shape[0]
-    norm_got = coeff_got[chip_rows:].reshape(-1, width)
-    new_norm_global, new_norm_momentum = outer_own(
-        norm_global, norm_momentum, norm_parts[0], norm_parts[2], norm_got[:norm_rows]
-    )
-    norm_weights = place_other(
-        place_own(new_norm_global, rep_index), norm_got[norm_rows:] + SHARE * given_norm, rep_index
-    )
+    kept_rows, coeff_mine = lax.optimization_barrier((kept_rows, coeff_mine))
+    coeff_half = coeff_mine + swap(coeff_mine, "rep")
     coeff_sum = place_pair(tp_index == 0, coeff_half, swap(coeff_half, "tp"))
     got_rows = swap(kept_rows, "rep")
     emb_grad = (

time: 44.6 us -> 43.2 us (0.969)
  waiting for transfers between devices: 3.14 us -> 7.73 us
  local copies, waits for them, and re-layouts: 7.73 us -> 3.15 us
  other arithmetic: 18 us -> 17.3 us
  matrix products: 3.63 us -> 2.97 us
    slice x5 -> x0, local copies, waits for them, and re-layouts: 5.84 us -> none  [the longest x3 3.05 us: step_body(): norm_got[norm_rows:] + SHARE * given_norm]
    ppermute x6, waiting for transfers between devices: 3.14 us -> 7.73 us  [swap(): return lax.ppermute(x, axis, perm=SWAP)]
    add x2, other arithmetic: 1.86 us -> 1.04 us  [outer_partial(): partial = KEEP * global_part - DECAY * momentum_part + SHARE * own_inner]
    unnamed x29 -> x35, local copies, waits for them, and re-layouts: 1.38 us -> 2.13 us
    dot_general x1, matrix products: 1.26 us -> 0.6 us  [step_body(): jnp.dot(emb_inner[0].astype(jnp.float32), basis_half, precision=lax.Preci...]
    dynamic_slice x1, local copies, waits for them, and re-layouts: 0.09 us -> 0.72 us  [step_body(): lax.dynamic_slice_in_dim(coeff_term, (1 - tp_index) * chip_rows, chip_row...]
    add x2 -> x3, other arithmetic: 2 us -> 2.6 us  [the longest x1 1.04 us: step_body(): attn_other = got_buffer[:attn_rows] + SHARE * given_attn.reshape(-1, width)]
    convert_element_type x2, other arithmetic: 1.66 us -> 1.07 us  [outer_sends(): given_inner = lax.dynamic_slice_in_dim(inner_all, (1 - rep_index) * owned...]
  transfers between devices with their start and end apart: 6 -> 6, of which waited for: 2 -> 2; matrix products, arithmetic and copies ran while one was open for 59% -> 48% of each run, Pallas kernels for 0% -> 0%
where the time goes in v5:
time: 43.2 us; the launch traced here: 42.7 us
  other arithmetic  17.3 us (40%)
  starting transfers between devices  10.5 us (24%)
  waiting for transfers between devices  7.73 us (18%)
  local copies, waits for them, and re-layouts  3.15 us (7%)
  matrix products  2.97 us (7%)
  between operations  0.95 us (2%)
    ppermute x6, starting transfers between devices, swap(): return lax.ppermute(x, axis, perm=SWAP)  10.5 us
    ppermute x6, waiting for transfers between devices, swap(): return lax.ppermute(x, axis, perm=SWAP)  7.73 us
    dynamic_update_slice x2, other arithmetic, place_own(): return lax.dynamic_update_slice_in_dim(empty, own, rep_index * rows, 0)  3.46 us
    unnamed x35, local copies, waits for them, and re-layouts  2.13 us
    add x1, other arithmetic, step_body(): new_emb_momentum = MOMENTUM * emb_momentum + own_grad  1.49 us
    dynamic_update_slice x1, other arithmetic, place_other(): lax.dynamic_update_slice_in_dim(placed, other, (1 - rep_index) * rows, 0)  1.4 us
    dot_general x1, matrix products, step_body(): jnp.dot(coeff_sum, basis_half.T, precision=lax.Precision.HIGHEST, preferr...  1.14 us
    convert_element_type x2, other arithmetic, outer_sends(): given_inner = lax.dynamic_slice_in_dim(inner_all, (1 - rep_index) * owned...  1.07 us
  transfers between devices with their start and end apart: 6, of which 2 were waited for; matrix products, arithmetic and copies ran while one was open for 48% of the time, Pallas kernels for 0%

profile of v5, /device:TPU:1, one launch (start us, length us, event | category | flops | bytes accessed | tf_op | source)
XLA Modules:
  0.0 42.7 jit_solution(2437666572151640554)
XLA Ops:
  0.7 1.1 %bitcast_convert_fusion = f32[12,16,512]{2,1,0:T(8,128)S(1)} fusion(bf16[1,24,16,512]{3,2,1,0:T(8,128)(2,1)} %param.13, s32[]{:T(128)S(6)} %select_n.92), kind=kLoop, calls=%fused_computation.30 | loop fusion | flops 98304 | bytes 589828 | tf_op jit(solution)/shard_map/convert_element_type | solution.py:34
  1.8 3.8 %collective-permute-start = (f32[12,16,512]{2,1,0:T(8,128)S(1)}, f32[12,16,512]{2,1,0:T(8,128)}, u32[]{:S(2)}, u32[]{:S(2)}) collective-permute-start(f32[12,16,512]{2,1,0:T(8,128)S(1)} %bitcast_convert_fusion), channel_id=1, source_target_pairs={{0,128},{128,0},{1,129},{129,1},{2,130},{130,2},{3,131},{131,3},{4... | collective-permute-start | bytes 1179656 | tf_op jit(solution)/shard_map/ppermute | solution.py:21
  5.6 1.1 %and_select_fusion.1 = (s32[2,8192]{1,0:T(2,128)S(1)}, s32[2,8192]{1,0:T(2,128)S(1)}) fusion(s32[2,8192]{1,0:T(2,128)} %param.21, s32[]{:T(128)S(6)} %mul.170), kind=kLoop, calls=%fused_computation.38 | loop fusion | flops 327680 | bytes 196612 | tf_op jit(solution)/shard_map/jit(floor_divide)/jit(_where)/select_n | solution.py:119
  6.6 0.9 %compare_and_fusion = pred[2,8192]{1,0:T(4,128)(4,1)S(1)} fusion(s32[2,8192]{1,0:T(2,128)} %param.21, s32[]{:T(128)S(6)} %mul.170), kind=kLoop, calls=%fused_computation.37 | loop fusion | flops 65536 | bytes 81924 | tf_op jit(solution)/shard_map/and | solution.py:116
  10.4 1.0 %collective-permute-start.2 = (f32[251,64]{0,1:T(8,128)}, f32[251,64]{0,1:T(8,128)}, u32[]{:S(2)}, u32[]{:S(2)}) collective-permute-start(f32[251,64]{0,1:T(8,128)} %constant_dynamic-slice_fusion.2), channel_id=1, source_target_pairs={{0,1},{1,0},{2,3},{3,2},{4,5},{5,4},{6,7},{7,6},{8,9},{9,8},{10,11... | collective-permute-start | bytes 192776 | tf_op jit(solution)/shard_map/ppermute | solution.py:21
  11.4 0.8 %dynamic-slice_convert_fusion = f32[12,16,512]{2,1,0:T(8,128)} fusion(bf16[24,16,512]{2,1,0:T(8,128)(2,1)S(1)} %bitcast.45, s32[]{:T(128)S(6)} %select_n.91), kind=kLoop, calls=%fused_computation.32 | loop fusion | flops 98304 | bytes 589828 | tf_op jit(solution)/shard_map/convert_element_type | solution.py:40
  12.2 1.0 %multiply_add_fusion.1 = f32[12,16,512]{2,1,0:T(8,128)S(1)} fusion(f32[12,16,512]{2,1,0:T(8,128)S(1)} %copy-done.3, f32[12,16,512]{2,1,0:T(8,128)S(1)} %copy-done.5, bf16[24,16,512]{2,1,0:T(8,128)(2,1)} %bitcast.44, s32[]{:T(128)S(6)} %select_n.91), kind=kLoop, calls=%fused_computation.27 | loop fusion | flops 589824 | bytes 1376260 | tf_op jit(solution)/shard_map/add | solution.py:41
  14.2 0.9 %dynamic-slice_add_fusion = f32[251,64]{0,1:T(8,128)S(1)} fusion(f32[251,64]{0,1:T(8,128)} %collective-permute-done.2, f32[502,64]{0,1:T(8,128)S(1)} %copy-done.12, s32[]{:T(128)S(6)} %select_n.106), kind=kLoop, calls=%fused_computation.45 | loop fusion | flops 16064 | bytes 192772 | tf_op jit(solution)/shard_map/add | solution.py:152
  15.1 1.8 %collective-permute-start.3 = (f32[251,64]{0,1:T(8,128)S(1)}, f32[251,64]{0,1:T(8,128)S(1)}, u32[]{:S(2)}, u32[]{:S(2)}) collective-permute-start(f32[251,64]{0,1:T(8,128)S(1)} %dynamic-slice_add_fusion), channel_id=1, source_target_pairs={{0,128},{128,0},{1,129},{129,1},{2,130},{130,2},{3,131},{131,3},{4... | collective-permute-start | bytes 192776 | tf_op jit(solution)/shard_map/ppermute | solution.py:21
  16.9 0.8 %pad_maximum_fusion.1 = f32[196,512]{1,0:T(8,128)} fusion(f32[2,512]{1,0:T(2,128)S(1)} %multiply_add_fusion.3, f32[2,512]{1,0:T(2,128)S(1)} %get-tuple-element.62, f32[192,512]{1,0:T(8,128)S(1)} %bitcast.42), kind=kLoop, calls=%fused_computation.23 | loop fusion | flops 200704 | bytes 802816 | tf_op jit(solution)/shard_map/concatenate | solution.py:90
  17.7 1.2 %collective-permute-start.1 = (f32[196,512]{1,0:T(8,128)}, f32[196,512]{1,0:T(8,128)}, u32[]{:S(2)}, u32[]{:S(2)}) collective-permute-start(f32[196,512]{1,0:T(8,128)} %pad_maximum_fusion.1), channel_id=1, source_target_pairs={{0,128},{128,0},{1,129},{129,1},{2,130},{130,2},{3,131},{131,3},{4... | collective-permute-start | bytes 1204232 | tf_op jit(solution)/shard_map/ppermute | solution.py:21
  18.9 1.4 %collective-permute-done.3 = f32[251,64]{0,1:T(8,128)S(1)} collective-permute-done((f32[251,64]{0,1:T(8,128)S(1)}, f32[251,64]{0,1:T(8,128)S(1)}, u32[]{:S(2)}, u32[]{:S(2)}) %collective-permute-start.3) | collective-permute-done | bytes 64288 | tf_op jit(solution)/shard_map/ppermute | solution.py:21
  21.0 0.9 %collective-permute-start.4 = (f32[251,64]{0,1:T(8,128)}, f32[251,64]{0,1:T(8,128)}, u32[]{:S(2)}, u32[]{:S(2)}) collective-permute-start(f32[251,64]{0,1:T(8,128)} %add.106), channel_id=1, source_target_pairs={{0,1},{1,0},{2,3},{3,2},{4,5},{5,4},{6,7},{7,6},{8,9},{9,8},{10,11... | collective-permute-start | bytes 192776 | tf_op jit(solution)/shard_map/ppermute | solution.py:21
  21.9 1.8 %collective-permute-start.5 = (f32[251,512]{1,0:T(8,128)S(1)}, f32[251,512]{1,0:T(8,128)S(1)}, u32[]{:S(2)}, u32[]{:S(2)}) collective-permute-start(f32[251,512]{1,0:T(8,128)S(1)} %bitcast_subtract_fusion), channel_id=1, source_target_pairs={{0,128},{128,0},{1,129},{129,1},{2,130},{130,2},{3,131},{131,3},{4... | collective-permute-start | bytes 1542152 | tf_op jit(solution)/shard_map/ppermute | solution.py:21
  23.7 0.9 %broadcast_select_fusion.3 = (f32[251,64]{0,1:T(8,128)S(1)}, f32[251,64]{0,1:T(8,128)S(1)}) fusion(f32[251,64]{0,1:T(8,128)} %add.106, f32[251,64]{0,1:T(8,128)} %collective-permute-done.4, pred[]{:T(512)S(6)} %eq.34), kind=kLoop, calls=%fused_computation.51 | loop fusion | flops 32128 | bytes 257025 | tf_op jit(solution)/shard_map/jit(_where)/select_n | solution.py:25
  24.6 1.1 %convolution_multiply_fusion = f32[502,512]{1,0:T(8,128)S(1)} fusion(f32[251,64]{0,1:T(8,128)S(1)} %get-tuple-element.57, f32[251,64]{0,1:T(8,128)S(1)} %get-tuple-element.56, f32[1024,64]{0,1:T(8,128)S(1)} %copy-done.10, s32[]{:T(128)S(6)} %select_n.100), kind=kOutput, calls=%fused_computation.2 | convolution fusion | flops 197683584 | bytes 1290244 | tf_op jit(solution)/shard_map/dot_general | solution.py:159
  26.2 1.5 %reshape_add_fusion = f32[1,1,251,512]{3,1,2,0:T(1,128)} fusion(f32[251,512]{1,0:T(8,128)S(1)} %get-tuple-element.45, f32[1,1,251,512]{3,1,2,0:T(1,128)S(1)} %copy-done.2), kind=kLoop, calls=%fused_computation.20 | loop fusion | flops 257024 | bytes 1542144 | tf_op jit(solution)/shard_map/add | solution.py:170
  27.7 1.3 %copy.22 = f32[1,1,251,512]{3,1,2,0:T(1,128)} copy(f32[1,1,251,512]{3,2,1,0:T(8,128)S(1)} %bitcast_subtract_fusion.1) | data formatting | bytes 1028096
  29.1 2.1 %constant_dynamic-update-slice_fusion.2 = (f32[24,16,512]{2,1,0:T(8,128)S(1)}, f32[12,16,512]{2,1,0:T(8,128)}, f32[12,16,512]{2,1,0:T(8,128)}) fusion(f32[24,16,512]{2,1,0:T(8,128)S(1)} %broadcast_in_dim.6, s32[]{:T(128)S(6)} %select_n.91, f32[12,16,512]{2,1,0:T(8,128)S(1)} %multiply_add_fusion.1, f32[12,16,512]{2,1,0:T(8,128)} %collective-permute-done, ...), kind=kLoop, calls=%fused_computation.69 | loop fusion | flops 688128 | bytes 3145732 | tf_op jit(solution)/shard_map/dynamic_update_slice | solution.py:55
  31.2 1.0 %slice_add_fusion = f32[192,512]{1,0:T(8,128)S(1)} fusion(f32[196,512]{1,0:T(8,128)} %collective-permute-done.1, f32[12,16,512]{2,1,0:T(8,128)S(1)} %broadcast_multiply_fusion), kind=kLoop, calls=%fused_computation.24 | loop fusion | flops 98304 | bytes 1179648 | tf_op jit(solution)/shard_map/add | solution.py:100
  32.3 1.4 %constant_dynamic-update-slice_fusion = (f32[4,512]{1,0:T(4,128)S(1)}, f32[2,512]{1,0:T(2,128)}) fusion(f32[4,512]{1,0:T(4,128)S(1)} %broadcast_in_dim.7, s32[]{:T(128)S(6)} %select_n.94, f32[2,512]{1,0:T(2,128)S(1)} %multiply_add_fusion.3, f32[196,512]{1,0:T(8,128)} %collective-permute-done.1), kind=kLoop, calls=%fused_computation.65 | loop fusion | flops 2048 | bytes 16388 | tf_op jit(solution)/shard_map/dynamic_update_slice | solution.py:55
  33.7 1.4 %fusion.18 = (f32[4,512]{1,0:T(4,128)S(1)}, f32[2,512]{1,0:T(2,128)}) fusion(f32[4,512]{1,0:T(4,128)S(1)} %get-tuple-element.46, s32[]{:T(128)S(6)} %select_n.93, f32[196,512]{1,0:T(8,128)} %collective-permute-done.1, f32[2,512]{1,0:T(2,128)S(1)} %get-tuple-element.62, f32[2,512]{1,0:T(2,128)S(1)} %copy-done.14, f32[2,512]{1,0:T(2,128)S(1)} %get-tuple-element.28, ...), kind=kLoop, calls=%fused_computation.54 | loop fusion | flops 7168 | bytes 32772 | tf_op jit(solution)/shard_map/dynamic_update_slice | solution.py:60
  35.1 6.3 %collective-permute-done.5 = f32[251,512]{1,0:T(8,128)S(1)} collective-permute-done((f32[251,512]{1,0:T(8,128)S(1)}, f32[251,512]{1,0:T(8,128)S(1)}, u32[]{:S(2)}, u32[]{:S(2)}) %collective-permute-start.5) | collective-permute-done | bytes 514080 | tf_op jit(solution)/shard_map/ppermute | solution.py:21
  41.6 1.1 %pad_maximum_fusion = f32[502,512]{1,0:T(8,128)} fusion(f32[251,512]{1,0:T(8,128)S(1)} %get-tuple-element.51, f32[251,512]{1,0:T(8,128)S(1)} %get-tuple-element.50), kind=kLoop, calls=%fused_computation.11 | loop fusion | flops 257024 | bytes 2056192 | tf_op jit(solution)/shard_map/concatenate | solution.py:27
  (58 shorter events, 5.1 us)
Async XLA Ops:
  0.6 8.4 %copy-start = (bf16[1,502,512]{2,1,0:T(8,128)(2,1)S(1)}, bf16[1,502,512]{2,1,0:T(8,128)(2,1)}, u32[]{:S(2)}) copy-start(bf16[1,502,512]{2,1,0:T(8,128)(2,1)} %param.19) | copy-start | bytes 1542148
  0.7 7.7 %copy-start.1 = (f32[1,1,251,512]{3,1,2,0:T(1,128)S(1)}, f32[1,1,251,512]{3,1,2,0:T(1,128)}, u32[]{:S(2)}) copy-start(f32[1,1,251,512]{3,1,2,0:T(1,128)} %param.17) | copy-start | bytes 1542148
  0.7 7.7 %copy-start.10 = (f32[1024,64]{0,1:T(8,128)S(1)}, f32[1024,64]{0,1:T(8,128)}, u32[]{:S(2)}) copy-start(f32[1024,64]{0,1:T(8,128)} %param.20) | copy-start | bytes 786436
  1.8 27.2 %collective-permute-start = (f32[12,16,512]{2,1,0:T(8,128)S(1)}, f32[12,16,512]{2,1,0:T(8,128)}, u32[]{:S(2)}, u32[]{:S(2)}) collective-permute-start(f32[12,16,512]{2,1,0:T(8,128)S(1)} %bitcast_convert_fusion), channel_id=1, source_target_pairs={{0,128},{128,0},{1,129},{129,1},{2,130},{130,2},{3,131},{131,3},{4... | collective-permute-start | bytes 1179656 | tf_op jit(solution)/shard_map/ppermute | solution.py:21
  8.2 3.2 %copy-start.8 = (bf16[1,24,16,512]{3,2,1,0:T(8,128)(2,1)S(1)}, bf16[1,24,16,512]{3,2,1,0:T(8,128)(2,1)}, u32[]{:S(2)}) copy-start(bf16[1,24,16,512]{3,2,1,0:T(8,128)(2,1)} %param.13) | copy-start | bytes 1179652
  8.4 3.7 %copy-start.3 = (f32[12,16,512]{2,1,0:T(8,128)S(1)}, f32[12,16,512]{2,1,0:T(8,128)}, u32[]{:S(2)}) copy-start(f32[12,16,512]{2,1,0:T(8,128)} %param.12) | copy-start | bytes 1179652
  8.4 3.7 %copy-start.5 = (f32[12,16,512]{2,1,0:T(8,128)S(1)}, f32[12,16,512]{2,1,0:T(8,128)}, u32[]{:S(2)}) copy-start(f32[12,16,512]{2,1,0:T(8,128)} %param.11) | copy-start | bytes 1179652
  9.7 2.5 %copy-start.11 = (f32[502,64]{0,1:T(8,128)}, f32[502,64]{0,1:T(8,128)S(1)}, u32[]{:S(2)}) copy-start(f32[502,64]{0,1:T(8,128)S(1)} %fusion.2) | copy-start | bytes 385540
  9.7 3.5 %copy-start.2 = (f32[1,1,251,512]{3,1,2,0:T(1,128)S(1)}, f32[1,1,251,512]{3,1,2,0:T(1,128)}, u32[]{:S(2)}) copy-start(f32[1,1,251,512]{3,1,2,0:T(1,128)} %param.18) | copy-start | bytes 1542148
  10.4 3.6 %collective-permute-start.2 = (f32[251,64]{0,1:T(8,128)}, f32[251,64]{0,1:T(8,128)}, u32[]{:S(2)}, u32[]{:S(2)}) collective-permute-start(f32[251,64]{0,1:T(8,128)} %constant_dynamic-slice_fusion.2), channel_id=1, source_target_pairs={{0,1},{1,0},{2,3},{3,2},{4,5},{5,4},{6,7},{7,6},{8,9},{9,8},{10,11... | collective-permute-start | bytes 192776 | tf_op jit(solution)/shard_map/ppermute | solution.py:21
  13.2 0.7 %copy-start.13 = (f32[2,512]{1,0:T(2,128)S(1)}, f32[2,512]{1,0:T(2,128)}, u32[]{:S(2)}) copy-start(f32[2,512]{1,0:T(2,128)} %param.15) | copy-start | bytes 12292
  13.2 0.7 %copy-start.14 = (f32[2,512]{1,0:T(2,128)S(1)}, f32[2,512]{1,0:T(2,128)}, u32[]{:S(2)}) copy-start(f32[2,512]{1,0:T(2,128)} %param.14) | copy-start | bytes 12292
  13.2 0.7 %copy-start.15 = (bf16[1,4,512]{2,1,0:T(4,128)(2,1)S(1)}, bf16[1,4,512]{2,1,0:T(4,128)(2,1)}, u32[]{:S(2)}) copy-start(bf16[1,4,512]{2,1,0:T(4,128)(2,1)} %param.16) | copy-start | bytes 12292
  13.2 0.9 %copy-start.12 = (f32[502,64]{0,1:T(8,128)S(1)}, f32[502,64]{0,1:T(8,128)}, u32[]{:S(2)}) copy-start(f32[502,64]{0,1:T(8,128)} %copy-done.11) | copy-start | bytes 385540
  15.1 5.2 %collective-permute-start.3 = (f32[251,64]{0,1:T(8,128)S(1)}, f32[251,64]{0,1:T(8,128)S(1)}, u32[]{:S(2)}, u32[]{:S(2)}) collective-permute-start(f32[251,64]{0,1:T(8,128)S(1)} %dynamic-slice_add_fusion), channel_id=1, source_target_pairs={{0,128},{128,0},{1,129},{129,1},{2,130},{130,2},{3,131},{131,3},{4... | collective-permute-start | bytes 192776 | tf_op jit(solution)/shard_map/ppermute | solution.py:21
  17.7 13.5 %collective-permute-start.1 = (f32[196,512]{1,0:T(8,128)}, f32[196,512]{1,0:T(8,128)}, u32[]{:S(2)}, u32[]{:S(2)}) collective-permute-start(f32[196,512]{1,0:T(8,128)} %pad_maximum_fusion.1), channel_id=1, source_target_pairs={{0,128},{128,0},{1,129},{129,1},{2,130},{130,2},{3,131},{131,3},{4... | collective-permute-start | bytes 1204232 | tf_op jit(solution)/shard_map/ppermute | solution.py:21
  21.0 2.8 %collective-permute-start.4 = (f32[251,64]{0,1:T(8,128)}, f32[251,64]{0,1:T(8,128)}, u32[]{:S(2)}, u32[]{:S(2)}) collective-permute-start(f32[251,64]{0,1:T(8,128)} %add.106), channel_id=1, source_target_pairs={{0,1},{1,0},{2,3},{3,2},{4,5},{5,4},{6,7},{7,6},{8,9},{9,8},{10,11... | collective-permute-start | bytes 192776 | tf_op jit(solution)/shard_map/ppermute | solution.py:21
  21.9 19.5 %collective-permute-start.5 = (f32[251,512]{1,0:T(8,128)S(1)}, f32[251,512]{1,0:T(8,128)S(1)}, u32[]{:S(2)}, u32[]{:S(2)}) collective-permute-start(f32[251,512]{1,0:T(8,128)S(1)} %bitcast_subtract_fusion), channel_id=1, source_target_pairs={{0,128},{128,0},{1,129},{129,1},{2,130},{130,2},{3,131},{131,3},{4... | collective-permute-start | bytes 1542152 | tf_op jit(solution)/shard_map/ppermute | solution.py:21
  27.7 1.4 %copy-start.4 = (f32[12,16,512]{2,1,0:T(8,128)S(1)}, f32[12,16,512]{2,1,0:T(8,128)}, u32[]{:S(2)}) copy-start(f32[12,16,512]{2,1,0:T(8,128)} %param.12) | copy-start | bytes 1179652
  27.7 1.4 %copy-start.6 = (f32[12,16,512]{2,1,0:T(8,128)S(1)}, f32[12,16,512]{2,1,0:T(8,128)}, u32[]{:S(2)}) copy-start(f32[12,16,512]{2,1,0:T(8,128)} %param.11) | copy-start | bytes 1179652
  27.7 1.4 %copy-start.7 = (f32[12,16,512]{2,1,0:T(8,128)S(1)}, f32[12,16,512]{2,1,0:T(8,128)}, u32[]{:S(2)}) copy-start(f32[12,16,512]{2,1,0:T(8,128)} %dynamic-slice_convert_fusion) | copy-start | bytes 1179652
  32.3 9.3 %copy-start.9 = (f32[24,16,512]{2,1,0:T(8,128)}, f32[24,16,512]{2,1,0:T(8,128)S(1)}, u32[]{:S(2)}) copy-start(f32[24,16,512]{2,1,0:T(8,128)S(1)} %constant_dynamic-update-slice_fusion.1) | copy-start | bytes 2359300
  35.1 6.5 %copy-start.16 = (f32[4,512]{1,0:T(4,128)}, f32[4,512]{1,0:T(4,128)S(1)}, u32[]{:S(2)}) copy-start(f32[4,512]{1,0:T(4,128)S(1)} %get-tuple-element.53) | copy-start | bytes 24580

commit v6 on v5

--- a/solution.py
+++ b/solution.py
@@ -173,7 +173,14 @@
     new_emb_global, new_emb_momentum, own_flat, other_grad = lax.optimization_barrier(
         (new_emb_global, new_emb_momentum, own_flat, other_grad)
     )
-    emb_weights = place_pair(first_is_own, own_flat, got_rows - STEP * other_grad)
+    row_ids = lax.broadcasted_iota(jnp.int32, (block_rows, half_width), 0)
+    in_own_half = (row_ids >= half_start) & (row_ids < half_start + half_rows)
+    emb_weights = jnp.where(
+        in_own_half,
+        jnp.concatenate([own_flat, own_flat], axis=0),
+        jnp.concatenate([got_rows, got_rows], axis=0)
+        - STEP * jnp.concatenate([other_grad, other_grad], axis=0),
+    )
     return (
         new_attn_global,
         new_attn_momentum,

time: 43.2 us -> 43.5 us (level)
  the two profiles are of different devices: /device:TPU:1 before, /device:TPU:2 now
where the time goes in v6:
time: 43.5 us; the launch traced here: 42.6 us
  other arithmetic  14.9 us (34%)
  waiting for transfers between devices  11.8 us (27%)
  starting transfers between devices  10.3 us (24%)
  matrix products  2.97 us (7%)
  local copies, waits for them, and re-layouts  1.79 us (4%)
  between operations  0.98 us (2%)
    ppermute x6, waiting for transfers between devices, swap(): return lax.ppermute(x, axis, perm=SWAP)  11.8 us
    ppermute x6, starting transfers between devices, swap(): return lax.ppermute(x, axis, perm=SWAP)  10.3 us
    dynamic_update_slice x2, other arithmetic, place_own(): return lax.dynamic_update_slice_in_dim(empty, own, rep_index * rows, 0)  3.46 us
    convert_element_type x1, other arithmetic, outer_partial(): lax.dynamic_slice_in_dim(inner_all, rep_index * owned, owned, 0)  1.71 us
    add x1, other arithmetic, step_body(): new_emb_momentum = MOMENTUM * emb_momentum + own_grad  1.49 us
    unnamed x33, local copies, waits for them, and re-layouts  1.4 us
    dynamic_update_slice x1, other arithmetic, place_other(): lax.dynamic_update_slice_in_dim(placed, other, (1 - rep_index) * rows, 0)  1.4 us
    select_n x1, other arithmetic, step_body(): jnp.where(in_own_half, jnp.concatenate([own_flat, own_flat], axis=0), jnp...  1.24 us
  transfers between devices with their start and end apart: 6, of which 3 were waited for; matrix products, arithmetic and copies ran while one was open for 40% of the time, Pallas kernels for 0%

profile of v6, /device:TPU:2, one launch (start us, length us, event | category | flops | bytes accessed | tf_op | source)
XLA Modules:
  0.0 42.6 jit_solution(11048272873208209307)
XLA Ops:
  0.7 1.1 %bitcast_convert_fusion = f32[12,16,512]{2,1,0:T(8,128)S(1)} fusion(bf16[1,24,16,512]{3,2,1,0:T(8,128)(2,1)} %param.13, s32[]{:T(128)S(6)} %select_n.84), kind=kLoop, calls=%fused_computation.29 | loop fusion | flops 98304 | bytes 589828 | tf_op jit(solution)/shard_map/convert_element_type | solution.py:34
  1.8 3.3 %collective-permute-start = (f32[12,16,512]{2,1,0:T(8,128)S(1)}, f32[12,16,512]{2,1,0:T(8,128)}, u32[]{:S(2)}, u32[]{:S(2)}) collective-permute-start(f32[12,16,512]{2,1,0:T(8,128)S(1)} %bitcast_convert_fusion), channel_id=1, source_target_pairs={{0,128},{128,0},{1,129},{129,1},{2,130},{130,2},{3,131},{131,3},{4... | collective-permute-start | bytes 1179656 | tf_op jit(solution)/shard_map/ppermute | solution.py:21
  5.1 1.7 %dynamic-slice_convert_fusion = f32[12,16,512]{2,1,0:T(8,128)} fusion(bf16[24,16,512]{2,1,0:T(8,128)(2,1)} %bitcast.44, s32[]{:T(128)S(6)} %select_n.83), kind=kLoop, calls=%fused_computation.31 | loop fusion | flops 98304 | bytes 589828 | tf_op jit(solution)/shard_map/convert_element_type | solution.py:40
  7.0 0.8 %pad_maximum_fusion = f32[196,512]{1,0:T(8,128)} fusion(f32[2,512]{1,0:T(2,128)S(1)} %multiply_add_fusion.3, f32[2,512]{1,0:T(2,128)S(1)} %get-tuple-element.60, f32[192,512]{1,0:T(8,128)S(1)} %bitcast.42), kind=kLoop, calls=%fused_computation.24 | loop fusion | flops 200704 | bytes 802816 | tf_op jit(solution)/shard_map/concatenate | solution.py:90
  7.8 0.3 collective-permute-start.1
  8.5 0.6 %fusion.3 = pred[2,16,32]{2,1,0:T(8,128)(4,1)S(1)} fusion(s32[2,8192]{1,0:T(2,128)S(1)} %get-tuple-element.59, s32[2,8192]{1,0:T(2,128)S(1)} %get-tuple-element.58, pred[2,8192]{1,0:T(4,128)(4,1)S(1)} %compare_and_fusion), kind=kOutput, calls=%fused_computation.7 | convolution fusion | flops 17826816 | bytes 148480 | tf_op jit(solution)/shard_map/gik,gjk->gij/dot_general | solution.py:122
  9.3 0.6 %select_bitcast_fusion.1 = (f32[251,64]{0,1:T(8,128)S(1)}, f32[251,64]{0,1:T(8,128)S(1)}) fusion(pred[]{:T(512)S(6)} %eq.35, f32[1,1,251,512]{3,1,2,0:T(1,128)S(1)} %copy-done.1, f32[1024,64]{0,1:T(8,128)S(1)} %copy-done.10, s32[]{:T(128)S(6)} %select_n.92, f32[251]{0:T(256)S(1)} %dynamic_slice.39), kind=kOutput, calls=%fused_computation.46 | convolution fusion | flops 98745408 | bytes 774661 | tf_op jit(solution)/shard_map/dot_general | solution.py:135
  9.9 0.6 %fusion.2 = f32[502,64]{0,1:T(8,128)S(1)} fusion(bf16[1,502,512]{2,1,0:T(8,128)(2,1)S(1)} %copy-done, f32[251,64]{0,1:T(8,128)S(1)} %get-tuple-element.57, f32[251,64]{0,1:T(8,128)S(1)} %get-tuple-element.56, f32[1024,64]{0,1:T(8,128)S(1)} %copy-done.10, s32[]{:T(128)S(6)} %select_n.92, f32[502]{0:T(512)S(1)} %bitcast.46), kind=kOutput, calls=%fused_computation.5 | convolution fusion | flops 197490816 | bytes 908804 | tf_op jit(solution)/shard_map/dot_general | solution.py:138
  10.9 1.1 %collective-permute-done.2 = f32[251,64]{0,1:T(8,128)S(1)} collective-permute-done((f32[251,64]{0,1:T(8,128)S(1)}, f32[251,64]{0,1:T(8,128)S(1)}, u32[]{:S(2)}, u32[]{:S(2)}) %collective-permute-start.2) | collective-permute-done | bytes 64288 | tf_op jit(solution)/shard_map/ppermute | solution.py:21
  12.0 0.7 %dynamic-slice_add_fusion = f32[251,64]{0,1:T(8,128)} fusion(f32[251,64]{0,1:T(8,128)S(1)} %collective-permute-done.2, f32[502,64]{0,1:T(8,128)S(1)} %fusion.2, s32[]{:T(128)S(6)} %select_n.98), kind=kLoop, calls=%fused_computation.44 | loop fusion | flops 16064 | bytes 192772 | tf_op jit(solution)/shard_map/add | solution.py:152
  12.7 3.2 %collective-permute-start.3 = (f32[251,64]{0,1:T(8,128)}, f32[251,64]{0,1:T(8,128)}, u32[]{:S(2)}, u32[]{:S(2)}) collective-permute-start(f32[251,64]{0,1:T(8,128)} %dynamic-slice_add_fusion), channel_id=1, source_target_pairs={{0,128},{128,0},{1,129},{129,1},{2,130},{130,2},{3,131},{131,3},{4... | collective-permute-start | bytes 192776 | tf_op jit(solution)/shard_map/ppermute | solution.py:21
  15.9 8.6 %collective-permute-done.3 = f32[251,64]{0,1:T(8,128)} collective-permute-done((f32[251,64]{0,1:T(8,128)}, f32[251,64]{0,1:T(8,128)}, u32[]{:S(2)}, u32[]{:S(2)}) %collective-permute-start.3) | collective-permute-done | bytes 64288 | tf_op jit(solution)/shard_map/ppermute | solution.py:21
  24.6 0.9 %add.109 = f32[251,64]{0,1:T(8,128)S(1)} add(f32[251,64]{0,1:T(8,128)} %dynamic-slice_add_fusion, f32[251,64]{0,1:T(8,128)} %collective-permute-done.3) | non-fusion elementwise | flops 16064 | bytes 192768 | tf_op jit(solution)/shard_map/add | solution.py:155
  25.6 3.3 %collective-permute-start.5 = (f32[251,512]{1,0:T(8,128)S(1)}, f32[251,512]{1,0:T(8,128)S(1)}, u32[]{:S(2)}, u32[]{:S(2)}) collective-permute-start(f32[251,512]{1,0:T(8,128)S(1)} %bitcast_subtract_fusion), channel_id=1, source_target_pairs={{0,128},{128,0},{1,129},{129,1},{2,130},{130,2},{3,131},{131,3},{4... | collective-permute-start | bytes 1542152 | tf_op jit(solution)/shard_map/ppermute | solution.py:21
  28.9 1.1 %convolution_multiply_fusion = f32[502,512]{1,0:T(8,128)S(1)} fusion(f32[251,64]{0,1:T(8,128)S(1)} %get-tuple-element.55, f32[251,64]{0,1:T(8,128)S(1)} %get-tuple-element.54, f32[1024,64]{0,1:T(8,128)S(1)} %copy-done.10, s32[]{:T(128)S(6)} %select_n.92), kind=kOutput, calls=%fused_computation.2 | convolution fusion | flops 197683584 | bytes 1290244 | tf_op jit(solution)/shard_map/dot_general | solution.py:159
  30.0 0.2 multiply_subtract_fusion
  30.4 1.5 %reshape_add_fusion = f32[1,1,251,512]{3,1,2,0:T(1,128)} fusion(f32[251,512]{1,0:T(8,128)S(1)} %get-tuple-element.45, f32[1,1,251,512]{3,1,2,0:T(1,128)S(1)} %copy-done.2), kind=kLoop, calls=%fused_computation.21 | loop fusion | flops 257024 | bytes 1542144 | tf_op jit(solution)/shard_map/add | solution.py:170
  31.9 1.3 %copy.22 = f32[1,1,251,512]{3,1,2,0:T(1,128)} copy(f32[1,1,251,512]{3,2,1,0:T(8,128)S(1)} %bitcast_subtract_fusion.1) | data formatting | bytes 1028096
  33.4 2.1 %constant_dynamic-update-slice_fusion.2 = (f32[24,16,512]{2,1,0:T(8,128)S(1)}, f32[12,16,512]{2,1,0:T(8,128)}, f32[12,16,512]{2,1,0:T(8,128)}) fusion(f32[24,16,512]{2,1,0:T(8,128)S(1)} %broadcast_in_dim.6, s32[]{:T(128)S(6)} %select_n.83, f32[12,16,512]{2,1,0:T(8,128)S(1)} %multiply_add_fusion.1, f32[12,16,512]{2,1,0:T(8,128)} %collective-permute-done, ...), kind=kLoop, calls=%fused_computation.68 | loop fusion | flops 688128 | bytes 3145732 | tf_op jit(solution)/shard_map/dynamic_update_slice | solution.py:55
  35.5 1.0 %slice_add_fusion = f32[192,512]{1,0:T(8,128)S(1)} fusion(f32[196,512]{1,0:T(8,128)} %collective-permute-done.1, f32[12,16,512]{2,1,0:T(8,128)S(1)} %broadcast_multiply_fusion), kind=kLoop, calls=%fused_computation.25 | loop fusion | flops 98304 | bytes 1179648 | tf_op jit(solution)/shard_map/add | solution.py:100
  36.6 1.4 %constant_dynamic-update-slice_fusion = (f32[4,512]{1,0:T(4,128)S(1)}, f32[2,512]{1,0:T(2,128)}) fusion(f32[4,512]{1,0:T(4,128)S(1)} %broadcast_in_dim.7, s32[]{:T(128)S(6)} %select_n.86, f32[2,512]{1,0:T(2,128)S(1)} %multiply_add_fusion.3, f32[196,512]{1,0:T(8,128)} %collective-permute-done.1), kind=kLoop, calls=%fused_computation.64 | loop fusion | flops 2048 | bytes 16388 | tf_op jit(solution)/shard_map/dynamic_update_slice | solution.py:55
  37.9 1.4 %fusion.18 = (f32[4,512]{1,0:T(4,128)S(1)}, f32[2,512]{1,0:T(2,128)}) fusion(f32[4,512]{1,0:T(4,128)S(1)} %get-tuple-element.46, s32[]{:T(128)S(6)} %select_n.85, f32[196,512]{1,0:T(8,128)} %collective-permute-done.1, f32[2,512]{1,0:T(2,128)S(1)} %get-tuple-element.60, f32[2,512]{1,0:T(2,128)S(1)} %copy-done.13, f32[2,512]{1,0:T(2,128)S(1)} %get-tuple-element.28, ...), kind=kLoop, calls=%fused_computation.53 | loop fusion | flops 7168 | bytes 32772 | tf_op jit(solution)/shard_map/dynamic_update_slice | solution.py:60
  39.3 2.0 %collective-permute-done.5 = f32[251,512]{1,0:T(8,128)S(1)} collective-permute-done((f32[251,512]{1,0:T(8,128)S(1)}, f32[251,512]{1,0:T(8,128)S(1)}, u32[]{:S(2)}, u32[]{:S(2)}) %collective-permute-start.5) | collective-permute-done | bytes 514080 | tf_op jit(solution)/shard_map/ppermute | solution.py:21
  41.4 1.2 %maximum_select_fusion = f32[502,512]{1,0:T(8,128)} fusion(f32[251,512]{1,0:T(8,128)S(1)} %get-tuple-element.33, f32[251,512]{1,0:T(8,128)S(1)} %collective-permute-done.5, f32[251,512]{1,0:T(8,128)S(1)} %get-tuple-element.34, pred[502]{0:T(512)(128)(4,1)S(1)} %fusion.26), kind=kLoop, calls=%fused_computation.11 | loop fusion | flops 1542144 | bytes 2570742 | tf_op jit(solution)/shard_map/jit(_where)/select_n | solution.py:178
  (56 shorter events, 1.5 us)
Async XLA Ops:
  0.6 9.3 %copy-start = (bf16[1,502,512]{2,1,0:T(8,128)(2,1)S(1)}, bf16[1,502,512]{2,1,0:T(8,128)(2,1)}, u32[]{:S(2)}) copy-start(bf16[1,502,512]{2,1,0:T(8,128)(2,1)} %param.19) | copy-start | bytes 1542148
  0.7 6.2 %copy-start.8 = (bf16[1,24,16,512]{3,2,1,0:T(8,128)(2,1)S(1)}, bf16[1,24,16,512]{3,2,1,0:T(8,128)(2,1)}, u32[]{:S(2)}) copy-start(bf16[1,24,16,512]{3,2,1,0:T(8,128)(2,1)} %param.13) | copy-start | bytes 1179652
  0.7 6.2 %copy-start.3 = (f32[12,16,512]{2,1,0:T(8,128)S(1)}, f32[12,16,512]{2,1,0:T(8,128)}, u32[]{:S(2)}) copy-start(f32[12,16,512]{2,1,0:T(8,128)} %param.12) | copy-start | bytes 1179652
  0.7 6.1 %copy-start.5 = (f32[12,16,512]{2,1,0:T(8,128)S(1)}, f32[12,16,512]{2,1,0:T(8,128)}, u32[]{:S(2)}) copy-start(f32[12,16,512]{2,1,0:T(8,128)} %param.11) | copy-start | bytes 1179652
  1.8 5.2 %copy-start.14 = (bf16[1,4,512]{2,1,0:T(4,128)(2,1)S(1)}, bf16[1,4,512]{2,1,0:T(4,128)(2,1)}, u32[]{:S(2)}) copy-start(bf16[1,4,512]{2,1,0:T(4,128)(2,1)} %param.16) | copy-start | bytes 12292
  1.8 5.2 %copy-start.12 = (f32[2,512]{1,0:T(2,128)S(1)}, f32[2,512]{1,0:T(2,128)}, u32[]{:S(2)}) copy-start(f32[2,512]{1,0:T(2,128)} %param.15) | copy-start | bytes 12292
  1.8 5.2 %copy-start.13 = (f32[2,512]{1,0:T(2,128)S(1)}, f32[2,512]{1,0:T(2,128)}, u32[]{:S(2)}) copy-start(f32[2,512]{1,0:T(2,128)} %param.14) | copy-start | bytes 12292
  1.8 31.4 %collective-permute-start = (f32[12,16,512]{2,1,0:T(8,128)S(1)}, f32[12,16,512]{2,1,0:T(8,128)}, u32[]{:S(2)}, u32[]{:S(2)}) collective-permute-start(f32[12,16,512]{2,1,0:T(8,128)S(1)} %bitcast_convert_fusion), channel_id=1, source_target_pairs={{0,128},{128,0},{1,129},{129,1},{2,130},{130,2},{3,131},{131,3},{4... | collective-permute-start | bytes 1179656 | tf_op jit(solution)/shard_map/ppermute | solution.py:21
  6.8 1.3 %copy-start.11 = (s32[2,8192]{1,0:T(2,128)S(1)}, s32[2,8192]{1,0:T(2,128)}, u32[]{:S(2)}) copy-start(s32[2,8192]{1,0:T(2,128)} %param.21) | copy-start | bytes 196612
  7.8 1.5 %copy-start.1 = (f32[1,1,251,512]{3,1,2,0:T(1,128)S(1)}, f32[1,1,251,512]{3,1,2,0:T(1,128)}, u32[]{:S(2)}) copy-start(f32[1,1,251,512]{3,1,2,0:T(1,128)} %param.17) | copy-start | bytes 1542148
  7.8 1.5 %copy-start.10 = (f32[1024,64]{0,1:T(8,128)S(1)}, f32[1024,64]{0,1:T(8,128)}, u32[]{:S(2)}) copy-start(f32[1024,64]{0,1:T(8,128)} %param.20) | copy-start | bytes 786436
  7.8 27.7 %collective-permute-start.1 = (f32[196,512]{1,0:T(8,128)}, f32[196,512]{1,0:T(8,128)}, u32[]{:S(2)}, u32[]{:S(2)}) collective-permute-start(f32[196,512]{1,0:T(8,128)} %pad_maximum_fusion), channel_id=1, source_target_pairs={{0,128},{128,0},{1,129},{129,1},{2,130},{130,2},{3,131},{131,3},{4... | collective-permute-start | bytes 1204232 | tf_op jit(solution)/shard_map/ppermute | solution.py:21
  9.1 1.6 %copy-start.2 = (f32[1,1,251,512]{3,1,2,0:T(1,128)S(1)}, f32[1,1,251,512]{3,1,2,0:T(1,128)}, u32[]{:S(2)}) copy-start(f32[1,1,251,512]{3,1,2,0:T(1,128)} %param.18) | copy-start | bytes 1542148
  10.6 1.3 %collective-permute-start.2 = (f32[251,64]{0,1:T(8,128)S(1)}, f32[251,64]{0,1:T(8,128)S(1)}, u32[]{:S(2)}, u32[]{:S(2)}) collective-permute-start(f32[251,64]{0,1:T(8,128)S(1)} %constant_dynamic-slice_fusion.2), channel_id=1, source_target_pairs={{0,1},{1,0},{2,3},{3,2},{4,5},{5,4},{6,7},{7,6},{8,9},{9,8},{10,11... | collective-permute-start | bytes 192776 | tf_op jit(solution)/shard_map/ppermute | solution.py:21
  12.7 11.9 %collective-permute-start.3 = (f32[251,64]{0,1:T(8,128)}, f32[251,64]{0,1:T(8,128)}, u32[]{:S(2)}, u32[]{:S(2)}) collective-permute-start(f32[251,64]{0,1:T(8,128)} %dynamic-slice_add_fusion), channel_id=1, source_target_pairs={{0,128},{128,0},{1,129},{129,1},{2,130},{130,2},{3,131},{131,3},{4... | collective-permute-start | bytes 192776 | tf_op jit(solution)/shard_map/ppermute | solution.py:21
  25.4 3.4 %collective-permute-start.4 = (f32[251,64]{0,1:T(8,128)S(1)}, f32[251,64]{0,1:T(8,128)S(1)}, u32[]{:S(2)}, u32[]{:S(2)}) collective-permute-start(f32[251,64]{0,1:T(8,128)S(1)} %add.109), channel_id=1, source_target_pairs={{0,1},{1,0},{2,3},{3,2},{4,5},{5,4},{6,7},{7,6},{8,9},{9,8},{10,11... | collective-permute-start | bytes 192776 | tf_op jit(solution)/shard_map/ppermute | solution.py:21
  25.6 15.8 %collective-permute-start.5 = (f32[251,512]{1,0:T(8,128)S(1)}, f32[251,512]{1,0:T(8,128)S(1)}, u32[]{:S(2)}, u32[]{:S(2)}) collective-permute-start(f32[251,512]{1,0:T(8,128)S(1)} %bitcast_subtract_fusion), channel_id=1, source_target_pairs={{0,128},{128,0},{1,129},{129,1},{2,130},{130,2},{3,131},{131,3},{4... | collective-permute-start | bytes 1542152 | tf_op jit(solution)/shard_map/ppermute | solution.py:21
  31.9 1.4 %copy-start.4 = (f32[12,16,512]{2,1,0:T(8,128)S(1)}, f32[12,16,512]{2,1,0:T(8,128)}, u32[]{:S(2)}) copy-start(f32[12,16,512]{2,1,0:T(8,128)} %param.12) | copy-start | bytes 1179652
  31.9 1.4 %copy-start.6 = (f32[12,16,512]{2,1,0:T(8,128)S(1)}, f32[12,16,512]{2,1,0:T(8,128)}, u32[]{:S(2)}) copy-start(f32[12,16,512]{2,1,0:T(8,128)} %param.11) | copy-start | bytes 1179652
  31.9 1.4 %copy-start.7 = (f32[12,16,512]{2,1,0:T(8,128)S(1)}, f32[12,16,512]{2,1,0:T(8,128)}, u32[]{:S(2)}) copy-start(f32[12,16,512]{2,1,0:T(8,128)} %dynamic-slice_convert_fusion) | copy-start | bytes 1179652
  36.6 6.1 %copy-start.9 = (f32[24,16,512]{2,1,0:T(8,128)}, f32[24,16,512]{2,1,0:T(8,128)S(1)}, u32[]{:S(2)}) copy-start(f32[24,16,512]{2,1,0:T(8,128)S(1)} %constant_dynamic-update-slice_fusion.1) | copy-start | bytes 2359300
  39.3 3.3 %copy-start.15 = (f32[4,512]{1,0:T(4,128)}, f32[4,512]{1,0:T(4,128)S(1)}, u32[]{:S(2)}) copy-start(f32[4,512]{1,0:T(4,128)S(1)} %get-tuple-element.51) | copy-start | bytes 24580

commit v7 on v5

--- a/solution.py
+++ b/solution.py
@@ -75,21 +75,26 @@
 ):
     rep_index = lax.axis_index("rep")
     first_is_own = rep_index == 0
-    width = attn_global.shape[-1]
+    own_rows = emb_global[0, 0]
+    own_momentum = emb_momentum[0, 0]
+    kept_rows = own_rows - DECAY * own_momentum
+    given_norm = outer_sends(norm_global, norm_inner[0], rep_index)
+    norm_parts = (given_norm,) + outer_partial(norm_global, norm_momentum, norm_inner[0], rep_index)
+    norm_parts = (norm_parts[1], norm_parts[0], norm_parts[2])
+    half_rows = kept_rows.shape[0]
+    norm_rows = given_norm.shape[0]
+    rows_sent = jnp.concatenate([kept_rows, given_norm, norm_parts[2]], axis=0)
+    kept_rows, rows_sent = lax.optimization_barrier((kept_rows, rows_sent))
+    rows_got = swap(rows_sent, "rep")
+    got_rows = rows_got[:half_rows]
+    norm_got = rows_got[half_rows:]
     given_attn = outer_sends(attn_global, attn_inner[0], rep_index)
     got_attn_inner = swap(given_attn, "rep")
-    given_norm = outer_sends(norm_global, norm_inner[0], rep_index)
     attn_parts = (given_attn,) + outer_partial(
         attn_global, attn_momentum, lax.optimization_barrier(attn_inner[0]), rep_index
     )
-    norm_parts = (given_norm,) + outer_partial(norm_global, norm_momentum, norm_inner[0], rep_index)
     attn_parts = (attn_parts[1], attn_parts[0], attn_parts[2])
-    norm_parts = (norm_parts[1], norm_parts[0], norm_parts[2])
-    attn_rows = attn_parts[2].size // width
-    norm_rows = given_norm.shape[0]
-    sent = jnp.concatenate([attn_parts[2].reshape(-1, width), given_norm, norm_parts[2]], axis=0)
-    sent = lax.optimization_barrier(sent)
-    got_buffer = swap(sent, "rep")
+    got_attn_partial = swap(attn_parts[2], "rep")
     new_attn_global, new_attn_momentum = outer_own(
         attn_global, attn_momentum, attn_parts[0], attn_parts[2], got_attn_inner
     )
@@ -97,9 +102,7 @@
     new_attn_global, new_attn_momentum, attn_placed = lax.optimization_barrier(
         (new_attn_global, new_attn_momentum, attn_placed)
     )
-    attn_other = got_buffer[:attn_rows] + SHARE * given_attn.reshape(-1, width)
-    attn_weights = place_other(attn_placed, attn_other.reshape(attn_global.shape), rep_index)
-    norm_got = got_buffer[attn_rows:]
+    attn_weights = place_other(attn_placed, got_attn_partial + SHARE * given_attn, rep_index)
     new_norm_global, new_norm_momentum = outer_own(
         norm_global, norm_momentum, norm_parts[0], norm_parts[2], norm_got[:norm_rows]
     )
@@ -108,7 +111,6 @@
     )
 
     block_rows = emb_inner.shape[1]
-    half_rows = emb_global.shape[2]
     half_width = emb_global.shape[3]
     row_start = lax.axis_index("fsdp") * block_rows
     half_start = rep_index * half_rows
@@ -130,8 +132,6 @@
     own_mask = lax.dynamic_index_in_dim(touched_masks, rep_index, 0, keepdims=False)
     half_counts = lax.dynamic_slice_in_dim(counts, half_start, half_rows, 0)
     basis_half = lax.dynamic_slice_in_dim(basis, lax.axis_index("tp") * half_width, half_width, 0)
-    own_rows = emb_global[0, 0]
-    own_momentum = emb_momentum[0, 0]
     global_coeff = jnp.dot(
         own_rows, basis_half, precision=lax.Precision.HIGHEST, preferred_element_type=jnp.float32
     )
@@ -150,11 +150,8 @@
     coeff_given = lax.dynamic_slice_in_dim(coeff_term, (1 - tp_index) * chip_rows, chip_rows, 0)
     coeff_kept = lax.dynamic_slice_in_dim(coeff_term, tp_index * chip_rows, chip_rows, 0)
     coeff_mine = coeff_kept + swap(coeff_given, "tp")
-    kept_rows = own_rows - DECAY * own_momentum
-    kept_rows, coeff_mine = lax.optimization_barrier((kept_rows, coeff_mine))
     coeff_half = coeff_mine + swap(coeff_mine, "rep")
     coeff_sum = place_pair(tp_index == 0, coeff_half, swap(coeff_half, "tp"))
-    got_rows = swap(kept_rows, "rep")
     emb_grad = (
         jnp.dot(
             coeff_sum,

time: 43.2 us -> 48.3 us (1.12)
  starting transfers between devices: 10.5 us -> 13.3 us
  waiting for transfers between devices: 7.73 us -> 9.46 us
    ppermute x6, starting transfers between devices: 10.5 us -> 13.3 us  [swap(): return lax.ppermute(x, axis, perm=SWAP)]
    ppermute x6, waiting for transfers between devices: 7.73 us -> 9.46 us  [swap(): return lax.ppermute(x, axis, perm=SWAP)]
    dynamic_update_slice x1 -> x2, other arithmetic: 1.4 us -> 2.46 us  [place_other(): lax.dynamic_update_slice_in_dim(placed, other, (1 - rep_index) * rows, 0)]
    select_n x2, other arithmetic: 1.05 us -> 2.09 us  [place_pair(): first = jnp.where(first_is_own, own, other)]
    add x1 -> x0, other arithmetic: 1.04 us -> none  [step_body(): attn_other = got_buffer[:attn_rows] + SHARE * given_attn.reshape(-1, width)]
    convert_element_type x1, other arithmetic: 0.79 us -> 1.71 us  [outer_partial(): lax.dynamic_slice_in_dim(inner_all, rep_index * owned, owned, 0)]
    and x1, other arithmetic: 0.91 us -> 0.07 us  [step_body(): inside = (offsets >= 0) & (offsets < block_rows)]
    select_n x1, other arithmetic: 1.07 us -> 0.23 us  [step_body(): offsets[:, None, :] // LOW]
  transfers between devices with their start and end apart: 6 -> 6, of which waited for: 2 -> 3; matrix products, arithmetic and copies ran while one was open for 48% -> 35% of each run, Pallas kernels for 0% -> 0%
where the time goes in v7:
time: 48.3 us; the launch traced here: 47.9 us
  other arithmetic  17.6 us (36%)
  starting transfers between devices  13.3 us (28%)
  waiting for transfers between devices  9.46 us (20%)
  local copies, waits for them, and re-layouts  3.6 us (7%)
  matrix products  2.97 us (6%)
  between operations  0.88 us (2%)
    ppermute x6, starting transfers between devices, swap(): return lax.ppermute(x, axis, perm=SWAP)  13.3 us
    ppermute x6, waiting for transfers between devices, swap(): return lax.ppermute(x, axis, perm=SWAP)  9.46 us
    dynamic_update_slice x2, other arithmetic, place_own(): return lax.dynamic_update_slice_in_dim(empty, own, rep_index * rows, 0)  3.53 us
    unnamed x31, local copies, waits for them, and re-layouts  2.63 us
    dynamic_update_slice x2, other arithmetic, place_other(): lax.dynamic_update_slice_in_dim(placed, other, (1 - rep_index) * rows, 0)  2.46 us
    select_n x2, other arithmetic, place_pair(): first = jnp.where(first_is_own, own, other)  2.09 us
    convert_element_type x1, other arithmetic, outer_partial(): lax.dynamic_slice_in_dim(inner_all, rep_index * owned, owned, 0)  1.71 us
    add x1, other arithmetic, step_body(): new_emb_momentum = MOMENTUM * emb_momentum + own_grad  1.49 us
  transfers between devices with their start and end apart: 6, of which 3 were waited for; matrix products, arithmetic and copies ran while one was open for 35% of the time, Pallas kernels for 0%

profile of v7, /device:TPU:1, one launch (start us, length us, event | category | flops | bytes accessed | tf_op | source)
XLA Modules:
  0.0 47.9 jit_solution(4966232119921983648)
XLA Ops:
  0.7 1.1 %bitcast_convert_fusion = f32[12,16,512]{2,1,0:T(8,128)S(1)} fusion(bf16[1,24,16,512]{3,2,1,0:T(8,128)(2,1)} %param.13, s32[]{:T(128)S(6)} %select_n.92), kind=kLoop, calls=%fused_computation.30 | loop fusion | flops 98304 | bytes 589828 | tf_op jit(solution)/shard_map/convert_element_type | solution.py:34
  1.8 3.8 %collective-permute-start = (f32[12,16,512]{2,1,0:T(8,128)S(1)}, f32[12,16,512]{2,1,0:T(8,128)}, u32[]{:S(2)}, u32[]{:S(2)}) collective-permute-start(f32[12,16,512]{2,1,0:T(8,128)S(1)} %bitcast_convert_fusion), channel_id=1, source_target_pairs={{0,128},{128,0},{1,129},{129,1},{2,130},{130,2},{3,131},{131,3},{4... | collective-permute-start | bytes 1179656 | tf_op jit(solution)/shard_map/ppermute | solution.py:21
  5.6 1.7 %dynamic-slice_convert_fusion = f32[12,16,512]{2,1,0:T(8,128)} fusion(bf16[24,16,512]{2,1,0:T(8,128)(2,1)} %bitcast.38, s32[]{:T(128)S(6)} %select_n.91), kind=kLoop, calls=%fused_computation.31 | loop fusion | flops 98304 | bytes 589828 | tf_op jit(solution)/shard_map/convert_element_type | solution.py:40
  7.3 0.9 %multiply_add_fusion.1 = f32[12,16,512]{2,1,0:T(8,128)} fusion(f32[12,16,512]{2,1,0:T(8,128)S(1)} %copy-done.3, f32[12,16,512]{2,1,0:T(8,128)S(1)} %copy-done.4, bf16[24,16,512]{2,1,0:T(8,128)(2,1)S(1)} %bitcast.39, s32[]{:T(128)S(6)} %select_n.91), kind=kLoop, calls=%fused_computation.27 | loop fusion | flops 589824 | bytes 1376260 | tf_op jit(solution)/shard_map/add | solution.py:41
  11.3 0.7 %constant_dynamic-slice_fusion.2 = f32[251,64]{0,1:T(8,128)} fusion(f32[502,64]{0,1:T(8,128)S(1)} %fusion.2, s32[]{:T(128)S(6)} %select_n.107), kind=kLoop, calls=%fused_computation.61 | loop fusion | bytes 128516 | tf_op jit(solution)/shard_map/dynamic_slice | solution.py:150
  12.0 3.0 %collective-permute-start.3 = (f32[251,64]{0,1:T(8,128)}, f32[251,64]{0,1:T(8,128)}, u32[]{:S(2)}, u32[]{:S(2)}) collective-permute-start(f32[251,64]{0,1:T(8,128)} %constant_dynamic-slice_fusion.2), channel_id=1, source_target_pairs={{0,1},{1,0},{2,3},{3,2},{4,5},{5,4},{6,7},{7,6},{8,9},{9,8},{10,11... | collective-permute-start | bytes 192776 | tf_op jit(solution)/shard_map/ppermute | solution.py:21
  15.1 1.1 %collective-permute-done.3 = f32[251,64]{0,1:T(8,128)} collective-permute-done((f32[251,64]{0,1:T(8,128)}, f32[251,64]{0,1:T(8,128)}, u32[]{:S(2)}, u32[]{:S(2)}) %collective-permute-start.3) | collective-permute-done | bytes 64288 | tf_op jit(solution)/shard_map/ppermute | solution.py:21
  16.2 1.0 %dynamic-slice_add_fusion = f32[251,64]{0,1:T(8,128)S(1)} fusion(f32[251,64]{0,1:T(8,128)} %collective-permute-done.3, f32[502,64]{0,1:T(8,128)} %copy-done.9, s32[]{:T(128)S(6)} %select_n.106), kind=kLoop, calls=%fused_computation.44 | loop fusion | flops 16064 | bytes 192772 | tf_op jit(solution)/shard_map/add | solution.py:152
  17.2 1.3 %collective-permute-start.4 = (f32[251,64]{0,1:T(8,128)S(1)}, f32[251,64]{0,1:T(8,128)S(1)}, u32[]{:S(2)}, u32[]{:S(2)}) collective-permute-start(f32[251,64]{0,1:T(8,128)S(1)} %dynamic-slice_add_fusion), channel_id=1, source_target_pairs={{0,128},{128,0},{1,129},{129,1},{2,130},{130,2},{3,131},{131,3},{4... | collective-permute-start | bytes 192776 | tf_op jit(solution)/shard_map/ppermute | solution.py:21
  18.5 4.7 %collective-permute-done.4 = f32[251,64]{0,1:T(8,128)S(1)} collective-permute-done((f32[251,64]{0,1:T(8,128)S(1)}, f32[251,64]{0,1:T(8,128)S(1)}, u32[]{:S(2)}, u32[]{:S(2)}) %collective-permute-start.4) | collective-permute-done | bytes 64288 | tf_op jit(solution)/shard_map/ppermute | solution.py:21
  23.9 2.3 %collective-permute-start.5 = (f32[251,64]{0,1:T(8,128)}, f32[251,64]{0,1:T(8,128)}, u32[]{:S(2)}, u32[]{:S(2)}) collective-permute-start(f32[251,64]{0,1:T(8,128)} %add.106), channel_id=1, source_target_pairs={{0,1},{1,0},{2,3},{3,2},{4,5},{5,4},{6,7},{7,6},{8,9},{9,8},{10,11... | collective-permute-start | bytes 192776 | tf_op jit(solution)/shard_map/ppermute | solution.py:21
  26.2 0.8 %pad_maximum_fusion.1 = f32[255,512]{1,0:T(8,128)} fusion(f32[2,512]{1,0:T(2,128)S(1)} %multiply_add_fusion.3, f32[2,512]{1,0:T(2,128)S(1)} %get-tuple-element.62, f32[251,512]{1,0:T(8,128)S(1)} %bitcast_subtract_fusion), kind=kLoop, calls=%fused_computation.13 | loop fusion | flops 261120 | bytes 1044480 | tf_op jit(solution)/shard_map/concatenate | solution.py:86
  27.0 3.0 %collective-permute-start.2 = (f32[255,512]{1,0:T(8,128)}, f32[255,512]{1,0:T(8,128)}, u32[]{:S(2)}, u32[]{:S(2)}) collective-permute-start(f32[255,512]{1,0:T(8,128)} %pad_maximum_fusion.1), channel_id=1, source_target_pairs={{0,128},{128,0},{1,129},{129,1},{2,130},{130,2},{3,131},{131,3},{4... | collective-permute-start | bytes 1566728 | tf_op jit(solution)/shard_map/ppermute | solution.py:21
  30.0 0.9 %broadcast_select_fusion.3 = (f32[251,64]{0,1:T(8,128)S(1)}, f32[251,64]{0,1:T(8,128)S(1)}) fusion(f32[251,64]{0,1:T(8,128)} %add.106, f32[251,64]{0,1:T(8,128)} %collective-permute-done.5, pred[]{:T(512)S(6)} %eq.34), kind=kLoop, calls=%fused_computation.50 | loop fusion | flops 32128 | bytes 257025 | tf_op jit(solution)/shard_map/jit(_where)/select_n | solution.py:25
  30.8 1.1 %convolution_multiply_fusion = f32[502,512]{1,0:T(8,128)S(1)} fusion(f32[251,64]{0,1:T(8,128)S(1)} %get-tuple-element.57, f32[251,64]{0,1:T(8,128)S(1)} %get-tuple-element.56, f32[1024,64]{0,1:T(8,128)S(1)} %copy-done.8, s32[]{:T(128)S(6)} %select_n.100), kind=kOutput, calls=%fused_computation.2 | convolution fusion | flops 197683584 | bytes 1290244 | tf_op jit(solution)/shard_map/dot_general | solution.py:156
  32.4 1.5 %reshape_add_fusion = f32[1,1,251,512]{3,1,2,0:T(1,128)} fusion(f32[251,512]{1,0:T(8,128)S(1)} %get-tuple-element.45, f32[1,1,251,512]{3,1,2,0:T(1,128)S(1)} %copy-done.2), kind=kLoop, calls=%fused_computation.21 | loop fusion | flops 257024 | bytes 1542144 | tf_op jit(solution)/shard_map/add | solution.py:167
  33.9 1.3 %copy.22 = f32[1,1,251,512]{3,1,2,0:T(1,128)} copy(f32[1,1,251,512]{3,2,1,0:T(8,128)S(1)} %bitcast_subtract_fusion.1) | data formatting | bytes 1028096
  35.3 2.2 %constant_dynamic-update-slice_fusion.1 = (f32[24,16,512]{2,1,0:T(8,128)S(1)}, f32[12,16,512]{2,1,0:T(8,128)}, f32[12,16,512]{2,1,0:T(8,128)}) fusion(f32[24,16,512]{2,1,0:T(8,128)S(1)} %broadcast_in_dim.6, s32[]{:T(128)S(6)} %select_n.91, f32[12,16,512]{2,1,0:T(8,128)} %multiply_add_fusion.1, f32[12,16,512]{2,1,0:T(8,128)} %collective-permute-done, ...), kind=kLoop, calls=%fused_computation.67 | loop fusion | flops 688128 | bytes 3145732 | tf_op jit(solution)/shard_map/dynamic_update_slice | solution.py:55
  37.5 1.1 %add_dynamic-update-slice_fusion = f32[24,16,512]{2,1,0:T(8,128)S(1)} fusion(f32[24,16,512]{2,1,0:T(8,128)S(1)} %get-tuple-element.26, s32[]{:T(128)S(6)} %select_n.92, f32[12,16,512]{2,1,0:T(8,128)} %collective-permute-done.1, f32[12,16,512]{2,1,0:T(8,128)S(1)} %bitcast_convert_fusion), kind=kLoop, calls=%fused_computation.24 | loop fusion | flops 196608 | bytes 1179652 | tf_op jit(solution)/shard_map/dynamic_update_slice | solution.py:60
  38.6 3.7 %collective-permute-done.2 = f32[255,512]{1,0:T(8,128)} collective-permute-done((f32[255,512]{1,0:T(8,128)}, f32[255,512]{1,0:T(8,128)}, u32[]{:S(2)}, u32[]{:S(2)}) %collective-permute-start.2) | collective-permute-done | bytes 522272 | tf_op jit(solution)/shard_map/ppermute | solution.py:21
  42.3 1.2 %broadcast_select_fusion.1 = (f32[251,512]{1,0:T(8,128)S(1)}, f32[251,512]{1,0:T(8,128)S(1)}) fusion(f32[251,512]{1,0:T(8,128)S(1)} %get-tuple-element.33, pred[]{:T(512)S(6)} %eq.35, f32[251,512]{1,0:T(8,128)S(1)} %get-tuple-element.34, f32[255,512]{1,0:T(8,128)} %collective-permute-done.2), kind=kLoop, calls=%fused_computation.29 | loop fusion | flops 514048 | bytes 2570241 | tf_op jit(solution)/shard_map/jit(_where)/select_n | solution.py:25
  43.5 1.1 %pad_maximum_fusion = f32[502,512]{1,0:T(8,128)} fusion(f32[251,512]{1,0:T(8,128)S(1)} %get-tuple-element.51, f32[251,512]{1,0:T(8,128)S(1)} %get-tuple-element.50), kind=kLoop, calls=%fused_computation.11 | loop fusion | flops 257024 | bytes 2056192 | tf_op jit(solution)/shard_map/concatenate | solution.py:27
  44.6 1.3 %constant_dynamic-update-slice_fusion = (f32[4,512]{1,0:T(4,128)S(1)}, f32[2,512]{1,0:T(2,128)}) fusion(f32[4,512]{1,0:T(4,128)S(1)} %broadcast_in_dim.7, s32[]{:T(128)S(6)} %select_n.93, f32[2,512]{1,0:T(2,128)S(1)} %multiply_add_fusion.3, f32[255,512]{1,0:T(8,128)} %collective-permute-done.2), kind=kLoop, calls=%fused_computation.64 | loop fusion | flops 2048 | bytes 16388 | tf_op jit(solution)/shard_map/dynamic_update_slice | solution.py:55
  45.9 1.4 %fusion.18 = (f32[4,512]{1,0:T(4,128)S(1)}, f32[2,512]{1,0:T(2,128)}) fusion(f32[4,512]{1,0:T(4,128)S(1)} %get-tuple-element.46, s32[]{:T(128)S(6)} %select_n.94, f32[255,512]{1,0:T(8,128)} %collective-permute-done.2, f32[2,512]{1,0:T(2,128)S(1)} %get-tuple-element.62, f32[2,512]{1,0:T(2,128)S(1)} %copy-done.12, f32[2,512]{1,0:T(2,128)S(1)} %get-tuple-element.29, ...), kind=kLoop, calls=%fused_computation.53 | loop fusion | flops 7168 | bytes 32772 | tf_op jit(solution)/shard_map/dynamic_update_slice | solution.py:60
  (52 shorter events, 4.9 us)
Async XLA Ops:
  0.6 9.4 %copy-start = (bf16[1,502,512]{2,1,0:T(8,128)(2,1)S(1)}, bf16[1,502,512]{2,1,0:T(8,128)(2,1)}, u32[]{:S(2)}) copy-start(bf16[1,502,512]{2,1,0:T(8,128)(2,1)} %param.19) | copy-start | bytes 1542148
  0.7 6.7 %copy-start.6 = (bf16[1,24,16,512]{3,2,1,0:T(8,128)(2,1)S(1)}, bf16[1,24,16,512]{3,2,1,0:T(8,128)(2,1)}, u32[]{:S(2)}) copy-start(bf16[1,24,16,512]{3,2,1,0:T(8,128)(2,1)} %param.13) | copy-start | bytes 1179652
  0.7 6.7 %copy-start.3 = (f32[12,16,512]{2,1,0:T(8,128)S(1)}, f32[12,16,512]{2,1,0:T(8,128)}, u32[]{:S(2)}) copy-start(f32[12,16,512]{2,1,0:T(8,128)} %param.12) | copy-start | bytes 1179652
  0.7 6.7 %copy-start.4 = (f32[12,16,512]{2,1,0:T(8,128)S(1)}, f32[12,16,512]{2,1,0:T(8,128)}, u32[]{:S(2)}) copy-start(f32[12,16,512]{2,1,0:T(8,128)} %param.11) | copy-start | bytes 1179652
  1.8 6.4 %copy-start.10 = (s32[2,8192]{1,0:T(2,128)S(1)}, s32[2,8192]{1,0:T(2,128)}, u32[]{:S(2)}) copy-start(s32[2,8192]{1,0:T(2,128)} %param.21) | copy-start | bytes 196612
  1.8 33.4 %collective-permute-start = (f32[12,16,512]{2,1,0:T(8,128)S(1)}, f32[12,16,512]{2,1,0:T(8,128)}, u32[]{:S(2)}, u32[]{:S(2)}) collective-permute-start(f32[12,16,512]{2,1,0:T(8,128)S(1)} %bitcast_convert_fusion), channel_id=1, source_target_pairs={{0,128},{128,0},{1,129},{129,1},{2,130},{130,2},{3,131},{131,3},{4... | collective-permute-start | bytes 1179656 | tf_op jit(solution)/shard_map/ppermute | solution.py:21
  8.2 1.2 %copy-start.1 = (f32[1,1,251,512]{3,1,2,0:T(1,128)S(1)}, f32[1,1,251,512]{3,1,2,0:T(1,128)}, u32[]{:S(2)}) copy-start(f32[1,1,251,512]{3,1,2,0:T(1,128)} %param.17) | copy-start | bytes 1542148
  8.2 1.2 %copy-start.8 = (f32[1024,64]{0,1:T(8,128)S(1)}, f32[1024,64]{0,1:T(8,128)}, u32[]{:S(2)}) copy-start(f32[1024,64]{0,1:T(8,128)} %param.20) | copy-start | bytes 786436
  8.2 29.3 %collective-permute-start.1 = (f32[12,16,512]{2,1,0:T(8,128)}, f32[12,16,512]{2,1,0:T(8,128)}, u32[]{:S(2)}, u32[]{:S(2)}) collective-permute-start(f32[12,16,512]{2,1,0:T(8,128)} %multiply_add_fusion.1), channel_id=1, source_target_pairs={{0,128},{128,0},{1,129},{129,1},{2,130},{130,2},{3,131},{131,3},{4... | collective-permute-start | bytes 1179656 | tf_op jit(solution)/shard_map/ppermute | solution.py:21
  9.2 5.8 %copy-start.2 = (f32[1,1,251,512]{3,1,2,0:T(1,128)S(1)}, f32[1,1,251,512]{3,1,2,0:T(1,128)}, u32[]{:S(2)}) copy-start(f32[1,1,251,512]{3,1,2,0:T(1,128)} %param.18) | copy-start | bytes 1542148
  10.6 0.7 %copy-start.9 = (f32[502,64]{0,1:T(8,128)}, f32[502,64]{0,1:T(8,128)S(1)}, u32[]{:S(2)}) copy-start(f32[502,64]{0,1:T(8,128)S(1)} %fusion.2) | copy-start | bytes 385540
  11.3 3.8 %copy-start.11 = (f32[2,512]{1,0:T(2,128)S(1)}, f32[2,512]{1,0:T(2,128)}, u32[]{:S(2)}) copy-start(f32[2,512]{1,0:T(2,128)} %param.15) | copy-start | bytes 12292
  11.3 3.8 %copy-start.12 = (f32[2,512]{1,0:T(2,128)S(1)}, f32[2,512]{1,0:T(2,128)}, u32[]{:S(2)}) copy-start(f32[2,512]{1,0:T(2,128)} %param.14) | copy-start | bytes 12292
  11.3 3.8 %copy-start.13 = (bf16[1,4,512]{2,1,0:T(4,128)(2,1)S(1)}, bf16[1,4,512]{2,1,0:T(4,128)(2,1)}, u32[]{:S(2)}) copy-start(bf16[1,4,512]{2,1,0:T(4,128)(2,1)} %param.16) | copy-start | bytes 12292
  12.0 4.2 %collective-permute-start.3 = (f32[251,64]{0,1:T(8,128)}, f32[251,64]{0,1:T(8,128)}, u32[]{:S(2)}, u32[]{:S(2)}) collective-permute-start(f32[251,64]{0,1:T(8,128)} %constant_dynamic-slice_fusion.2), channel_id=1, source_target_pairs={{0,1},{1,0},{2,3},{3,2},{4,5},{5,4},{6,7},{7,6},{8,9},{9,8},{10,11... | collective-permute-start | bytes 192776 | tf_op jit(solution)/shard_map/ppermute | solution.py:21
  17.2 6.0 %collective-permute-start.4 = (f32[251,64]{0,1:T(8,128)S(1)}, f32[251,64]{0,1:T(8,128)S(1)}, u32[]{:S(2)}, u32[]{:S(2)}) collective-permute-start(f32[251,64]{0,1:T(8,128)S(1)} %dynamic-slice_add_fusion), channel_id=1, source_target_pairs={{0,128},{128,0},{1,129},{129,1},{2,130},{130,2},{3,131},{131,3},{4... | collective-permute-start | bytes 192776 | tf_op jit(solution)/shard_map/ppermute | solution.py:21
  23.9 6.1 %collective-permute-start.5 = (f32[251,64]{0,1:T(8,128)}, f32[251,64]{0,1:T(8,128)}, u32[]{:S(2)}, u32[]{:S(2)}) collective-permute-start(f32[251,64]{0,1:T(8,128)} %add.106), channel_id=1, source_target_pairs={{0,1},{1,0},{2,3},{3,2},{4,5},{5,4},{6,7},{7,6},{8,9},{9,8},{10,11... | collective-permute-start | bytes 192776 | tf_op jit(solution)/shard_map/ppermute | solution.py:21
  27.0 15.3 %collective-permute-start.2 = (f32[255,512]{1,0:T(8,128)}, f32[255,512]{1,0:T(8,128)}, u32[]{:S(2)}, u32[]{:S(2)}) collective-permute-start(f32[255,512]{1,0:T(8,128)} %pad_maximum_fusion.1), channel_id=1, source_target_pairs={{0,128},{128,0},{1,129},{129,1},{2,130},{130,2},{3,131},{131,3},{4... | collective-permute-start | bytes 1566728 | tf_op jit(solution)/shard_map/ppermute | solution.py:21
  33.9 1.4 %copy-start.5 = (f32[12,16,512]{2,1,0:T(8,128)S(1)}, f32[12,16,512]{2,1,0:T(8,128)}, u32[]{:S(2)}) copy-start(f32[12,16,512]{2,1,0:T(8,128)} %dynamic-slice_convert_fusion) | copy-start | bytes 1179652
  38.6 4.9 %copy-start.7 = (f32[24,16,512]{2,1,0:T(8,128)}, f32[24,16,512]{2,1,0:T(8,128)S(1)}, u32[]{:S(2)}) copy-start(f32[24,16,512]{2,1,0:T(8,128)S(1)} %add_dynamic-update-slice_fusion) | copy-start | bytes 2359300
  47.3 0.6 %copy-start.14 = (f32[4,512]{1,0:T(4,128)}, f32[4,512]{1,0:T(4,128)S(1)}, u32[]{:S(2)}) copy-start(f32[4,512]{1,0:T(4,128)S(1)} %get-tuple-element.53) | copy-start | bytes 24580

commit v8 on v5

--- a/solution.py
+++ b/solution.py
@@ -154,7 +154,12 @@
     kept_rows, coeff_mine = lax.optimization_barrier((kept_rows, coeff_mine))
     coeff_half = coeff_mine + swap(coeff_mine, "rep")
     coeff_sum = place_pair(tp_index == 0, coeff_half, swap(coeff_half, "tp"))
-    got_rows = swap(kept_rows, "rep")
+    lead = half_rows % 8
+    pad_rows = lead + half_rows + (-(lead + half_rows)) % 8
+    shifted = jnp.pad(kept_rows, ((lead, pad_rows - lead - half_rows), (0, 0)))
+    plain = jnp.pad(kept_rows, ((0, pad_rows - half_rows), (0, 0)))
+    rows_sent = jnp.where(rep_index == 1, shifted, plain)
+    got_rows = swap(rows_sent, "rep")
     emb_grad = (
         jnp.dot(
             coeff_sum,
@@ -170,10 +175,24 @@
     new_emb_momentum = MOMENTUM * emb_momentum + own_grad
     own_flat = kept_rows - STEP * lax.dynamic_slice_in_dim(emb_grad, half_start, half_rows, 0)
     other_grad = lax.dynamic_slice_in_dim(emb_grad, (1 - rep_index) * half_rows, half_rows, 0)
-    new_emb_global, new_emb_momentum, own_flat, other_grad = lax.optimization_barrier(
-        (new_emb_global, new_emb_momentum, own_flat, other_grad)
-    )
-    emb_weights = place_pair(first_is_own, own_flat, got_rows - STEP * other_grad)
+    own_full = place_pair(first_is_own, own_flat, jnp.zeros_like(own_flat))
+    new_emb_global, new_emb_momentum, own_full = lax.optimization_barrier(
+        (new_emb_global, new_emb_momentum, own_full)
+    )
+    aligned_start = half_rows - lead
+    other_full = jnp.where(
+        first_is_own,
+        jnp.concatenate(
+            [jnp.zeros((aligned_start, half_width), jnp.float32), got_rows[: block_rows - aligned_start]],
+            axis=0,
+        ),
+        jnp.concatenate(
+            [got_rows, jnp.zeros((block_rows - pad_rows, half_width), jnp.float32)], axis=0
+        ),
+    )
+    row_ids = lax.broadcasted_iota(jnp.int32, (block_rows, half_width), 0)
+    in_own_half = (row_ids >= half_start) & (row_ids < half_start + half_rows)
+    emb_weights = jnp.where(in_own_half, own_full, other_full - STEP * emb_grad)
     return (
         new_attn_global,
         new_attn_momentum,

time: 43.2 us -> 49 us (1.13)
  waiting for transfers between devices: 7.73 us -> 18.2 us
  other arithmetic: 17.3 us -> 14.2 us
  local copies, waits for them, and re-layouts: 3.15 us -> 2.44 us
  starting transfers between devices: 10.5 us -> 9.8 us
    ppermute x6, waiting for transfers between devices: 7.73 us -> 18.2 us  [swap(): return lax.ppermute(x, axis, perm=SWAP)]
    select_n x0 -> x3, other arithmetic: none -> 1.35 us  [the longest x1 1.18 us: step_body(): emb_weights = jnp.where(in_own_half, own_full, other_full - STEP * emb_grad)]
    convert_element_type x2, other arithmetic: 1.07 us -> 0.05 us  [outer_sends(): given_inner = lax.dynamic_slice_in_dim(inner_all, (1 - rep_index) * owned...]
    concatenate x1, other arithmetic: 1.06 us -> 0.1 us  [place_pair(): return jnp.concatenate([first, second], axis=0)]
    add x2, other arithmetic: 1.04 us -> 0.12 us  [outer_partial(): partial = KEEP * global_part - DECAY * momentum_part + SHARE * own_inner]
    select_n x2, other arithmetic: 1.05 us -> 0.16 us  [place_pair(): first = jnp.where(first_is_own, own, other)]
    ppermute x6, starting transfers between devices: 10.5 us -> 9.8 us  [swap(): return lax.ppermute(x, axis, perm=SWAP)]
    unnamed x35, local copies, waits for them, and re-layouts: 2.13 us -> 1.41 us
  transfers between devices with their start and end apart: 6 -> 6, of which waited for: 2 -> 2; matrix products, arithmetic and copies ran while one was open for 48% -> 28% of each run, Pallas kernels for 0% -> 0%
where the time goes in v8:
time: 49 us; the launch traced here: 48.6 us
  waiting for transfers between devices  18.2 us (37%)
  other arithmetic  14.2 us (29%)
  starting transfers between devices  9.8 us (20%)
  matrix products  2.97 us (6%)
  local copies, waits for them, and re-layouts  2.44 us (5%)
  between operations  1.02 us (2%)
    ppermute x6, waiting for transfers between devices, swap(): return lax.ppermute(x, axis, perm=SWAP)  18.2 us
    ppermute x6, starting transfers between devices, swap(): return lax.ppermute(x, axis, perm=SWAP)  9.8 us
    dynamic_update_slice x2, other arithmetic, place_own(): return lax.dynamic_update_slice_in_dim(empty, own, rep_index * rows, 0)  3.46 us
    add x1, other arithmetic, step_body(): new_emb_momentum = MOMENTUM * emb_momentum + own_grad  1.49 us
    unnamed x35, local copies, waits for them, and re-layouts  1.41 us
    dynamic_update_slice x1, other arithmetic, place_other(): lax.dynamic_update_slice_in_dim(placed, other, (1 - rep_index) * rows, 0)  1.4 us
    select_n x1, other arithmetic, step_body(): emb_weights = jnp.where(in_own_half, own_full, other_full - STEP * emb_grad)  1.18 us
    select_n x1, other arithmetic, step_body(): offsets[:, None, :] // LOW  1.17 us
  transfers between devices with their start and end apart: 6, of which 2 were waited for; matrix products, arithmetic and copies ran while one was open for 28% of the time, Pallas kernels for 0%

profile of v8, /device:TPU:1, one launch (start us, length us, event | category | flops | bytes accessed | tf_op | source)
XLA Modules:
  0.0 48.6 jit_solution(13832561009917963402)
XLA Ops:
  0.7 1.2 %and_select_fusion.1 = (s32[2,8192]{1,0:T(2,128)S(1)}, s32[2,8192]{1,0:T(2,128)S(1)}) fusion(s32[2,8192]{1,0:T(2,128)} %param.21, s32[]{:T(128)S(6)} %mul.171), kind=kLoop, calls=%fused_computation.39 | loop fusion | flops 327680 | bytes 196612 | tf_op jit(solution)/shard_map/jit(floor_divide)/jit(_where)/select_n | solution.py:119
  1.9 0.9 %compare_and_fusion = pred[2,8192]{1,0:T(4,128)(4,1)S(1)} fusion(s32[2,8192]{1,0:T(2,128)} %param.21, s32[]{:T(128)S(6)} %mul.171), kind=kLoop, calls=%fused_computation.38 | loop fusion | flops 65536 | bytes 81924 | tf_op jit(solution)/shard_map/and | solution.py:116
  2.8 0.6 %fusion.3 = pred[2,16,32]{2,1,0:T(8,128)(4,1)S(1)} fusion(s32[2,8192]{1,0:T(2,128)S(1)} %get-tuple-element.56, s32[2,8192]{1,0:T(2,128)S(1)} %get-tuple-element.55, pred[2,8192]{1,0:T(4,128)(4,1)S(1)} %compare_and_fusion), kind=kOutput, calls=%fused_computation.7 | convolution fusion | flops 17826816 | bytes 148480 | tf_op jit(solution)/shard_map/gik,gjk->gij/dot_general | solution.py:122
  3.6 0.6 %select_bitcast_fusion.1 = (f32[251,64]{0,1:T(8,128)S(1)}, f32[251,64]{0,1:T(8,128)S(1)}) fusion(pred[]{:T(512)S(6)} %eq.38, f32[1,1,251,512]{3,1,2,0:T(1,128)S(1)} %copy-done.1, f32[1024,64]{0,1:T(8,128)S(1)} %copy-done.10, s32[]{:T(128)S(6)} %select_n.117, f32[251]{0:T(256)S(1)} %dynamic_slice.36), kind=kOutput, calls=%fused_computation.48 | convolution fusion | flops 98745408 | bytes 774661 | tf_op jit(solution)/shard_map/dot_general | solution.py:135
  4.9 0.7 %constant_dynamic-slice_fusion.1 = f32[251,64]{0,1:T(8,128)} fusion(f32[502,64]{0,1:T(8,128)S(1)} %fusion.2, s32[]{:T(128)S(6)} %select_n.124), kind=kLoop, calls=%fused_computation.62 | loop fusion | bytes 128516 | tf_op jit(solution)/shard_map/dynamic_slice | solution.py:150
  5.6 3.2 %collective-permute-start.2 = (f32[251,64]{0,1:T(8,128)}, f32[251,64]{0,1:T(8,128)}, u32[]{:S(2)}, u32[]{:S(2)}) collective-permute-start(f32[251,64]{0,1:T(8,128)} %constant_dynamic-slice_fusion.1), channel_id=1, source_target_pairs={{0,1},{1,0},{2,3},{3,2},{4,5},{5,4},{6,7},{7,6},{8,9},{9,8},{10,11... | collective-permute-start | bytes 192776 | tf_op jit(solution)/shard_map/ppermute | solution.py:21
  8.9 1.3 %collective-permute-start = (f32[12,16,512]{2,1,0:T(8,128)S(1)}, f32[12,16,512]{2,1,0:T(8,128)}, u32[]{:S(2)}, u32[]{:S(2)}) collective-permute-start(f32[12,16,512]{2,1,0:T(8,128)S(1)} %bitcast_convert_fusion), channel_id=1, source_target_pairs={{0,128},{128,0},{1,129},{129,1},{2,130},{130,2},{3,131},{131,3},{4... | collective-permute-start | bytes 1179656 | tf_op jit(solution)/shard_map/ppermute | solution.py:21
  10.2 0.8 %dynamic-slice_convert_fusion = f32[12,16,512]{2,1,0:T(8,128)} fusion(bf16[24,16,512]{2,1,0:T(8,128)(2,1)S(1)} %bitcast.46, s32[]{:T(128)S(6)} %select_n.108), kind=kLoop, calls=%fused_computation.33 | loop fusion | flops 98304 | bytes 589828 | tf_op jit(solution)/shard_map/convert_element_type | solution.py:40
  11.2 0.8 %pad_maximum_fusion.1 = f32[196,512]{1,0:T(8,128)} fusion(f32[2,512]{1,0:T(2,128)S(1)} %multiply_add_fusion.3, f32[2,512]{1,0:T(2,128)S(1)} %get-tuple-element.57, f32[192,512]{1,0:T(8,128)S(1)} %bitcast.43), kind=kLoop, calls=%fused_computation.24 | loop fusion | flops 200704 | bytes 802816 | tf_op jit(solution)/shard_map/concatenate | solution.py:90
  12.0 1.8 %collective-permute-start.1 = (f32[196,512]{1,0:T(8,128)}, f32[196,512]{1,0:T(8,128)}, u32[]{:S(2)}, u32[]{:S(2)}) collective-permute-start(f32[196,512]{1,0:T(8,128)} %pad_maximum_fusion.1), channel_id=1, source_target_pairs={{0,128},{128,0},{1,129},{129,1},{2,130},{130,2},{3,131},{131,3},{4... | collective-permute-start | bytes 1204232 | tf_op jit(solution)/shard_map/ppermute | solution.py:21
  13.9 1.0 %dynamic-slice_add_fusion = f32[251,64]{0,1:T(8,128)S(1)} fusion(f32[251,64]{0,1:T(8,128)} %collective-permute-done.2, f32[502,64]{0,1:T(8,128)} %copy-done.12, s32[]{:T(128)S(6)} %select_n.123), kind=kLoop, calls=%fused_computation.46 | loop fusion | flops 16064 | bytes 192772 | tf_op jit(solution)/shard_map/add | solution.py:152
  15.0 1.3 %collective-permute-start.3 = (f32[251,64]{0,1:T(8,128)S(1)}, f32[251,64]{0,1:T(8,128)S(1)}, u32[]{:S(2)}, u32[]{:S(2)}) collective-permute-start(f32[251,64]{0,1:T(8,128)S(1)} %dynamic-slice_add_fusion), channel_id=1, source_target_pairs={{0,128},{128,0},{1,129},{129,1},{2,130},{130,2},{3,131},{131,3},{4... | collective-permute-start | bytes 192776 | tf_op jit(solution)/shard_map/ppermute | solution.py:21
  16.3 15.1 %collective-permute-done.3 = f32[251,64]{0,1:T(8,128)S(1)} collective-permute-done((f32[251,64]{0,1:T(8,128)S(1)}, f32[251,64]{0,1:T(8,128)S(1)}, u32[]{:S(2)}, u32[]{:S(2)}) %collective-permute-start.3) | collective-permute-done | bytes 64288 | tf_op jit(solution)/shard_map/ppermute | solution.py:21
  31.3 1.0 %collective-permute-start.4 = (f32[251,64]{0,1:T(8,128)S(1)}, f32[251,64]{0,1:T(8,128)S(1)}, u32[]{:S(2)}, u32[]{:S(2)}) collective-permute-start(f32[251,64]{0,1:T(8,128)S(1)} %add.114), channel_id=1, source_target_pairs={{0,1},{1,0},{2,3},{3,2},{4,5},{5,4},{6,7},{7,6},{8,9},{9,8},{10,11... | collective-permute-start | bytes 192776 | tf_op jit(solution)/shard_map/ppermute | solution.py:21
  32.4 1.3 %collective-permute-start.5 = (f32[256,512]{1,0:T(8,128)S(1)}, f32[256,512]{1,0:T(8,128)S(1)}, u32[]{:S(2)}, u32[]{:S(2)}) collective-permute-start(f32[256,512]{1,0:T(8,128)S(1)} %pad_select_fusion), channel_id=1, source_target_pairs={{0,128},{128,0},{1,129},{129,1},{2,130},{130,2},{3,131},{131,3},{4... | collective-permute-start | bytes 1572872 | tf_op jit(solution)/shard_map/ppermute | solution.py:21
  33.7 1.1 %convolution_multiply_fusion = f32[502,512]{1,0:T(8,128)S(1)} fusion(f32[251,64]{0,1:T(8,128)S(1)} %get-tuple-element.52, f32[251,64]{0,1:T(8,128)S(1)} %get-tuple-element.51, f32[1024,64]{0,1:T(8,128)S(1)} %copy-done.11, s32[]{:T(128)S(6)} %select_n.117), kind=kOutput, calls=%fused_computation.2 | convolution fusion | flops 197683584 | bytes 1290244 | tf_op jit(solution)/shard_map/dot_general | solution.py:164
  35.3 1.5 %reshape_add_fusion = f32[1,1,251,512]{3,1,2,0:T(1,128)} fusion(f32[251,512]{1,0:T(8,128)S(1)} %get-tuple-element.43, f32[1,1,251,512]{3,1,2,0:T(1,128)S(1)} %copy-done.2), kind=kLoop, calls=%fused_computation.21 | loop fusion | flops 257024 | bytes 1542144 | tf_op jit(solution)/shard_map/add | solution.py:175
  36.9 1.3 %copy.22 = f32[1,1,251,512]{3,1,2,0:T(1,128)} copy(f32[1,1,251,512]{3,2,1,0:T(8,128)S(1)} %bitcast_subtract_fusion.1) | data formatting | bytes 1028096
  38.4 2.1 %constant_dynamic-update-slice_fusion.2 = (f32[24,16,512]{2,1,0:T(8,128)S(1)}, f32[12,16,512]{2,1,0:T(8,128)}, f32[12,16,512]{2,1,0:T(8,128)}) fusion(f32[24,16,512]{2,1,0:T(8,128)S(1)} %broadcast_in_dim.8, s32[]{:T(128)S(6)} %select_n.108, f32[12,16,512]{2,1,0:T(8,128)S(1)} %multiply_add_fusion.1, f32[12,16,512]{2,1,0:T(8,128)} %collective-permute-done, ...), kind=kLoop, calls=%fused_computation.69 | loop fusion | flops 688128 | bytes 3145732 | tf_op jit(solution)/shard_map/dynamic_update_slice | solution.py:55
  40.5 1.0 %slice_add_fusion = f32[192,512]{1,0:T(8,128)S(1)} fusion(f32[196,512]{1,0:T(8,128)} %collective-permute-done.1, f32[12,16,512]{2,1,0:T(8,128)S(1)} %broadcast_multiply_fusion), kind=kLoop, calls=%fused_computation.25 | loop fusion | flops 98304 | bytes 1179648 | tf_op jit(solution)/shard_map/add | solution.py:100
  41.6 1.4 %constant_dynamic-update-slice_fusion = (f32[4,512]{1,0:T(4,128)S(1)}, f32[2,512]{1,0:T(2,128)}) fusion(f32[4,512]{1,0:T(4,128)S(1)} %broadcast_in_dim.9, s32[]{:T(128)S(6)} %select_n.111, f32[2,512]{1,0:T(2,128)S(1)} %multiply_add_fusion.3, f32[196,512]{1,0:T(8,128)} %collective-permute-done.1), kind=kLoop, calls=%fused_computation.65 | loop fusion | flops 2048 | bytes 16388 | tf_op jit(solution)/shard_map/dynamic_update_slice | solution.py:55
  42.9 1.4 %fusion.18 = (f32[4,512]{1,0:T(4,128)S(1)}, f32[2,512]{1,0:T(2,128)}) fusion(f32[4,512]{1,0:T(4,128)S(1)} %get-tuple-element.44, s32[]{:T(128)S(6)} %select_n.110, f32[196,512]{1,0:T(8,128)} %collective-permute-done.1, f32[2,512]{1,0:T(2,128)S(1)} %get-tuple-element.57, f32[2,512]{1,0:T(2,128)S(1)} %copy-done.14, f32[2,512]{1,0:T(2,128)S(1)} %get-tuple-element.27, ...), kind=kLoop, calls=%fused_computation.55 | loop fusion | flops 7168 | bytes 32772 | tf_op jit(solution)/shard_map/dynamic_update_slice | solution.py:60
  44.3 3.1 %collective-permute-done.5 = f32[256,512]{1,0:T(8,128)S(1)} collective-permute-done((f32[256,512]{1,0:T(8,128)S(1)}, f32[256,512]{1,0:T(8,128)S(1)}, u32[]{:S(2)}, u32[]{:S(2)}) %collective-permute-start.5) | collective-permute-done | bytes 524320 | tf_op jit(solution)/shard_map/ppermute | solution.py:21
  47.4 1.2 %subtract_select_fusion = f32[502,512]{1,0:T(8,128)} fusion(f32[502,512]{1,0:T(8,128)S(1)} %pad_maximum_fusion, f32[502,512]{1,0:T(8,128)S(1)} %convolution_multiply_fusion, f32[256,512]{1,0:T(8,128)S(1)} %collective-permute-done.5, f32[254,512]{1,0:T(8,128)S(1)} %bitcast.44, pred[502]{0:T(512)(128)(4,1)S(1)} %fusion.26, pred[]{:T(512)S(6)} %eq.38), kind=kLoop, calls=%fused_computation.12 | loop fusion | flops 1028096 | bytes 4129271 | tf_op jit(solution)/shard_map/jit(_where)/select_n | solution.py:195
  (61 shorter events, 2.0 us)
Async XLA Ops:
  0.6 3.6 %copy-start = (bf16[1,502,512]{2,1,0:T(8,128)(2,1)S(1)}, bf16[1,502,512]{2,1,0:T(8,128)(2,1)}, u32[]{:S(2)}) copy-start(bf16[1,502,512]{2,1,0:T(8,128)(2,1)} %param.19) | copy-start | bytes 1542148
  0.7 3.0 %copy-start.1 = (f32[1,1,251,512]{3,1,2,0:T(1,128)S(1)}, f32[1,1,251,512]{3,1,2,0:T(1,128)}, u32[]{:S(2)}) copy-start(f32[1,1,251,512]{3,1,2,0:T(1,128)} %param.17) | copy-start | bytes 1542148
  0.7 3.0 %copy-start.10 = (f32[1024,64]{0,1:T(8,128)S(1)}, f32[1024,64]{0,1:T(8,128)}, u32[]{:S(2)}) copy-start(f32[1024,64]{0,1:T(8,128)} %param.20) | copy-start | bytes 786436
  3.4 5.4 %copy-start.8 = (bf16[1,24,16,512]{3,2,1,0:T(8,128)(2,1)S(1)}, bf16[1,24,16,512]{3,2,1,0:T(8,128)(2,1)}, u32[]{:S(2)}) copy-start(bf16[1,24,16,512]{3,2,1,0:T(8,128)(2,1)} %param.13) | copy-start | bytes 1179652
  4.3 6.7 %copy-start.3 = (f32[12,16,512]{2,1,0:T(8,128)S(1)}, f32[12,16,512]{2,1,0:T(8,128)}, u32[]{:S(2)}) copy-start(f32[12,16,512]{2,1,0:T(8,128)} %param.12) | copy-start | bytes 1179652
  4.3 6.7 %copy-start.5 = (f32[12,16,512]{2,1,0:T(8,128)S(1)}, f32[12,16,512]{2,1,0:T(8,128)}, u32[]{:S(2)}) copy-start(f32[12,16,512]{2,1,0:T(8,128)} %param.11) | copy-start | bytes 1179652
  4.9 3.9 %copy-start.12 = (f32[502,64]{0,1:T(8,128)}, f32[502,64]{0,1:T(8,128)S(1)}, u32[]{:S(2)}) copy-start(f32[502,64]{0,1:T(8,128)S(1)} %fusion.2) | copy-start | bytes 385540
  5.6 8.3 %collective-permute-start.2 = (f32[251,64]{0,1:T(8,128)}, f32[251,64]{0,1:T(8,128)}, u32[]{:S(2)}, u32[]{:S(2)}) collective-permute-start(f32[251,64]{0,1:T(8,128)} %constant_dynamic-slice_fusion.1), channel_id=1, source_target_pairs={{0,1},{1,0},{2,3},{3,2},{4,5},{5,4},{6,7},{7,6},{8,9},{9,8},{10,11... | collective-permute-start | bytes 192776 | tf_op jit(solution)/shard_map/ppermute | solution.py:21
  8.9 2.2 %copy-start.15 = (bf16[1,4,512]{2,1,0:T(4,128)(2,1)S(1)}, bf16[1,4,512]{2,1,0:T(4,128)(2,1)}, u32[]{:S(2)}) copy-start(bf16[1,4,512]{2,1,0:T(4,128)(2,1)} %param.16) | copy-start | bytes 12292
  8.9 2.3 %copy-start.13 = (f32[2,512]{1,0:T(2,128)S(1)}, f32[2,512]{1,0:T(2,128)}, u32[]{:S(2)}) copy-start(f32[2,512]{1,0:T(2,128)} %param.15) | copy-start | bytes 12292
  8.9 2.3 %copy-start.14 = (f32[2,512]{1,0:T(2,128)S(1)}, f32[2,512]{1,0:T(2,128)}, u32[]{:S(2)}) copy-start(f32[2,512]{1,0:T(2,128)} %param.14) | copy-start | bytes 12292
  8.9 29.4 %collective-permute-start = (f32[12,16,512]{2,1,0:T(8,128)S(1)}, f32[12,16,512]{2,1,0:T(8,128)}, u32[]{:S(2)}, u32[]{:S(2)}) collective-permute-start(f32[12,16,512]{2,1,0:T(8,128)S(1)} %bitcast_convert_fusion), channel_id=1, source_target_pairs={{0,128},{128,0},{1,129},{129,1},{2,130},{130,2},{3,131},{131,3},{4... | collective-permute-start | bytes 1179656 | tf_op jit(solution)/shard_map/ppermute | solution.py:21
  11.0 2.7 %copy-start.2 = (f32[1,1,251,512]{3,1,2,0:T(1,128)S(1)}, f32[1,1,251,512]{3,1,2,0:T(1,128)}, u32[]{:S(2)}) copy-start(f32[1,1,251,512]{3,1,2,0:T(1,128)} %param.18) | copy-start | bytes 1542148
  12.0 28.5 %collective-permute-start.1 = (f32[196,512]{1,0:T(8,128)}, f32[196,512]{1,0:T(8,128)}, u32[]{:S(2)}, u32[]{:S(2)}) collective-permute-start(f32[196,512]{1,0:T(8,128)} %pad_maximum_fusion.1), channel_id=1, source_target_pairs={{0,128},{128,0},{1,129},{129,1},{2,130},{130,2},{3,131},{131,3},{4... | collective-permute-start | bytes 1204232 | tf_op jit(solution)/shard_map/ppermute | solution.py:21
  13.9 19.8 %copy-start.11 = (f32[1024,64]{0,1:T(8,128)S(1)}, f32[1024,64]{0,1:T(8,128)}, u32[]{:S(2)}) copy-start(f32[1024,64]{0,1:T(8,128)} %param.20) | copy-start | bytes 786436
  15.0 16.4 %collective-permute-start.3 = (f32[251,64]{0,1:T(8,128)S(1)}, f32[251,64]{0,1:T(8,128)S(1)}, u32[]{:S(2)}, u32[]{:S(2)}) collective-permute-start(f32[251,64]{0,1:T(8,128)S(1)} %dynamic-slice_add_fusion), channel_id=1, source_target_pairs={{0,128},{128,0},{1,129},{129,1},{2,130},{130,2},{3,131},{131,3},{4... | collective-permute-start | bytes 192776 | tf_op jit(solution)/shard_map/ppermute | solution.py:21
  31.3 2.3 %collective-permute-start.4 = (f32[251,64]{0,1:T(8,128)S(1)}, f32[251,64]{0,1:T(8,128)S(1)}, u32[]{:S(2)}, u32[]{:S(2)}) collective-permute-start(f32[251,64]{0,1:T(8,128)S(1)} %add.114), channel_id=1, source_target_pairs={{0,1},{1,0},{2,3},{3,2},{4,5},{5,4},{6,7},{7,6},{8,9},{9,8},{10,11... | collective-permute-start | bytes 192776 | tf_op jit(solution)/shard_map/ppermute | solution.py:21
  32.4 15.1 %collective-permute-start.5 = (f32[256,512]{1,0:T(8,128)S(1)}, f32[256,512]{1,0:T(8,128)S(1)}, u32[]{:S(2)}, u32[]{:S(2)}) collective-permute-start(f32[256,512]{1,0:T(8,128)S(1)} %pad_select_fusion), channel_id=1, source_target_pairs={{0,128},{128,0},{1,129},{129,1},{2,130},{130,2},{3,131},{131,3},{4... | collective-permute-start | bytes 1572872 | tf_op jit(solution)/shard_map/ppermute | solution.py:21
  36.9 1.4 %copy-start.4 = (f32[12,16,512]{2,1,0:T(8,128)S(1)}, f32[12,16,512]{2,1,0:T(8,128)}, u32[]{:S(2)}) copy-start(f32[12,16,512]{2,1,0:T(8,128)} %param.12) | copy-start | bytes 1179652
  36.9 1.4 %copy-start.6 = (f32[12,16,512]{2,1,0:T(8,128)S(1)}, f32[12,16,512]{2,1,0:T(8,128)}, u32[]{:S(2)}) copy-start(f32[12,16,512]{2,1,0:T(8,128)} %param.11) | copy-start | bytes 1179652
  36.9 1.4 %copy-start.7 = (f32[12,16,512]{2,1,0:T(8,128)S(1)}, f32[12,16,512]{2,1,0:T(8,128)}, u32[]{:S(2)}) copy-start(f32[12,16,512]{2,1,0:T(8,128)} %dynamic-slice_convert_fusion) | copy-start | bytes 1179652
  41.6 7.1 %copy-start.9 = (f32[24,16,512]{2,1,0:T(8,128)}, f32[24,16,512]{2,1,0:T(8,128)S(1)}, u32[]{:S(2)}) copy-start(f32[24,16,512]{2,1,0:T(8,128)S(1)} %constant_dynamic-update-slice_fusion.1) | copy-start | bytes 2359300
  44.3 4.3 %copy-start.16 = (f32[4,512]{1,0:T(4,128)}, f32[4,512]{1,0:T(4,128)S(1)}, u32[]{:S(2)}) copy-start(f32[4,512]{1,0:T(4,128)S(1)} %get-tuple-element.48) | copy-start | bytes 24580

commit v9 on v8

--- a/solution.py
+++ b/solution.py
@@ -76,8 +76,21 @@
     rep_index = lax.axis_index("rep")
     first_is_own = rep_index == 0
     width = attn_global.shape[-1]
-    given_attn = outer_sends(attn_global, attn_inner[0], rep_index)
-    got_attn_inner = swap(given_attn, "rep")
+    owned = attn_global.shape[0]
+    first_mats = owned // 3
+    given_start = (1 - rep_index) * owned
+    given_head = lax.optimization_barrier(
+        lax.dynamic_slice_in_dim(attn_inner[0], given_start, first_mats, 0).astype(jnp.float32)
+    )
+    got_head = swap(given_head, "rep")
+    given_tail = lax.optimization_barrier(
+        lax.dynamic_slice_in_dim(
+            attn_inner[0], given_start + first_mats, owned - first_mats, 0
+        ).astype(jnp.float32)
+    )
+    got_tail = swap(given_tail, "rep")
+    given_attn = jnp.concatenate([given_head, given_tail], axis=0)
+    got_attn_inner = jnp.concatenate([got_head, got_tail], axis=0)
     given_norm = outer_sends(norm_global, norm_inner[0], rep_index)
     attn_parts = (given_attn,) + outer_partial(
         attn_global, attn_momentum, lax.optimization_barrier(attn_inner[0]), rep_index

time: 49 us -> 45.8 us (0.935)
  waiting for transfers between devices: 18.2 us -> 10.4 us
  starting transfers between devices: 9.8 us -> 12 us
  local copies, waits for them, and re-layouts: 2.44 us -> 4.3 us
  other arithmetic: 14.2 us -> 14.8 us
    ppermute x6 -> x7, waiting for transfers between devices: 18.2 us -> 10.4 us  [swap(): return lax.ppermute(x, axis, perm=SWAP)]
    ppermute x6 -> x7, starting transfers between devices: 9.8 us -> 12 us  [swap(): return lax.ppermute(x, axis, perm=SWAP)]
    dynamic_update_slice x2, other arithmetic: 3.46 us -> 2.46 us  [place_own(): return lax.dynamic_update_slice_in_dim(empty, own, rep_index * rows, 0)]
    concatenate x0 -> x1, local copies, waits for them, and re-layouts: none -> 0.97 us  [step_body(): got_attn_inner = jnp.concatenate([got_head, got_tail], axis=0)]
    mul x1, other arithmetic: 0.04 us -> 0.94 us  [step_body(): attn_other = got_buffer[:attn_rows] + SHARE * given_attn.reshape(-1, width)]
    unnamed x35 -> x34, local copies, waits for them, and re-layouts: 1.41 us -> 2.31 us
    convert_element_type x0 -> x2, other arithmetic: none -> 0.68 us  [the longest x1 0.66 us: step_body(): lax.dynamic_slice_in_dim(attn_inner[0], given_start, first_mats, 0)]
  transfers between devices with their start and end apart: 6 -> 7, of which waited for: 2 -> 1; matrix products, arithmetic and copies ran while one was open for 28% -> 35% of each run, Pallas kernels for 0% -> 0%
where the time goes in v9:
time: 45.8 us; the launch traced here: 45.4 us
  other arithmetic  14.8 us (32%)
  starting transfers between devices  12 us (26%)
  waiting for transfers between devices  10.4 us (23%)
  local copies, waits for them, and re-layouts  4.3 us (9%)
  matrix products  2.96 us (6%)
  between operations  1 us (2%)
    ppermute x7, starting transfers between devices, swap(): return lax.ppermute(x, axis, perm=SWAP)  12 us
    ppermute x7, waiting for transfers between devices, swap(): return lax.ppermute(x, axis, perm=SWAP)  10.4 us
    dynamic_update_slice x2, other arithmetic, place_own(): return lax.dynamic_update_slice_in_dim(empty, own, rep_index * rows, 0)  2.46 us
    unnamed x34, local copies, waits for them, and re-layouts  2.31 us
    add x1, other arithmetic, step_body(): new_emb_momentum = MOMENTUM * emb_momentum + own_grad  1.49 us
    dynamic_update_slice x1, other arithmetic, place_other(): lax.dynamic_update_slice_in_dim(placed, other, (1 - rep_index) * rows, 0)  1.4 us
    select_n x1, other arithmetic, step_body(): emb_weights = jnp.where(in_own_half, own_full, other_full - STEP * emb_grad)  1.19 us
    select_n x1, other arithmetic, step_body(): offsets[:, None, :] // LOW  1.17 us
  transfers between devices with their start and end apart: 7, of which 1 were waited for; matrix products, arithmetic and copies ran while one was open for 35% of the time, Pallas kernels for 0%

profile of v9, /device:TPU:1, one launch (start us, length us, event | category | flops | bytes accessed | tf_op | source)
XLA Modules:
  0.0 45.4 jit_solution(13581472980123791459)
XLA Ops:
  0.7 1.2 %and_select_fusion.1 = (s32[2,8192]{1,0:T(2,128)S(1)}, s32[2,8192]{1,0:T(2,128)S(1)}) fusion(s32[2,8192]{1,0:T(2,128)} %param.21, s32[]{:T(128)S(6)} %mul.171), kind=kLoop, calls=%fused_computation.39 | loop fusion | flops 327680 | bytes 196612 | tf_op jit(solution)/shard_map/jit(floor_divide)/jit(_where)/select_n | solution.py:132
  1.9 0.9 %compare_and_fusion = pred[2,8192]{1,0:T(4,128)(4,1)S(1)} fusion(s32[2,8192]{1,0:T(2,128)} %param.21, s32[]{:T(128)S(6)} %mul.171), kind=kLoop, calls=%fused_computation.38 | loop fusion | flops 65536 | bytes 81924 | tf_op jit(solution)/shard_map/and | solution.py:129
  5.6 3.2 %collective-permute-start.3 = (f32[251,64]{0,1:T(8,128)}, f32[251,64]{0,1:T(8,128)}, u32[]{:S(2)}, u32[]{:S(2)}) collective-permute-start(f32[251,64]{0,1:T(8,128)} %constant_dynamic-slice_fusion.1), channel_id=1, source_target_pairs={{0,1},{1,0},{2,3},{3,2},{4,5},{5,4},{6,7},{7,6},{8,9},{9,8},{10,11... | collective-permute-start | bytes 192776 | tf_op jit(solution)/shard_map/ppermute | solution.py:21
  8.8 1.3 %collective-permute-start.1 = (f32[8,16,512]{2,1,0:T(8,128)S(1)}, f32[8,16,512]{2,1,0:T(8,128)}, u32[]{:S(2)}, u32[]{:S(2)}) collective-permute-start(f32[8,16,512]{2,1,0:T(8,128)S(1)} %bitcast_convert_fusion), channel_id=1, source_target_pairs={{0,128},{128,0},{1,129},{129,1},{2,130},{130,2},{3,131},{131,3},{4... | collective-permute-start | bytes 786440 | tf_op jit(solution)/shard_map/ppermute | solution.py:21
  10.8 1.8 %collective-permute-start = (f32[4,16,512]{2,1,0:T(8,128)}, f32[4,16,512]{2,1,0:T(8,128)}, u32[]{:S(2)}, u32[]{:S(2)}) collective-permute-start(f32[4,16,512]{2,1,0:T(8,128)} %bitcast_convert_fusion.1), channel_id=1, source_target_pairs={{0,128},{128,0},{1,129},{129,1},{2,130},{130,2},{3,131},{131,3},{4... | collective-permute-start | bytes 393224 | tf_op jit(solution)/shard_map/ppermute | solution.py:21
  12.6 0.8 %dynamic-slice_convert_fusion = f32[12,16,512]{2,1,0:T(8,128)} fusion(bf16[24,16,512]{2,1,0:T(8,128)(2,1)S(1)} %bitcast.49, s32[]{:T(128)S(6)} %select_n.111), kind=kLoop, calls=%fused_computation.32 | loop fusion | flops 98304 | bytes 589828 | tf_op jit(solution)/shard_map/convert_element_type | solution.py:40
  13.6 0.8 %pad_maximum_fusion.1 = f32[196,512]{1,0:T(8,128)} fusion(f32[2,512]{1,0:T(2,128)S(1)} %multiply_add_fusion.3, f32[2,512]{1,0:T(2,128)S(1)} %get-tuple-element.57, f32[192,512]{1,0:T(8,128)S(1)} %bitcast.46), kind=kLoop, calls=%fused_computation.24 | loop fusion | flops 200704 | bytes 802816 | tf_op jit(solution)/shard_map/concatenate | solution.py:103
  14.3 1.2 %collective-permute-start.2 = (f32[196,512]{1,0:T(8,128)}, f32[196,512]{1,0:T(8,128)}, u32[]{:S(2)}, u32[]{:S(2)}) collective-permute-start(f32[196,512]{1,0:T(8,128)} %pad_maximum_fusion.1), channel_id=1, source_target_pairs={{0,128},{128,0},{1,129},{129,1},{2,130},{130,2},{3,131},{131,3},{4... | collective-permute-start | bytes 1204232 | tf_op jit(solution)/shard_map/ppermute | solution.py:21
  15.5 0.9 %maximum_multiply_fusion = f32[12,16,512]{2,1,0:T(8,128)S(1)} fusion(f32[8,16,512]{2,1,0:T(8,128)S(1)} %bitcast_convert_fusion, f32[4,16,512]{2,1,0:T(8,128)} %bitcast_convert_fusion.1), kind=kLoop, calls=%fused_computation.26 | loop fusion | flops 196608 | bytes 786432 | tf_op jit(solution)/shard_map/mul | solution.py:113
  16.7 1.0 %dynamic-slice_add_fusion = f32[251,64]{0,1:T(8,128)S(1)} fusion(f32[251,64]{0,1:T(8,128)} %collective-permute-done.3, f32[502,64]{0,1:T(8,128)} %copy-done.11, s32[]{:T(128)S(6)} %select_n.127), kind=kLoop, calls=%fused_computation.47 | loop fusion | flops 16064 | bytes 192772 | tf_op jit(solution)/shard_map/add | solution.py:165
  17.7 1.9 %collective-permute-start.4 = (f32[251,64]{0,1:T(8,128)S(1)}, f32[251,64]{0,1:T(8,128)S(1)}, u32[]{:S(2)}, u32[]{:S(2)}) collective-permute-start(f32[251,64]{0,1:T(8,128)S(1)} %dynamic-slice_add_fusion), channel_id=1, source_target_pairs={{0,128},{128,0},{1,129},{129,1},{2,130},{130,2},{3,131},{131,3},{4... | collective-permute-start | bytes 192776 | tf_op jit(solution)/shard_map/ppermute | solution.py:21
  19.6 1.3 %collective-permute-start.6 = (f32[256,512]{1,0:T(8,128)S(1)}, f32[256,512]{1,0:T(8,128)S(1)}, u32[]{:S(2)}, u32[]{:S(2)}) collective-permute-start(f32[256,512]{1,0:T(8,128)S(1)} %pad_select_fusion), channel_id=1, source_target_pairs={{0,128},{128,0},{1,129},{129,1},{2,130},{130,2},{3,131},{131,3},{4... | collective-permute-start | bytes 1572872 | tf_op jit(solution)/shard_map/ppermute | solution.py:21
  20.9 10.3 %collective-permute-done.4 = f32[251,64]{0,1:T(8,128)S(1)} collective-permute-done((f32[251,64]{0,1:T(8,128)S(1)}, f32[251,64]{0,1:T(8,128)S(1)}, u32[]{:S(2)}, u32[]{:S(2)}) %collective-permute-start.4) | collective-permute-done | bytes 64288 | tf_op jit(solution)/shard_map/ppermute | solution.py:21
  31.3 1.4 %collective-permute-start.5 = (f32[251,64]{0,1:T(8,128)S(1)}, f32[251,64]{0,1:T(8,128)S(1)}, u32[]{:S(2)}, u32[]{:S(2)}) collective-permute-start(f32[251,64]{0,1:T(8,128)S(1)} %add.124), channel_id=1, source_target_pairs={{0,1},{1,0},{2,3},{3,2},{4,5},{5,4},{6,7},{7,6},{8,9},{9,8},{10,11... | collective-permute-start | bytes 192776 | tf_op jit(solution)/shard_map/ppermute | solution.py:21
  32.7 0.9 %constant_dynamic-update-slice_fusion.1 = f32[12,16,512]{2,1,0:T(8,128)S(1)} fusion(f32[4,16,512]{2,1,0:T(8,128)} %collective-permute-done), kind=kLoop, calls=%fused_computation.56 | loop fusion | bytes 262144
  33.7 1.1 %convolution_multiply_fusion = f32[502,512]{1,0:T(8,128)S(1)} fusion(f32[251,64]{0,1:T(8,128)S(1)} %get-tuple-element.52, f32[251,64]{0,1:T(8,128)S(1)} %get-tuple-element.51, f32[1024,64]{0,1:T(8,128)S(1)} %copy-done.10, s32[]{:T(128)S(6)} %select_n.121), kind=kOutput, calls=%fused_computation.2 | convolution fusion | flops 197683584 | bytes 1290244 | tf_op jit(solution)/shard_map/dot_general | solution.py:177
  35.3 1.5 %reshape_add_fusion = f32[1,1,251,512]{3,1,2,0:T(1,128)} fusion(f32[251,512]{1,0:T(8,128)S(1)} %get-tuple-element.43, f32[1,1,251,512]{3,1,2,0:T(1,128)S(1)} %copy-done.2), kind=kLoop, calls=%fused_computation.21 | loop fusion | flops 257024 | bytes 1542144 | tf_op jit(solution)/shard_map/add | solution.py:188
  36.8 1.3 %copy.22 = f32[1,1,251,512]{3,1,2,0:T(1,128)} copy(f32[1,1,251,512]{3,2,1,0:T(8,128)S(1)} %bitcast_subtract_fusion.1) | data formatting | bytes 1028096
  38.2 1.0 %constant_dynamic-update-slice_fusion = f32[12,16,512]{2,1,0:T(8,128)S(1)} fusion(f32[12,16,512]{2,1,0:T(8,128)S(1)} %constant_dynamic-update-slice_fusion.1, f32[8,16,512]{2,1,0:T(8,128)} %collective-permute-done.1), kind=kLoop, calls=%fused_computation.55 | loop fusion | bytes 524288 | tf_op jit(solution)/shard_map/concatenate | solution.py:93
  39.2 1.1 %constant_dynamic-update-slice_fusion.4 = (f32[24,16,512]{2,1,0:T(8,128)S(1)}, f32[12,16,512]{2,1,0:T(8,128)}, f32[12,16,512]{2,1,0:T(8,128)}) fusion(f32[24,16,512]{2,1,0:T(8,128)S(1)} %broadcast_in_dim.8, s32[]{:T(128)S(6)} %select_n.111, f32[12,16,512]{2,1,0:T(8,128)S(1)} %multiply_add_fusion.1, f32[12,16,512]{2,1,0:T(8,128)S(1)} %constant_dynamic-update-slice_fusion, ...), kind=kLoop, calls=%fused_computation.72 | loop fusion | flops 688128 | bytes 3145732 | tf_op jit(solution)/shard_map/dynamic_update_slice | solution.py:55
  40.3 1.0 %slice_add_fusion = f32[192,512]{1,0:T(8,128)S(1)} fusion(f32[196,512]{1,0:T(8,128)} %collective-permute-done.2, f32[12,16,512]{2,1,0:T(8,128)S(1)} %maximum_multiply_fusion), kind=kLoop, calls=%fused_computation.25 | loop fusion | flops 98304 | bytes 1179648 | tf_op jit(solution)/shard_map/add | solution.py:113
  41.5 1.4 %constant_dynamic-update-slice_fusion.2 = (f32[4,512]{1,0:T(4,128)S(1)}, f32[2,512]{1,0:T(2,128)}) fusion(f32[4,512]{1,0:T(4,128)S(1)} %broadcast_in_dim.9, s32[]{:T(128)S(6)} %select_n.115, f32[2,512]{1,0:T(2,128)S(1)} %multiply_add_fusion.3, f32[196,512]{1,0:T(8,128)} %collective-permute-done.2), kind=kLoop, calls=%fused_computation.68 | loop fusion | flops 2048 | bytes 16388 | tf_op jit(solution)/shard_map/dynamic_update_slice | solution.py:55
  42.8 1.4 %fusion.18 = (f32[4,512]{1,0:T(4,128)S(1)}, f32[2,512]{1,0:T(2,128)}) fusion(f32[4,512]{1,0:T(4,128)S(1)} %get-tuple-element.44, s32[]{:T(128)S(6)} %select_n.114, f32[196,512]{1,0:T(8,128)} %collective-permute-done.2, f32[2,512]{1,0:T(2,128)S(1)} %get-tuple-element.57, f32[2,512]{1,0:T(2,128)S(1)} %copy-done.13, f32[2,512]{1,0:T(2,128)S(1)} %get-tuple-element.27, ...), kind=kLoop, calls=%fused_computation.58 | loop fusion | flops 7168 | bytes 32772 | tf_op jit(solution)/shard_map/dynamic_update_slice | solution.py:60
  44.2 1.2 %subtract_select_fusion = f32[502,512]{1,0:T(8,128)} fusion(f32[502,512]{1,0:T(8,128)S(1)} %pad_maximum_fusion, f32[502,512]{1,0:T(8,128)S(1)} %convolution_multiply_fusion, f32[256,512]{1,0:T(8,128)S(1)} %collective-permute-done.6, f32[254,512]{1,0:T(8,128)S(1)} %bitcast.47, pred[502]{0:T(512)(128)(4,1)S(1)} %fusion.26, pred[]{:T(512)S(6)} %eq.38), kind=kLoop, calls=%fused_computation.12 | loop fusion | flops 1028096 | bytes 4129271 | tf_op jit(solution)/shard_map/jit(_where)/select_n | solution.py:208
  (64 shorter events, 4.5 us)
Async XLA Ops:
  0.6 3.6 %copy-start = (bf16[1,502,512]{2,1,0:T(8,128)(2,1)S(1)}, bf16[1,502,512]{2,1,0:T(8,128)(2,1)}, u32[]{:S(2)}) copy-start(bf16[1,502,512]{2,1,0:T(8,128)(2,1)} %param.19) | copy-start | bytes 1542148
  0.7 3.0 %copy-start.1 = (f32[1,1,251,512]{3,1,2,0:T(1,128)S(1)}, f32[1,1,251,512]{3,1,2,0:T(1,128)}, u32[]{:S(2)}) copy-start(f32[1,1,251,512]{3,1,2,0:T(1,128)} %param.17) | copy-start | bytes 1542148
  0.7 3.0 %copy-start.9 = (f32[1024,64]{0,1:T(8,128)S(1)}, f32[1024,64]{0,1:T(8,128)}, u32[]{:S(2)}) copy-start(f32[1024,64]{0,1:T(8,128)} %param.20) | copy-start | bytes 786436
  3.4 5.4 %copy-start.7 = (bf16[1,24,16,512]{3,2,1,0:T(8,128)(2,1)S(1)}, bf16[1,24,16,512]{3,2,1,0:T(8,128)(2,1)}, u32[]{:S(2)}) copy-start(bf16[1,24,16,512]{3,2,1,0:T(8,128)(2,1)} %param.13) | copy-start | bytes 1179652
  4.3 9.1 %copy-start.3 = (f32[12,16,512]{2,1,0:T(8,128)S(1)}, f32[12,16,512]{2,1,0:T(8,128)}, u32[]{:S(2)}) copy-start(f32[12,16,512]{2,1,0:T(8,128)} %param.12) | copy-start | bytes 1179652
  4.3 9.1 %copy-start.4 = (f32[12,16,512]{2,1,0:T(8,128)S(1)}, f32[12,16,512]{2,1,0:T(8,128)}, u32[]{:S(2)}) copy-start(f32[12,16,512]{2,1,0:T(8,128)} %param.11) | copy-start | bytes 1179652
  4.9 7.7 %copy-start.11 = (f32[502,64]{0,1:T(8,128)}, f32[502,64]{0,1:T(8,128)S(1)}, u32[]{:S(2)}) copy-start(f32[502,64]{0,1:T(8,128)S(1)} %fusion.2) | copy-start | bytes 385540
  5.6 11.0 %collective-permute-start.3 = (f32[251,64]{0,1:T(8,128)}, f32[251,64]{0,1:T(8,128)}, u32[]{:S(2)}, u32[]{:S(2)}) collective-permute-start(f32[251,64]{0,1:T(8,128)} %constant_dynamic-slice_fusion.1), channel_id=1, source_target_pairs={{0,1},{1,0},{2,3},{3,2},{4,5},{5,4},{6,7},{7,6},{8,9},{9,8},{10,11... | collective-permute-start | bytes 192776 | tf_op jit(solution)/shard_map/ppermute | solution.py:21
  8.8 29.3 %collective-permute-start.1 = (f32[8,16,512]{2,1,0:T(8,128)S(1)}, f32[8,16,512]{2,1,0:T(8,128)}, u32[]{:S(2)}, u32[]{:S(2)}) collective-permute-start(f32[8,16,512]{2,1,0:T(8,128)S(1)} %bitcast_convert_fusion), channel_id=1, source_target_pairs={{0,128},{128,0},{1,129},{129,1},{2,130},{130,2},{3,131},{131,3},{4... | collective-permute-start | bytes 786440 | tf_op jit(solution)/shard_map/ppermute | solution.py:21
  10.8 2.7 %copy-start.14 = (bf16[1,4,512]{2,1,0:T(4,128)(2,1)S(1)}, bf16[1,4,512]{2,1,0:T(4,128)(2,1)}, u32[]{:S(2)}) copy-start(bf16[1,4,512]{2,1,0:T(4,128)(2,1)} %param.16) | copy-start | bytes 12292
  10.8 2.7 %copy-start.12 = (f32[2,512]{1,0:T(2,128)S(1)}, f32[2,512]{1,0:T(2,128)}, u32[]{:S(2)}) copy-start(f32[2,512]{1,0:T(2,128)} %param.15) | copy-start | bytes 12292
  10.8 2.7 %copy-start.13 = (f32[2,512]{1,0:T(2,128)S(1)}, f32[2,512]{1,0:T(2,128)}, u32[]{:S(2)}) copy-start(f32[2,512]{1,0:T(2,128)} %param.14) | copy-start | bytes 12292
  10.8 21.9 %collective-permute-start = (f32[4,16,512]{2,1,0:T(8,128)}, f32[4,16,512]{2,1,0:T(8,128)}, u32[]{:S(2)}, u32[]{:S(2)}) collective-permute-start(f32[4,16,512]{2,1,0:T(8,128)} %bitcast_convert_fusion.1), channel_id=1, source_target_pairs={{0,128},{128,0},{1,129},{129,1},{2,130},{130,2},{3,131},{131,3},{4... | collective-permute-start | bytes 393224 | tf_op jit(solution)/shard_map/ppermute | solution.py:21
  13.5 3.0 %copy-start.2 = (f32[1,1,251,512]{3,1,2,0:T(1,128)S(1)}, f32[1,1,251,512]{3,1,2,0:T(1,128)}, u32[]{:S(2)}) copy-start(f32[1,1,251,512]{3,1,2,0:T(1,128)} %param.18) | copy-start | bytes 1542148
  14.3 26.0 %collective-permute-start.2 = (f32[196,512]{1,0:T(8,128)}, f32[196,512]{1,0:T(8,128)}, u32[]{:S(2)}, u32[]{:S(2)}) collective-permute-start(f32[196,512]{1,0:T(8,128)} %pad_maximum_fusion.1), channel_id=1, source_target_pairs={{0,128},{128,0},{1,129},{129,1},{2,130},{130,2},{3,131},{131,3},{4... | collective-permute-start | bytes 1204232 | tf_op jit(solution)/shard_map/ppermute | solution.py:21
  16.6 17.0 %copy-start.10 = (f32[1024,64]{0,1:T(8,128)S(1)}, f32[1024,64]{0,1:T(8,128)}, u32[]{:S(2)}) copy-start(f32[1024,64]{0,1:T(8,128)} %param.20) | copy-start | bytes 786436
  17.7 13.6 %collective-permute-start.4 = (f32[251,64]{0,1:T(8,128)S(1)}, f32[251,64]{0,1:T(8,128)S(1)}, u32[]{:S(2)}, u32[]{:S(2)}) collective-permute-start(f32[251,64]{0,1:T(8,128)S(1)} %dynamic-slice_add_fusion), channel_id=1, source_target_pairs={{0,128},{128,0},{1,129},{129,1},{2,130},{130,2},{3,131},{131,3},{4... | collective-permute-start | bytes 192776 | tf_op jit(solution)/shard_map/ppermute | solution.py:21
  19.6 24.6 %collective-permute-start.6 = (f32[256,512]{1,0:T(8,128)S(1)}, f32[256,512]{1,0:T(8,128)S(1)}, u32[]{:S(2)}, u32[]{:S(2)}) collective-permute-start(f32[256,512]{1,0:T(8,128)S(1)} %pad_select_fusion), channel_id=1, source_target_pairs={{0,128},{128,0},{1,129},{129,1},{2,130},{130,2},{3,131},{131,3},{4... | collective-permute-start | bytes 1572872 | tf_op jit(solution)/shard_map/ppermute | solution.py:21
  31.3 2.3 %collective-permute-start.5 = (f32[251,64]{0,1:T(8,128)S(1)}, f32[251,64]{0,1:T(8,128)S(1)}, u32[]{:S(2)}, u32[]{:S(2)}) collective-permute-start(f32[251,64]{0,1:T(8,128)S(1)} %add.124), channel_id=1, source_target_pairs={{0,1},{1,0},{2,3},{3,2},{4,5},{5,4},{6,7},{7,6},{8,9},{9,8},{10,11... | collective-permute-start | bytes 192776 | tf_op jit(solution)/shard_map/ppermute | solution.py:21
  36.8 2.4 %copy-start.5 = (f32[12,16,512]{2,1,0:T(8,128)S(1)}, f32[12,16,512]{2,1,0:T(8,128)}, u32[]{:S(2)}) copy-start(f32[12,16,512]{2,1,0:T(8,128)} %param.11) | copy-start | bytes 1179652
  36.8 2.4 %copy-start.6 = (f32[12,16,512]{2,1,0:T(8,128)S(1)}, f32[12,16,512]{2,1,0:T(8,128)}, u32[]{:S(2)}) copy-start(f32[12,16,512]{2,1,0:T(8,128)} %dynamic-slice_convert_fusion) | copy-start | bytes 1179652
  41.4 4.0 %copy-start.8 = (f32[24,16,512]{2,1,0:T(8,128)}, f32[24,16,512]{2,1,0:T(8,128)S(1)}, u32[]{:S(2)}) copy-start(f32[24,16,512]{2,1,0:T(8,128)S(1)} %constant_dynamic-update-slice_fusion.3) | copy-start | bytes 2359300
  44.2 1.2 %copy-start.15 = (f32[4,512]{1,0:T(4,128)}, f32[4,512]{1,0:T(4,128)S(1)}, u32[]{:S(2)}) copy-start(f32[4,512]{1,0:T(4,128)S(1)} %get-tuple-element.48) | copy-start | bytes 24580

commit v10 on v5

--- a/solution.py
+++ b/solution.py
@@ -154,7 +154,12 @@
     kept_rows, coeff_mine = lax.optimization_barrier((kept_rows, coeff_mine))
     coeff_half = coeff_mine + swap(coeff_mine, "rep")
     coeff_sum = place_pair(tp_index == 0, coeff_half, swap(coeff_half, "tp"))
-    got_rows = swap(kept_rows, "rep")
+    lead = half_rows % 8
+    pad_rows = lead + half_rows + (-(lead + half_rows)) % 8
+    shifted = jnp.pad(kept_rows, ((lead, pad_rows - lead - half_rows), (0, 0)))
+    plain = jnp.pad(kept_rows, ((0, pad_rows - half_rows), (0, 0)))
+    rows_sent = jnp.where(rep_index == 1, shifted, plain)
+    got_rows = swap(rows_sent, "rep")
     emb_grad = (
         jnp.dot(
             coeff_sum,
@@ -170,10 +175,19 @@
     new_emb_momentum = MOMENTUM * emb_momentum + own_grad
     own_flat = kept_rows - STEP * lax.dynamic_slice_in_dim(emb_grad, half_start, half_rows, 0)
     other_grad = lax.dynamic_slice_in_dim(emb_grad, (1 - rep_index) * half_rows, half_rows, 0)
-    new_emb_global, new_emb_momentum, own_flat, other_grad = lax.optimization_barrier(
-        (new_emb_global, new_emb_momentum, own_flat, other_grad)
-    )
-    emb_weights = place_pair(first_is_own, own_flat, got_rows - STEP * other_grad)
+    own_full = place_pair(first_is_own, own_flat, jnp.zeros_like(own_flat))
+    aligned_start = half_rows - lead
+    span = block_rows - aligned_start
+    update_start = (1 - rep_index) * aligned_start
+    own_part = lax.dynamic_slice_in_dim(own_full, update_start, span, 0)
+    grad_part = lax.dynamic_slice_in_dim(emb_grad, update_start, span, 0)
+    new_emb_global, new_emb_momentum, own_full, own_part, grad_part = lax.optimization_barrier(
+        (new_emb_global, new_emb_momentum, own_full, own_part, grad_part)
+    )
+    part_rows = update_start + lax.broadcasted_iota(jnp.int32, (span, half_width), 0)
+    in_own_half = (part_rows >= half_start) & (part_rows < half_start + half_rows)
+    update = jnp.where(in_own_half, own_part, got_rows[:span] - STEP * grad_part)
+    emb_weights = lax.dynamic_update_slice_in_dim(own_full, update, update_start, 0)
     return (
         new_attn_global,
         new_attn_momentum,

time: 43.2 us -> 49.6 us (1.15)
  waiting for transfers between devices: 7.73 us -> 16.8 us
  other arithmetic: 17.3 us -> 14.5 us
  local copies, waits for them, and re-layouts: 3.15 us -> 3.97 us
  starting transfers between devices: 10.5 us -> 9.8 us
    ppermute x6, waiting for transfers between devices: 7.73 us -> 16.8 us  [swap(): return lax.ppermute(x, axis, perm=SWAP)]
    convert_element_type x2, other arithmetic: 1.07 us -> 0.05 us  [outer_sends(): given_inner = lax.dynamic_slice_in_dim(inner_all, (1 - rep_index) * owned...]
    add x2, other arithmetic: 1.04 us -> 0.11 us  [outer_partial(): partial = KEEP * global_part - DECAY * momentum_part + SHARE * own_inner]
    select_n x2, other arithmetic: 1.05 us -> 0.16 us  [place_pair(): first = jnp.where(first_is_own, own, other)]
    ppermute x6, starting transfers between devices: 10.5 us -> 9.8 us  [swap(): return lax.ppermute(x, axis, perm=SWAP)]
    add x1, other arithmetic: 0.64 us -> 0.01 us  [step_body(): coeff_half = coeff_mine + swap(coeff_mine, 'rep')]
    dynamic_update_slice x0 -> x1, local copies, waits for them, and re-layouts: none -> 0.51 us  [step_body(): lax.dynamic_update_slice_in_dim(own_full, update, update_start, 0)]
    concatenate x1 -> x2, other arithmetic: 1.06 us -> 1.39 us  [place_pair(): return jnp.concatenate([first, second], axis=0)]
  transfers between devices with their start and end apart: 6 -> 6, of which waited for: 2 -> 2; matrix products, arithmetic and copies ran while one was open for 48% -> 30% of each run, Pallas kernels for 0% -> 0%
where the time goes in v10:
time: 49.6 us; the launch traced here: 49.1 us
  waiting for transfers between devices  16.8 us (34%)
  other arithmetic  14.5 us (29%)
  starting transfers between devices  9.8 us (20%)
  local copies, waits for them, and re-layouts  3.97 us (8%)
  matrix products  2.97 us (6%)
  between operations  1.07 us (2%)
    ppermute x6, waiting for transfers between devices, swap(): return lax.ppermute(x, axis, perm=SWAP)  16.8 us
    ppermute x6, starting transfers between devices, swap(): return lax.ppermute(x, axis, perm=SWAP)  9.8 us
    dynamic_update_slice x2, other arithmetic, place_own(): return lax.dynamic_update_slice_in_dim(empty, own, rep_index * rows, 0)  3.45 us
    unnamed x39, local copies, waits for them, and re-layouts  2.37 us
    add x1, other arithmetic, step_body(): new_emb_momentum = MOMENTUM * emb_momentum + own_grad  1.49 us
    dynamic_update_slice x1, other arithmetic, place_other(): lax.dynamic_update_slice_in_dim(placed, other, (1 - rep_index) * rows, 0)  1.4 us
    concatenate x2, other arithmetic, place_pair(): return jnp.concatenate([first, second], axis=0)  1.39 us
    select_n x1, other arithmetic, step_body(): offsets[:, None, :] // LOW  1.17 us
  transfers between devices with their start and end apart: 6, of which 2 were waited for; matrix products, arithmetic and copies ran while one was open for 30% of the time, Pallas kernels for 0%

profile of v10, /device:TPU:1, one launch (start us, length us, event | category | flops | bytes accessed | tf_op | source)
XLA Modules:
  0.0 49.1 jit_solution(14546563079927443645)
XLA Ops:
  0.7 1.2 %and_select_fusion.1 = (s32[2,8192]{1,0:T(2,128)S(1)}, s32[2,8192]{1,0:T(2,128)S(1)}) fusion(s32[2,8192]{1,0:T(2,128)} %param.21, s32[]{:T(128)S(6)} %mul.174), kind=kLoop, calls=%fused_computation.43 | loop fusion | flops 327680 | bytes 196612 | tf_op jit(solution)/shard_map/jit(floor_divide)/jit(_where)/select_n | solution.py:119
  1.9 0.9 %compare_and_fusion = pred[2,8192]{1,0:T(4,128)(4,1)S(1)} fusion(s32[2,8192]{1,0:T(2,128)} %param.21, s32[]{:T(128)S(6)} %mul.174), kind=kLoop, calls=%fused_computation.42 | loop fusion | flops 65536 | bytes 81924 | tf_op jit(solution)/shard_map/and | solution.py:116
  2.8 0.6 %fusion.3 = pred[2,16,32]{2,1,0:T(8,128)(4,1)S(1)} fusion(s32[2,8192]{1,0:T(2,128)S(1)} %get-tuple-element.60, s32[2,8192]{1,0:T(2,128)S(1)} %get-tuple-element.59, pred[2,8192]{1,0:T(4,128)(4,1)S(1)} %compare_and_fusion), kind=kOutput, calls=%fused_computation.10 | convolution fusion | flops 17826816 | bytes 148480 | tf_op jit(solution)/shard_map/gik,gjk->gij/dot_general | solution.py:122
  4.9 0.7 %constant_dynamic-slice_fusion.2 = f32[251,64]{0,1:T(8,128)} fusion(f32[502,64]{0,1:T(8,128)S(1)} %fusion.2, s32[]{:T(128)S(6)} %select_n.121), kind=kLoop, calls=%fused_computation.67 | loop fusion | bytes 128516 | tf_op jit(solution)/shard_map/dynamic_slice | solution.py:150
  5.6 3.2 %collective-permute-start.2 = (f32[251,64]{0,1:T(8,128)}, f32[251,64]{0,1:T(8,128)}, u32[]{:S(2)}, u32[]{:S(2)}) collective-permute-start(f32[251,64]{0,1:T(8,128)} %constant_dynamic-slice_fusion.2), channel_id=1, source_target_pairs={{0,1},{1,0},{2,3},{3,2},{4,5},{5,4},{6,7},{7,6},{8,9},{9,8},{10,11... | collective-permute-start | bytes 192776 | tf_op jit(solution)/shard_map/ppermute | solution.py:21
  8.9 1.3 %collective-permute-start = (f32[12,16,512]{2,1,0:T(8,128)S(1)}, f32[12,16,512]{2,1,0:T(8,128)}, u32[]{:S(2)}, u32[]{:S(2)}) collective-permute-start(f32[12,16,512]{2,1,0:T(8,128)S(1)} %bitcast_convert_fusion), channel_id=1, source_target_pairs={{0,128},{128,0},{1,129},{129,1},{2,130},{130,2},{3,131},{131,3},{4... | collective-permute-start | bytes 1179656 | tf_op jit(solution)/shard_map/ppermute | solution.py:21
  10.2 0.8 %dynamic-slice_convert_fusion = f32[12,16,512]{2,1,0:T(8,128)} fusion(bf16[24,16,512]{2,1,0:T(8,128)(2,1)S(1)} %bitcast.44, s32[]{:T(128)S(6)} %select_n.105), kind=kLoop, calls=%fused_computation.37 | loop fusion | flops 98304 | bytes 589828 | tf_op jit(solution)/shard_map/convert_element_type | solution.py:40
  11.2 0.8 %pad_maximum_fusion.1 = f32[196,512]{1,0:T(8,128)} fusion(f32[2,512]{1,0:T(2,128)S(1)} %multiply_add_fusion.3, f32[2,512]{1,0:T(2,128)S(1)} %get-tuple-element.61, f32[192,512]{1,0:T(8,128)S(1)} %bitcast.42), kind=kLoop, calls=%fused_computation.28 | loop fusion | flops 200704 | bytes 802816 | tf_op jit(solution)/shard_map/concatenate | solution.py:90
  11.9 1.8 %collective-permute-start.1 = (f32[196,512]{1,0:T(8,128)}, f32[196,512]{1,0:T(8,128)}, u32[]{:S(2)}, u32[]{:S(2)}) collective-permute-start(f32[196,512]{1,0:T(8,128)} %pad_maximum_fusion.1), channel_id=1, source_target_pairs={{0,128},{128,0},{1,129},{129,1},{2,130},{130,2},{3,131},{131,3},{4... | collective-permute-start | bytes 1204232 | tf_op jit(solution)/shard_map/ppermute | solution.py:21
  13.9 1.0 %dynamic-slice_add_fusion = f32[251,64]{0,1:T(8,128)S(1)} fusion(f32[251,64]{0,1:T(8,128)} %collective-permute-done.2, f32[502,64]{0,1:T(8,128)} %copy-done.14, s32[]{:T(128)S(6)} %select_n.120), kind=kLoop, calls=%fused_computation.50 | loop fusion | flops 16064 | bytes 192772 | tf_op jit(solution)/shard_map/add | solution.py:152
  15.0 1.3 %collective-permute-start.3 = (f32[251,64]{0,1:T(8,128)S(1)}, f32[251,64]{0,1:T(8,128)S(1)}, u32[]{:S(2)}, u32[]{:S(2)}) collective-permute-start(f32[251,64]{0,1:T(8,128)S(1)} %dynamic-slice_add_fusion), channel_id=1, source_target_pairs={{0,128},{128,0},{1,129},{129,1},{2,130},{130,2},{3,131},{131,3},{4... | collective-permute-start | bytes 192776 | tf_op jit(solution)/shard_map/ppermute | solution.py:21
  16.3 15.1 %collective-permute-done.3 = f32[251,64]{0,1:T(8,128)S(1)} collective-permute-done((f32[251,64]{0,1:T(8,128)S(1)}, f32[251,64]{0,1:T(8,128)S(1)}, u32[]{:S(2)}, u32[]{:S(2)}) %collective-permute-start.3) | collective-permute-done | bytes 64288 | tf_op jit(solution)/shard_map/ppermute | solution.py:21
  31.3 1.0 %collective-permute-start.4 = (f32[251,64]{0,1:T(8,128)S(1)}, f32[251,64]{0,1:T(8,128)S(1)}, u32[]{:S(2)}, u32[]{:S(2)}) collective-permute-start(f32[251,64]{0,1:T(8,128)S(1)} %add.122), channel_id=1, source_target_pairs={{0,1},{1,0},{2,3},{3,2},{4,5},{5,4},{6,7},{7,6},{8,9},{9,8},{10,11... | collective-permute-start | bytes 192776 | tf_op jit(solution)/shard_map/ppermute | solution.py:21
  32.4 1.3 %collective-permute-start.5 = (f32[256,512]{1,0:T(8,128)S(1)}, f32[256,512]{1,0:T(8,128)S(1)}, u32[]{:S(2)}, u32[]{:S(2)}) collective-permute-start(f32[256,512]{1,0:T(8,128)S(1)} %pad_select_fusion), channel_id=1, source_target_pairs={{0,128},{128,0},{1,129},{129,1},{2,130},{130,2},{3,131},{131,3},{4... | collective-permute-start | bytes 1572872 | tf_op jit(solution)/shard_map/ppermute | solution.py:21
  33.7 1.1 %convolution_multiply_fusion = f32[502,512]{1,0:T(8,128)S(1)} fusion(f32[251,64]{0,1:T(8,128)S(1)} %get-tuple-element.56, f32[251,64]{0,1:T(8,128)S(1)} %get-tuple-element.55, f32[1024,64]{0,1:T(8,128)S(1)} %copy-done.13, s32[]{:T(128)S(6)} %select_n.114), kind=kOutput, calls=%fused_computation.2 | convolution fusion | flops 197683584 | bytes 1290244 | tf_op jit(solution)/shard_map/dot_general | solution.py:164
  35.1 1.5 %reshape_add_fusion = f32[1,1,251,512]{3,1,2,0:T(1,128)} fusion(f32[251,512]{1,0:T(8,128)S(1)} %get-tuple-element.47, f32[1,1,251,512]{3,1,2,0:T(1,128)S(1)} %copy-done.2), kind=kLoop, calls=%fused_computation.25 | loop fusion | flops 257024 | bytes 1542144 | tf_op jit(solution)/shard_map/add | solution.py:175
  36.6 1.1 %pad_maximum_fusion = f32[502,512]{1,0:T(8,128)} fusion(f32[251,512]{1,0:T(8,128)S(1)} %broadcast_select_fusion, f32[251,512]{1,0:T(8,128)S(1)} %get-tuple-element.46), kind=kLoop, calls=%fused_computation.4 | loop fusion | flops 257024 | bytes 2056192 | tf_op jit(solution)/shard_map/concatenate | solution.py:27
  38.3 1.3 %copy.22 = f32[1,1,251,512]{3,1,2,0:T(1,128)} copy(f32[1,1,251,512]{3,2,1,0:T(8,128)S(1)} %bitcast_subtract_fusion.1) | data formatting | bytes 1028096
  39.7 2.1 %constant_dynamic-update-slice_fusion.2 = (f32[24,16,512]{2,1,0:T(8,128)S(1)}, f32[12,16,512]{2,1,0:T(8,128)}, f32[12,16,512]{2,1,0:T(8,128)}) fusion(f32[24,16,512]{2,1,0:T(8,128)S(1)} %broadcast_in_dim.8, s32[]{:T(128)S(6)} %select_n.105, f32[12,16,512]{2,1,0:T(8,128)S(1)} %multiply_add_fusion.1, f32[12,16,512]{2,1,0:T(8,128)} %collective-permute-done, ...), kind=kLoop, calls=%fused_computation.74 | loop fusion | flops 688128 | bytes 3145732 | tf_op jit(solution)/shard_map/dynamic_update_slice | solution.py:55
  41.8 1.0 %slice_add_fusion = f32[192,512]{1,0:T(8,128)S(1)} fusion(f32[196,512]{1,0:T(8,128)} %collective-permute-done.1, f32[12,16,512]{2,1,0:T(8,128)S(1)} %broadcast_multiply_fusion), kind=kLoop, calls=%fused_computation.29 | loop fusion | flops 98304 | bytes 1179648 | tf_op jit(solution)/shard_map/add | solution.py:100
  42.9 1.4 %constant_dynamic-update-slice_fusion = (f32[4,512]{1,0:T(4,128)S(1)}, f32[2,512]{1,0:T(2,128)}) fusion(f32[4,512]{1,0:T(4,128)S(1)} %broadcast_in_dim.9, s32[]{:T(128)S(6)} %select_n.108, f32[2,512]{1,0:T(2,128)S(1)} %multiply_add_fusion.3, f32[196,512]{1,0:T(8,128)} %collective-permute-done.1), kind=kLoop, calls=%fused_computation.70 | loop fusion | flops 2048 | bytes 16388 | tf_op jit(solution)/shard_map/dynamic_update_slice | solution.py:55
  44.3 1.4 %fusion.20 = (f32[4,512]{1,0:T(4,128)S(1)}, f32[2,512]{1,0:T(2,128)}) fusion(f32[4,512]{1,0:T(4,128)S(1)} %get-tuple-element.48, s32[]{:T(128)S(6)} %select_n.107, f32[196,512]{1,0:T(8,128)} %collective-permute-done.1, f32[2,512]{1,0:T(2,128)S(1)} %get-tuple-element.61, f32[2,512]{1,0:T(2,128)S(1)} %copy-done.16, f32[2,512]{1,0:T(2,128)S(1)} %get-tuple-element.29, ...), kind=kLoop, calls=%fused_computation.59 | loop fusion | flops 7168 | bytes 32772 | tf_op jit(solution)/shard_map/dynamic_update_slice | solution.py:60
  45.7 1.7 %collective-permute-done.5 = f32[256,512]{1,0:T(8,128)S(1)} collective-permute-done((f32[256,512]{1,0:T(8,128)S(1)}, f32[256,512]{1,0:T(8,128)S(1)}, u32[]{:S(2)}, u32[]{:S(2)}) %collective-permute-start.5) | collective-permute-done | bytes 524320 | tf_op jit(solution)/shard_map/ppermute | solution.py:21
  48.2 1.0 %copy-done.9 = f32[502,512]{1,0:T(8,128)} copy-done((f32[502,512]{1,0:T(8,128)}, f32[502,512]{1,0:T(8,128)S(1)}, u32[]{:S(2)}) %copy-start.9) | copy-done | bytes 1028120
  (68 shorter events, 3.6 us)
Async XLA Ops:
  0.6 3.6 %copy-start = (bf16[1,502,512]{2,1,0:T(8,128)(2,1)S(1)}, bf16[1,502,512]{2,1,0:T(8,128)(2,1)}, u32[]{:S(2)}) copy-start(bf16[1,502,512]{2,1,0:T(8,128)(2,1)} %param.19) | copy-start | bytes 1542148
  0.7 3.0 %copy-start.1 = (f32[1,1,251,512]{3,1,2,0:T(1,128)S(1)}, f32[1,1,251,512]{3,1,2,0:T(1,128)}, u32[]{:S(2)}) copy-start(f32[1,1,251,512]{3,1,2,0:T(1,128)} %param.17) | copy-start | bytes 1542148
  0.7 3.0 %copy-start.12 = (f32[1024,64]{0,1:T(8,128)S(1)}, f32[1024,64]{0,1:T(8,128)}, u32[]{:S(2)}) copy-start(f32[1024,64]{0,1:T(8,128)} %param.20) | copy-start | bytes 786436
  3.4 5.4 %copy-start.10 = (bf16[1,24,16,512]{3,2,1,0:T(8,128)(2,1)S(1)}, bf16[1,24,16,512]{3,2,1,0:T(8,128)(2,1)}, u32[]{:S(2)}) copy-start(bf16[1,24,16,512]{3,2,1,0:T(8,128)(2,1)} %param.13) | copy-start | bytes 1179652
  4.3 6.7 %copy-start.3 = (f32[12,16,512]{2,1,0:T(8,128)S(1)}, f32[12,16,512]{2,1,0:T(8,128)}, u32[]{:S(2)}) copy-start(f32[12,16,512]{2,1,0:T(8,128)} %param.12) | copy-start | bytes 1179652
  4.3 6.7 %copy-start.5 = (f32[12,16,512]{2,1,0:T(8,128)S(1)}, f32[12,16,512]{2,1,0:T(8,128)}, u32[]{:S(2)}) copy-start(f32[12,16,512]{2,1,0:T(8,128)} %param.11) | copy-start | bytes 1179652
  4.9 3.9 %copy-start.14 = (f32[502,64]{0,1:T(8,128)}, f32[502,64]{0,1:T(8,128)S(1)}, u32[]{:S(2)}) copy-start(f32[502,64]{0,1:T(8,128)S(1)} %fusion.2) | copy-start | bytes 385540
  5.6 8.3 %collective-permute-start.2 = (f32[251,64]{0,1:T(8,128)}, f32[251,64]{0,1:T(8,128)}, u32[]{:S(2)}, u32[]{:S(2)}) collective-permute-start(f32[251,64]{0,1:T(8,128)} %constant_dynamic-slice_fusion.2), channel_id=1, source_target_pairs={{0,1},{1,0},{2,3},{3,2},{4,5},{5,4},{6,7},{7,6},{8,9},{9,8},{10,11... | collective-permute-start | bytes 192776 | tf_op jit(solution)/shard_map/ppermute | solution.py:21
  8.9 2.2 %copy-start.17 = (bf16[1,4,512]{2,1,0:T(4,128)(2,1)S(1)}, bf16[1,4,512]{2,1,0:T(4,128)(2,1)}, u32[]{:S(2)}) copy-start(bf16[1,4,512]{2,1,0:T(4,128)(2,1)} %param.16) | copy-start | bytes 12292
  8.9 2.2 %copy-start.15 = (f32[2,512]{1,0:T(2,128)S(1)}, f32[2,512]{1,0:T(2,128)}, u32[]{:S(2)}) copy-start(f32[2,512]{1,0:T(2,128)} %param.15) | copy-start | bytes 12292
  8.9 2.2 %copy-start.16 = (f32[2,512]{1,0:T(2,128)S(1)}, f32[2,512]{1,0:T(2,128)}, u32[]{:S(2)}) copy-start(f32[2,512]{1,0:T(2,128)} %param.14) | copy-start | bytes 12292
  8.9 30.7 %collective-permute-start = (f32[12,16,512]{2,1,0:T(8,128)S(1)}, f32[12,16,512]{2,1,0:T(8,128)}, u32[]{:S(2)}, u32[]{:S(2)}) collective-permute-start(f32[12,16,512]{2,1,0:T(8,128)S(1)} %bitcast_convert_fusion), channel_id=1, source_target_pairs={{0,128},{128,0},{1,129},{129,1},{2,130},{130,2},{3,131},{131,3},{4... | collective-permute-start | bytes 1179656 | tf_op jit(solution)/shard_map/ppermute | solution.py:21
  11.0 2.7 %copy-start.2 = (f32[1,1,251,512]{3,1,2,0:T(1,128)S(1)}, f32[1,1,251,512]{3,1,2,0:T(1,128)}, u32[]{:S(2)}) copy-start(f32[1,1,251,512]{3,1,2,0:T(1,128)} %param.18) | copy-start | bytes 1542148
  11.9 29.9 %collective-permute-start.1 = (f32[196,512]{1,0:T(8,128)}, f32[196,512]{1,0:T(8,128)}, u32[]{:S(2)}, u32[]{:S(2)}) collective-permute-start(f32[196,512]{1,0:T(8,128)} %pad_maximum_fusion.1), channel_id=1, source_target_pairs={{0,128},{128,0},{1,129},{129,1},{2,130},{130,2},{3,131},{131,3},{4... | collective-permute-start | bytes 1204232 | tf_op jit(solution)/shard_map/ppermute | solution.py:21
  13.9 19.8 %copy-start.13 = (f32[1024,64]{0,1:T(8,128)S(1)}, f32[1024,64]{0,1:T(8,128)}, u32[]{:S(2)}) copy-start(f32[1024,64]{0,1:T(8,128)} %param.20) | copy-start | bytes 786436
  15.0 16.4 %collective-permute-start.3 = (f32[251,64]{0,1:T(8,128)S(1)}, f32[251,64]{0,1:T(8,128)S(1)}, u32[]{:S(2)}, u32[]{:S(2)}) collective-permute-start(f32[251,64]{0,1:T(8,128)S(1)} %dynamic-slice_add_fusion), channel_id=1, source_target_pairs={{0,128},{128,0},{1,129},{129,1},{2,130},{130,2},{3,131},{131,3},{4... | collective-permute-start | bytes 192776 | tf_op jit(solution)/shard_map/ppermute | solution.py:21
  31.3 2.3 %collective-permute-start.4 = (f32[251,64]{0,1:T(8,128)S(1)}, f32[251,64]{0,1:T(8,128)S(1)}, u32[]{:S(2)}, u32[]{:S(2)}) collective-permute-start(f32[251,64]{0,1:T(8,128)S(1)} %add.122), channel_id=1, source_target_pairs={{0,1},{1,0},{2,3},{3,2},{4,5},{5,4},{6,7},{7,6},{8,9},{9,8},{10,11... | collective-permute-start | bytes 192776 | tf_op jit(solution)/shard_map/ppermute | solution.py:21
  32.4 15.1 %collective-permute-start.5 = (f32[256,512]{1,0:T(8,128)S(1)}, f32[256,512]{1,0:T(8,128)S(1)}, u32[]{:S(2)}, u32[]{:S(2)}) collective-permute-start(f32[256,512]{1,0:T(8,128)S(1)} %pad_select_fusion), channel_id=1, source_target_pairs={{0,128},{128,0},{1,129},{129,1},{2,130},{130,2},{3,131},{131,3},{4... | collective-permute-start | bytes 1572872 | tf_op jit(solution)/shard_map/ppermute | solution.py:21
  38.2 1.4 %copy-start.4 = (f32[12,16,512]{2,1,0:T(8,128)S(1)}, f32[12,16,512]{2,1,0:T(8,128)}, u32[]{:S(2)}) copy-start(f32[12,16,512]{2,1,0:T(8,128)} %param.12) | copy-start | bytes 1179652
  38.3 1.4 %copy-start.6 = (f32[12,16,512]{2,1,0:T(8,128)S(1)}, f32[12,16,512]{2,1,0:T(8,128)}, u32[]{:S(2)}) copy-start(f32[12,16,512]{2,1,0:T(8,128)} %param.11) | copy-start | bytes 1179652
  38.3 1.4 %copy-start.7 = (f32[12,16,512]{2,1,0:T(8,128)S(1)}, f32[12,16,512]{2,1,0:T(8,128)}, u32[]{:S(2)}) copy-start(f32[12,16,512]{2,1,0:T(8,128)} %dynamic-slice_convert_fusion) | copy-start | bytes 1179652
  42.9 4.7 %copy-start.11 = (f32[24,16,512]{2,1,0:T(8,128)}, f32[24,16,512]{2,1,0:T(8,128)S(1)}, u32[]{:S(2)}) copy-start(f32[24,16,512]{2,1,0:T(8,128)S(1)} %constant_dynamic-update-slice_fusion.1) | copy-start | bytes 2359300
  45.7 1.9 %copy-start.18 = (f32[4,512]{1,0:T(4,128)}, f32[4,512]{1,0:T(4,128)S(1)}, u32[]{:S(2)}) copy-start(f32[4,512]{1,0:T(4,128)S(1)} %get-tuple-element.52) | copy-start | bytes 24580
  45.7 1.9 %copy-start.8 = (f32[502,512]{1,0:T(8,128)S(1)}, f32[502,512]{1,0:T(8,128)}, u32[]{:S(2)}) copy-start(f32[502,512]{1,0:T(8,128)} %pad_maximum_fusion) | copy-start | bytes 3084292
  (1 other events, 1.0 us)
